TPU v7x, 256 devices: a whole 4x4x8 slice. The times are simulated.
256 devices in a mesh: dp: 2 (over core), ctx: 8 (over y, z_lo), feat: 16 (over x, z_hi).
Axes of the slice: x: 4, y: 4, z: 8 (z_hi: 4, z_lo: 2; z = z_hi * 2 + z_lo), core: 2. Of those that a mesh axis runs over, the one named last changes fastest.
Arguments:
- out_grads: bfloat16 [2048, 28672], P(('dp', 'ctx'), 'feat'), may hold values from -6 to 6
- acts: bfloat16 [2048, 8192], P(('dp', 'ctx'), 'feat'), may hold values from -6 to 6
- domain_ids: int32 [2048], P(('dp', 'ctx')), may hold values from 0 to 7
- domain_weights: int32 [8], replicated, may hold values from 1 to 4
Outputs:
- grad_factor: bfloat16 [28672, 28672], P(('dp', 'ctx'), 'feat')
- act_factor: bfloat16 [8192, 8192], P(('dp', 'ctx'), 'feat')
All inputs are finite; a program needn't handle non-finite values.
Results may differ from a plain program's by a relative error of at most 0.003.
Values may be sent and summed in bfloat16 or wider, within the bound.
No kernel may reach another device: no remote copies, remote signals or barrier semaphores. Data moves between devices by JAX's collectives and lax.ppermute only.
A program may use at most 128 MiB of HBM per device.

v0:
```python
import jax
import jax.numpy as jnp
from jax import lax
from jax.sharding import PartitionSpec as P


def from_root(block, axis, owner):
    block = jnp.where(lax.axis_index(axis) == owner, block, jnp.zeros_like(block))
    return lax.psum(block, axis)


def weigh_rows(tok_ids, rows, domain_weights):
    labels = jnp.arange(domain_weights.shape[0], dtype=jnp.int32)
    match = tok_ids[:, None] == labels[None, :]
    tok_weight = jnp.sum(jnp.where(match, domain_weights[None, :], 0), axis=1).astype(jnp.float32)
    return (tok_weight[:, None] * rows.astype(jnp.float32)).astype(jnp.bfloat16)


def contract_tokens(left, right):
    return lax.dot_general(
        left, right, (((0,), (0,)), ((), ())), preferred_element_type=jnp.float32
    )


def local(out_grads, acts, domain_ids, domain_weights):
    group_size = lax.axis_size(("dp", "ctx"))
    inv_count = 1.0 / (out_grads.shape[0] * group_size)
    all_grads, all_acts, all_ids = (
        lax.all_gather(out_grads, ("dp", "ctx"), axis=0, tiled=True),
        lax.all_gather(acts, ("dp", "ctx"), axis=0, tiled=True),
        lax.all_gather(domain_ids, ("dp", "ctx"), axis=0, tiled=True),
    )
    tile_ratio = lax.axis_size("feat") // group_size
    first_root = lax.axis_index(("dp", "ctx")) * tile_ratio
    copy_grads = from_root(all_grads, "feat", first_root + 0)
    copy_acts = from_root(all_acts, "feat", first_root + 0)
    grad_sum = contract_tokens(copy_grads, weigh_rows(all_ids, all_grads, domain_weights))
    act_sum = contract_tokens(copy_acts, weigh_rows(all_ids, all_acts, domain_weights))
    grad_factor = (grad_sum * inv_count).astype(jnp.bfloat16)
    act_factor = (act_sum * inv_count).astype(jnp.bfloat16)
    return (grad_factor, act_factor)


def solution(mesh):
    in_specs = (P(("dp", "ctx"), "feat"), P(("dp", "ctx"), "feat"), P(("dp", "ctx")), P())
    out_specs = (P(("dp", "ctx"), "feat"), P(("dp", "ctx"), "feat"))
    return jax.shard_map(local, mesh=mesh, in_specs=in_specs, out_specs=out_specs, check_vma=False)
```

profile of v0, /device:TPU:41, one launch (start us, length us, event | category | flops | bytes accessed | tf_op | source)
XLA Modules:
  0.0 559.2 jit_solution(695061584460823528)
XLA Ops:
  7.2 0.0 all-gather.6.cloned.1.call-start
  7.2 0.7 all-gather.6.cloned.1.call-update
  7.9 0.0 all-gather.4.cloned.1.call-start
  7.9 0.7 all-gather.4.cloned.1.call-update
  8.6 0.0 all-reduce.3.cloned.1.call-start
  8.7 39.6 %all-gather.6.cloned.1.call-done = bf16[2048,512]{1,0:T(8,128)(2,1)} async-done(((bf16[128,512]{1,0:T(8,128)(2,1)}), bf16[2048,512]{1,0:T(8,128)(2,1)}) %all-gather.6.cloned.1.call-update) | async-done | bytes 2097168 | tf_op jit(solution)/shard_map/all_gather | solution.py:30
  48.3 1.5 broadcast_select_fusion.1
  49.8 51.1 %all-gather.4.cloned.1.call-done = bf16[2048,1792]{1,0:T(8,128)(2,1)} async-done(((bf16[128,1792]{1,0:T(8,128)(2,1)}), bf16[2048,1792]{1,0:T(8,128)(2,1)}) %all-gather.4.cloned.1.call-update) | async-done | bytes 7340048 | tf_op jit(solution)/shard_map/all_gather | solution.py:29
  100.9 3.4 broadcast_select_fusion
  104.3 0.0 copy-start.1
  104.3 0.0 copy-start.2
  104.3 0.0 all-reduce.3.cloned.1.call-update
  104.3 0.6 copy-done.1
  104.9 25.4 %all-gather = s32[16,1,128]{2,1,0:T(1,128)S(1)} all-gather(s32[1,1,128]{2,1,0:T(1,128)S(1)} %bitcast.5), channel_id=1, replica_groups=mesh['dp'=2,'ctx'=8,'feat'=16] {'dp','ctx'}, dimensions={0}, use_global_device_ids=true | all-gather | bytes 8704 | tf_op jit(solution)/shard_map/all_gather | solution.py:31
  130.3 0.0 copy-done.2
  130.3 0.1 select_reduce_fusion
  130.4 399.4 %all-reduce.3.cloned.1.call-done = (bf16[2048,1792]{1,0:T(8,128)(2,1)}, bf16[2048,512]{1,0:T(8,128)(2,1)}) async-done(((bf16[2048,1792]{1,0:T(8,128)(2,1)}, bf16[2048,512]{1,0:T(8,128)(2,1)}), (bf16[2048,1792]{1,0:T(8,128)(2,1)}, bf16[2048,512]{1,0:T(8,128)(2,1)})) %all-reduce.3.cloned.1.call-update) | async-done | bytes 9437200 | tf_op jit(solution)/shard_map/psum | solution.py:9
  529.8 0.0 copy-start
  529.8 0.0 copy-start.3
  529.8 20.7 %multiply_convert_fusion.1 = bf16[1792,1792]{1,0:T(8,128)(2,1)} fusion(bf16[2048,1792]{1,0:T(8,128)(2,1)} %get-tuple-element.2, bf16[2048,1792]{1,0:T(8,128)(2,1)} %all-gather.4.cloned.1.call-done, f32[2048]{0:T(1024)S(1)} %convert_element_type.26), kind=kOutput, calls=%fused_computation.1 | convolution fusion | flops 13170769920 | bytes 21110784 | tf_op jit(solution)/shard_map/dot_general | solution.py:20
  550.5 0.0 copy-done
  550.5 0.0 copy-done.3
  550.5 2.1 fusion.4
  (1 shorter events, 0.0 us)
Async XLA Ops:
  7.2 41.2 %all-gather.6.cloned.1.call-start = ((), (), s32[]{:S(2)}) async-start(), calls=%async_computation.1 | async-start | bytes 2228224 | tf_op jit(solution)/shard_map/all_gather | solution.py:30
  7.9 93.0 %all-gather.4.cloned.1.call-start = ((), (), s32[]{:S(2)}) async-start(), calls=%async_computation | async-start | bytes 7798784 | tf_op jit(solution)/shard_map/all_gather | solution.py:29
  8.6 521.1 %all-reduce.3.cloned.1.call-start = ((), (), s32[]{:S(2)}) async-start(), calls=%async_computation.2 | async-start | bytes 18874368 | tf_op jit(solution)/shard_map/psum | solution.py:9
  104.3 0.7 copy-start.1
  104.3 26.0 %copy-start.2 = (s32[8]{0:T(128)S(1)}, s32[8]{0:T(128)}, u32[]{:S(2)}) copy-start(s32[8]{0:T(128)} %param.7) | copy-start | bytes 100
  529.8 20.7 %copy-start = (bf16[2048,512]{1,0:T(8,128)(2,1)S(1)}, bf16[2048,512]{1,0:T(8,128)(2,1)}, u32[]{:S(2)}) copy-start(bf16[2048,512]{1,0:T(8,128)(2,1)} %all-gather.6.cloned.1.call-done) | copy-start | bytes 6291460
  529.8 20.7 %copy-start.3 = (bf16[2048,512]{1,0:T(8,128)(2,1)S(1)}, bf16[2048,512]{1,0:T(8,128)(2,1)}, u32[]{:S(2)}) copy-start(bf16[2048,512]{1,0:T(8,128)(2,1)} %get-tuple-element.3) | copy-start | bytes 6291460
Sparse Core Ops, SparseCore 0:
  9.9 38.4 all-gather.5
  50.2 50.6 all-gather.3
  104.4 425.3 all-reduce.2
where the time goes:
time: 559 us
  waiting for transfers between devices  491 us (88%)
  blocking collectives  25.4 us (5%)
  matrix products  22.9 us (4%)
  between operations  13.8 us (2%)
    psum x1, waiting for transfers between devices, from_root(): return lax.psum(block, axis)  399 us
    all_gather x1, waiting for transfers between devices, local(): lax.all_gather(out_grads, ('dp', 'ctx'), axis=0, tiled=True)  51.1 us
    all_gather x1, waiting for transfers between devices, local(): lax.all_gather(acts, ('dp', 'ctx'), axis=0, tiled=True)  39.6 us
    all_gather x1, blocking collectives, local(): lax.all_gather(domain_ids, ('dp', 'ctx'), axis=0, tiled=True)  25.4 us
    dot_general x2, matrix products, contract_tokens(): lax.dot_general(left, right, (((0,), (0,)), ((), ())), preferred_element_...  22.9 us
  transfers between devices with their start and end apart: 3, of which 3 were waited for; matrix products, arithmetic and copies ran while one was open for 0% of the time, Pallas kernels for 0%

commit v1 on v0

v1 whole, which is shorter than its diff:
```python
import jax
import jax.numpy as jnp
from jax import lax
from jax.sharding import PartitionSpec as P

ROWS = ("dp", "ctx")


def token_weights(tok_ids, domain_weights):
    labels = jnp.arange(domain_weights.shape[0], dtype=jnp.int32)
    match = tok_ids[:, None] == labels[None, :]
    return jnp.sum(jnp.where(match, domain_weights[None, :], 0), axis=1).astype(jnp.float32)


def contract_tokens(left, right):
    return lax.dot_general(
        left, right, (((0,), (0,)), ((), ())), preferred_element_type=jnp.float32
    )


def transpose_pairs(n_rows, n_cols):
    return [(c * n_cols + r, r * n_cols + c) for r in range(n_rows) for c in range(n_cols)]


def local(out_grads, acts, domain_ids, domain_weights):
    n_rows = lax.axis_size(ROWS)
    n_cols = lax.axis_size("feat")
    assert n_rows == n_cols
    inv_count = 1.0 / (out_grads.shape[0] * n_rows)
    width_g = out_grads.shape[1]
    both = jnp.concatenate([out_grads, acts], axis=1)
    tok_weight = token_weights(domain_ids, domain_weights)
    weighted = (tok_weight[:, None] * both.astype(jnp.float32)).astype(jnp.bfloat16)
    cols = lax.all_gather(weighted, ROWS, axis=0, tiled=True)
    swapped = lax.ppermute(both, ROWS + ("feat",), transpose_pairs(n_rows, n_cols))
    rows = lax.all_gather(swapped, "feat", axis=0, tiled=True)
    grad_sum = contract_tokens(rows[:, :width_g], cols[:, :width_g])
    act_sum = contract_tokens(rows[:, width_g:], cols[:, width_g:])
    grad_factor = (grad_sum * inv_count).astype(jnp.bfloat16)
    act_factor = (act_sum * inv_count).astype(jnp.bfloat16)
    return (grad_factor, act_factor)


def solution(mesh):
    in_specs = (P(ROWS, "feat"), P(ROWS, "feat"), P(ROWS), P())
    out_specs = (P(ROWS, "feat"), P(ROWS, "feat"))
    return jax.shard_map(local, mesh=mesh, in_specs=in_specs, out_specs=out_specs, check_vma=False)
```

time: 559 us -> 253 us (0.45)
  waiting for transfers between devices: 491 us -> 198 us
  blocking collectives: 25.4 us -> 0 us
  starting transfers between devices: 0.11 us -> 10.5 us
    psum x1 -> x0, waiting for transfers between devices: 399 us -> none  [from_root(): return lax.psum(block, axis)]
    all_gather x2, waiting for transfers between devices: 90.7 us -> 165 us  [the longest x1 129 us: local(): rows = lax.all_gather(swapped, 'feat', axis=0, tiled=True)]
    ppermute x0 -> x1, waiting for transfers between devices: none -> 33.9 us  [local(): lax.ppermute(both, ROWS + ('feat',), transpose_pairs(n_rows, n_cols))]
    all_gather x1 -> x0, blocking collectives: 25.4 us -> none  [local(): lax.all_gather(domain_ids, ('dp', 'ctx'), axis=0, tiled=True)]
    ppermute x0 -> x1, starting transfers between devices: none -> 10.4 us  [local(): lax.ppermute(both, ROWS + ('feat',), transpose_pairs(n_rows, n_cols))]
where the time goes in v1:
time: 253 us; the launch traced here: 252 us
  waiting for transfers between devices  198 us (78%)
  matrix products  24.1 us (10%)
  between operations  14.1 us (6%)
  starting transfers between devices  10.5 us (4%)
  local copies, waits for them, and re-layouts  2.79 us (1%)
    all_gather x1, waiting for transfers between devices, local(): rows = lax.all_gather(swapped, 'feat', axis=0, tiled=True)  129 us
    all_gather x1, waiting for transfers between devices, local(): cols = lax.all_gather(weighted, ROWS, axis=0, tiled=True)  35.4 us
    ppermute x1, waiting for transfers between devices, local(): lax.ppermute(both, ROWS + ('feat',), transpose_pairs(n_rows, n_cols))  33.9 us
    dot_general x2, matrix products, contract_tokens(): lax.dot_general(left, right, (((0,), (0,)), ((), ())), preferred_element_...  24.1 us
    ppermute x1, starting transfers between devices, local(): lax.ppermute(both, ROWS + ('feat',), transpose_pairs(n_rows, n_cols))  10.4 us
  transfers between devices with their start and end apart: 3, of which 3 were waited for; matrix products, arithmetic and copies ran while one was open for 0% of the time, Pallas kernels for 0%

profile of v1, /device:TPU:41, one launch (start us, length us, event | category | flops | bytes accessed | tf_op | source)
XLA Modules:
  0.0 251.6 jit_solution(7597429235137689880)
XLA Ops:
  7.2 0.0 all-gather.5.cloned.1.call-start
  7.2 0.8 select_reduce_fusion
  8.0 1.0 constant_dynamic-update-slice_fusion.1
  9.0 0.9 constant_dynamic-update-slice_fusion
  9.9 1.0 multiply_convert_fusion.1
  10.9 0.0 all-gather.5.cloned.1.call-update
  10.9 0.0 all-gather.3.cloned.1.call-start
  11.0 10.4 %collective-permute-start = (bf16[128,2304]{1,0:T(8,128)(2,1)S(1)}, bf16[128,2304]{1,0:T(8,128)(2,1)S(1)}, u32[]{:S(2)}, u32[]{:S(2)}) collective-permute-start(bf16[128,2304]{1,0:T(8,128)(2,1)S(1)} %constant_dynamic-update-slice_fusion), channel_id=1, source_target_pairs={{0,0},{16,1},{32,2},{48,3},{64,4},{80,5},{96,6},{112,7},{128,8},{1... | collective-permute-start | bytes 1769480 | tf_op jit(solution)/shard_map/ppermute | solution.py:35
  21.4 33.9 %collective-permute-done = bf16[128,2304]{1,0:T(8,128)(2,1)S(1)} collective-permute-done((bf16[128,2304]{1,0:T(8,128)(2,1)S(1)}, bf16[128,2304]{1,0:T(8,128)(2,1)S(1)}, u32[]{:S(2)}, u32[]{:S(2)}) %collective-permute-start) | collective-permute-done | bytes 589856 | tf_op jit(solution)/shard_map/ppermute | solution.py:35
  55.3 0.0 copy-start
  55.3 0.8 copy-done
  56.1 0.0 all-gather.3.cloned.1.call-update
  56.1 35.4 %all-gather.5.cloned.1.call-done = bf16[2048,2304]{1,0:T(8,128)(2,1)} async-done(((bf16[128,2304]{1,0:T(8,128)(2,1)}), bf16[2048,2304]{1,0:T(8,128)(2,1)}) %all-gather.5.cloned.1.call-update) | async-done | bytes 9437200 | tf_op jit(solution)/shard_map/all_gather | solution.py:34
  91.5 129.2 %all-gather.3.cloned.1.call-done = bf16[2048,2304]{1,0:T(8,128)(2,1)} async-done(((bf16[128,2304]{1,0:T(8,128)(2,1)}), bf16[2048,2304]{1,0:T(8,128)(2,1)}) %all-gather.3.cloned.1.call-update) | async-done | bytes 9437200 | tf_op jit(solution)/shard_map/all_gather | solution.py:36
  220.7 4.3 %fusion.10 = bf16[512,512]{1,0:T(8,128)(2,1)} fusion(bf16[2048,2304]{1,0:T(8,128)(2,1)} %all-gather.5.cloned.1.call-done, bf16[2048,2304]{1,0:T(8,128)(2,1)} %all-gather.3.cloned.1.call-done), kind=kOutput, calls=%fused_computation.7 | convolution fusion | flops 1074266112 | bytes 4718592 | tf_op jit(solution)/shard_map/dot_general | solution.py:16
  225.0 19.7 %multiply_convert_fusion = bf16[1792,1792]{1,0:T(8,128)(2,1)} fusion(bf16[2048,2304]{1,0:T(8,128)(2,1)} %all-gather.5.cloned.1.call-done, bf16[2048,2304]{1,0:T(8,128)(2,1)} %all-gather.3.cloned.1.call-done), kind=kOutput, calls=%fused_computation | convolution fusion | flops 13159759872 | bytes 21102592 | tf_op jit(solution)/shard_map/dot_general | solution.py:16
  (1 shorter events, 0.0 us)
Async XLA Ops:
  7.2 84.4 %all-gather.5.cloned.1.call-start = ((), (), s32[]{:S(2)}) async-start(), calls=%async_computation.1 | async-start | bytes 10027008 | tf_op jit(solution)/shard_map/all_gather | solution.py:34
  10.9 209.8 %all-gather.3.cloned.1.call-start = ((), (), s32[]{:S(2)}) async-start(), calls=%async_computation | async-start | bytes 10027008 | tf_op jit(solution)/shard_map/all_gather | solution.py:36
  11.0 44.3 %collective-permute-start = (bf16[128,2304]{1,0:T(8,128)(2,1)S(1)}, bf16[128,2304]{1,0:T(8,128)(2,1)S(1)}, u32[]{:S(2)}, u32[]{:S(2)}) collective-permute-start(bf16[128,2304]{1,0:T(8,128)(2,1)S(1)} %constant_dynamic-update-slice_fusion), channel_id=1, source_target_pairs={{0,0},{16,1},{32,2},{48,3},{64,4},{80,5},{96,6},{112,7},{128,8},{1... | collective-permute-start | bytes 1769480 | tf_op jit(solution)/shard_map/ppermute | solution.py:35
  55.3 0.8 copy-start
Sparse Core Ops, SparseCore 0:
  11.1 80.4 all-gather.4
  94.0 126.6 all-gather.2

commit v2 on v1

--- a/solution.py
+++ b/solution.py
@@ -4,6 +4,7 @@
 from jax.sharding import PartitionSpec as P
 
 ROWS = ("dp", "ctx")
+PAIR = 2
 
 
 def token_weights(tok_ids, domain_weights):
@@ -18,22 +19,59 @@
     )
 
 
-def transpose_pairs(n_rows, n_cols):
-    return [(c * n_cols + r, r * n_cols + c) for r in range(n_rows) for c in range(n_cols)]
+def split_row(r, n_ring):
+    per_dp = n_ring * PAIR
+    return r // per_dp, (r % per_dp) // PAIR, r % PAIR
+
+
+def token_block(r, p, n_dp, n_ring):
+    dp, y, z = split_row(r, n_ring)
+    ddp, dy, dz = split_row(p, n_ring)
+    return ((dp + ddp) % n_dp) * n_ring * PAIR + ((y + dy) % n_ring) * PAIR + (z + dz) % PAIR
+
+
+def transpose_pairs(n_rows, n_cols, n_dp, n_ring):
+    return [(token_block(r, c, n_dp, n_ring) * n_cols + r, r * n_cols + c)
+            for r in range(n_rows) for c in range(n_cols)]
+
+
+def ctx_shift(n_ring, dy, dz):
+    pairs = []
+    for y in range(n_ring):
+        for z in range(PAIR):
+            src = ((y + dy) % n_ring) * PAIR + (z + dz) % PAIR
+            pairs.append((src, y * PAIR + z))
+    return pairs
+
+
+def gather_columns(block, n_dp, n_ring):
+    half = block.shape[0]
+    near = lax.ppermute(block, "ctx", ctx_shift(n_ring, 0, 1))
+    own = jnp.concatenate([block, near], axis=0)
+    ahead = lax.ppermute(own, "ctx", ctx_shift(n_ring, 1, 0))
+    behind = lax.ppermute(own, "ctx", ctx_shift(n_ring, -1, 0))
+    far_a = lax.ppermute(ahead[:half], "ctx", ctx_shift(n_ring, 1, 0))
+    far_b = lax.ppermute(behind[half:], "ctx", ctx_shift(n_ring, -1, 0))
+    mine = jnp.concatenate([own, ahead, far_a, far_b, behind], axis=0)
+    other = lax.ppermute(mine, "dp", [(1, 0), (0, 1)])
+    return jnp.concatenate([mine, other], axis=0)
 
 
 def local(out_grads, acts, domain_ids, domain_weights):
-    n_rows = lax.axis_size(ROWS)
+    n_dp = lax.axis_size("dp")
+    n_ctx = lax.axis_size("ctx")
+    n_rows = n_dp * n_ctx
     n_cols = lax.axis_size("feat")
-    assert n_rows == n_cols
+    n_ring = n_ctx // PAIR
+    assert n_rows == n_cols and n_dp == 2 and n_ring == 4 and n_ctx % PAIR == 0
     inv_count = 1.0 / (out_grads.shape[0] * n_rows)
     width_g = out_grads.shape[1]
     both = jnp.concatenate([out_grads, acts], axis=1)
     tok_weight = token_weights(domain_ids, domain_weights)
     weighted = (tok_weight[:, None] * both.astype(jnp.float32)).astype(jnp.bfloat16)
-    cols = lax.all_gather(weighted, ROWS, axis=0, tiled=True)
-    swapped = lax.ppermute(both, ROWS + ("feat",), transpose_pairs(n_rows, n_cols))
+    swapped = lax.ppermute(both, ROWS + ("feat",), transpose_pairs(n_rows, n_cols, n_dp, n_ring))
     rows = lax.all_gather(swapped, "feat", axis=0, tiled=True)
+    cols = gather_columns(weighted, n_dp, n_ring)
     grad_sum = contract_tokens(rows[:, :width_g], cols[:, :width_g])
     act_sum = contract_tokens(rows[:, width_g:], cols[:, width_g:])
     grad_factor = (grad_sum * inv_count).astype(jnp.bfloat16)

time: 253 us -> 206 us (0.81)
  waiting for transfers between devices: 198 us -> 139 us
  local copies, waits for them, and re-layouts: 2.79 us -> 11.2 us
  starting transfers between devices: 10.5 us -> 16.2 us
    all_gather x1, waiting for transfers between devices: 129 us -> 55.4 us  [local(): rows = lax.all_gather(swapped, 'feat', axis=0, tiled=True)]
    ppermute x1 -> x7, waiting for transfers between devices: 33.9 us -> 83.7 us  [the longest x1 24.8 us: gather_columns(): ahead = lax.ppermute(own, 'ctx', ctx_shift(n_ring, 1, 0))]
    all_gather x1 -> x0, waiting for transfers between devices: 35.4 us -> none  [local(): cols = lax.all_gather(weighted, ROWS, axis=0, tiled=True)]
    ppermute x1 -> x7, starting transfers between devices: 10.4 us -> 16.1 us  [the longest x1 10.4 us: local(): lax.ppermute(both, ROWS + ('feat',), transpose_pairs(n_rows, n_cols, n_dp...]
    unnamed x3 -> x8, local copies, waits for them, and re-layouts: 1.88 us -> 6.64 us
    concatenate x0 -> x2, local copies, waits for them, and re-layouts: none -> 3.59 us  [the longest x1 2.42 us: gather_columns(): return jnp.concatenate([mine, other], axis=0)]
  transfers between devices with their start and end apart: 3 -> 8, of which waited for: 3 -> 7; matrix products, arithmetic and copies ran while one was open for 0% -> 5% of each run, Pallas kernels for 0% -> 0%
where the time goes in v2:
time: 206 us
  waiting for transfers between devices  139 us (67%)
  matrix products  24.1 us (12%)
  starting transfers between devices  16.2 us (8%)
  between operations  14.1 us (7%)
  local copies, waits for them, and re-layouts  11.2 us (5%)
    all_gather x1, waiting for transfers between devices, local(): rows = lax.all_gather(swapped, 'feat', axis=0, tiled=True)  55.4 us
    ppermute x1, waiting for transfers between devices, gather_columns(): ahead = lax.ppermute(own, 'ctx', ctx_shift(n_ring, 1, 0))  24.8 us
    ppermute x1, waiting for transfers between devices, local(): lax.ppermute(both, ROWS + ('feat',), transpose_pairs(n_rows, n_cols, n_dp...  24.5 us
    dot_general x2, matrix products, contract_tokens(): lax.dot_general(left, right, (((0,), (0,)), ((), ())), preferred_element_...  24.1 us
    ppermute x1, waiting for transfers between devices, gather_columns(): near = lax.ppermute(block, 'ctx', ctx_shift(n_ring, 0, 1))  15.2 us
    ppermute x1, starting transfers between devices, local(): lax.ppermute(both, ROWS + ('feat',), transpose_pairs(n_rows, n_cols, n_dp...  10.4 us
    ppermute x1, waiting for transfers between devices, gather_columns(): far_a = lax.ppermute(ahead[:half], 'ctx', ctx_shift(n_ring, 1, 0))  10 us
    ppermute x1, waiting for transfers between devices, gather_columns(): other = lax.ppermute(mine, 'dp', [(1, 0), (0, 1)])  7.54 us
  transfers between devices with their start and end apart: 8, of which 7 were waited for; matrix products, arithmetic and copies ran while one was open for 5% of the time, Pallas kernels for 0%

profile of v2, /device:TPU:41, one launch (start us, length us, event | category | flops | bytes accessed | tf_op | source)
XLA Modules:
  0.0 205.8 jit_solution(11662627242992253323)
XLA Ops:
  7.2 0.0 all-gather.2.cloned.1.call-start
  7.2 1.0 constant_dynamic-update-slice_fusion.1
  8.3 0.9 constant_dynamic-update-slice_fusion
  9.2 10.4 %collective-permute-start = (bf16[128,2304]{1,0:T(8,128)(2,1)S(1)}, bf16[128,2304]{1,0:T(8,128)(2,1)S(1)}, u32[]{:S(2)}, u32[]{:S(2)}) collective-permute-start(bf16[128,2304]{1,0:T(8,128)(2,1)S(1)} %constant_dynamic-update-slice_fusion), channel_id=1, source_target_pairs={{0,0},{16,1},{32,2},{48,3},{64,4},{80,5},{96,6},{112,7},{128,8},{1... | collective-permute-start | bytes 1769480 | tf_op jit(solution)/shard_map/ppermute | solution.py:72
  19.6 24.5 %collective-permute-done = bf16[128,2304]{1,0:T(8,128)(2,1)S(1)} collective-permute-done((bf16[128,2304]{1,0:T(8,128)(2,1)S(1)}, bf16[128,2304]{1,0:T(8,128)(2,1)S(1)}, u32[]{:S(2)}, u32[]{:S(2)}) %collective-permute-start) | collective-permute-done | bytes 589856 | tf_op jit(solution)/shard_map/ppermute | solution.py:72
  44.1 0.0 copy-start
  44.1 0.8 copy-done
  44.9 0.0 all-gather.2.cloned.1.call-update
  44.9 0.8 select_reduce_fusion
  45.7 0.2 constant_dynamic-update-slice_fusion.7
  45.9 0.1 collective-permute-start.1
  46.0 15.2 %collective-permute-done.1 = bf16[128,2304]{1,0:T(8,128)(2,1)S(1)} collective-permute-done((bf16[128,2304]{1,0:T(8,128)(2,1)S(1)}, bf16[128,2304]{1,0:T(8,128)(2,1)S(1)}, u32[]{:S(2)}, u32[]{:S(2)}) %collective-permute-start.1) | collective-permute-done | bytes 589856 | tf_op jit(solution)/shard_map/ppermute | solution.py:49
  61.1 0.1 pad_maximum_fusion
  61.2 0.1 collective-permute-start.2
  61.3 1.5 collective-permute-start.4
  62.8 0.9 constant_dynamic-update-slice_fusion.14
  63.6 24.8 %collective-permute-done.2 = bf16[256,2304]{1,0:T(8,128)(2,1)S(1)} collective-permute-done((bf16[256,2304]{1,0:T(8,128)(2,1)S(1)}, bf16[256,2304]{1,0:T(8,128)(2,1)S(1)}, u32[]{:S(2)}, u32[]{:S(2)}) %collective-permute-start.2) | collective-permute-done | bytes 1179680 | tf_op jit(solution)/shard_map/ppermute | solution.py:51
  88.5 0.4 collective-permute-start.3
  88.9 0.9 constant_dynamic-update-slice_fusion.6
  89.8 0.0 collective-permute-done.4
  89.9 1.2 collective-permute-start.5
  91.1 1.2 constant_dynamic-update-slice_fusion.5
  92.3 10.0 %collective-permute-done.3 = bf16[128,2304]{1,0:T(8,128)(2,1)S(1)} collective-permute-done((bf16[128,2304]{1,0:T(8,128)(2,1)S(1)}, bf16[128,2304]{1,0:T(8,128)(2,1)S(1)}, u32[]{:S(2)}, u32[]{:S(2)}) %collective-permute-start.3) | collective-permute-done | bytes 589856 | tf_op jit(solution)/shard_map/ppermute | solution.py:53
  102.3 0.9 constant_dynamic-update-slice_fusion.4
  103.2 1.7 collective-permute-done.5
  104.9 0.9 constant_dynamic-update-slice_fusion.3
  105.8 1.2 constant_dynamic-update-slice_fusion.2
  106.9 2.5 %collective-permute-start.6 = (bf16[1024,2304]{1,0:T(8,128)(2,1)S(1)}, bf16[1024,2304]{1,0:T(8,128)(2,1)S(1)}, u32[]{:S(2)}, u32[]{:S(2)}) collective-permute-start(bf16[1024,2304]{1,0:T(8,128)(2,1)S(1)} %get-tuple-element.4), channel_id=1, source_target_pairs={{128,0},{0,128},{129,1},{1,129},{130,2},{2,130},{131,3},{3,131},{1... | collective-permute-start | bytes 14155784 | tf_op jit(solution)/shard_map/ppermute | solution.py:56
  109.4 7.5 %collective-permute-done.6 = bf16[1024,2304]{1,0:T(8,128)(2,1)S(1)} collective-permute-done((bf16[1024,2304]{1,0:T(8,128)(2,1)S(1)}, bf16[1024,2304]{1,0:T(8,128)(2,1)S(1)}, u32[]{:S(2)}, u32[]{:S(2)}) %collective-permute-start.6) | collective-permute-done | bytes 4718624 | tf_op jit(solution)/shard_map/ppermute | solution.py:56
  117.0 2.4 %constant_dynamic-update-slice_fusion.8 = bf16[2048,2304]{1,0:T(8,128)(2,1)} fusion(bf16[2048,2304]{1,0:T(8,128)(2,1)} %get-tuple-element.5, bf16[1024,2304]{1,0:T(8,128)(2,1)S(1)} %collective-permute-done.6), kind=kLoop, calls=%fused_computation.18 | loop fusion | bytes 9437184 | tf_op jit(solution)/shard_map/concatenate | solution.py:57
  119.4 55.4 %all-gather.2.cloned.1.call-done = bf16[2048,2304]{1,0:T(8,128)(2,1)} async-done(((bf16[128,2304]{1,0:T(8,128)(2,1)}), bf16[2048,2304]{1,0:T(8,128)(2,1)}) %all-gather.2.cloned.1.call-update) | async-done | bytes 9437200 | tf_op jit(solution)/shard_map/all_gather | solution.py:73
  174.9 19.7 %multiply_convert_fusion = bf16[1792,1792]{1,0:T(8,128)(2,1)} fusion(bf16[2048,2304]{1,0:T(8,128)(2,1)} %constant_dynamic-update-slice_fusion.8, bf16[2048,2304]{1,0:T(8,128)(2,1)} %all-gather.2.cloned.1.call-done), kind=kOutput, calls=%fused_computation | convolution fusion | flops 13159759872 | bytes 21102592 | tf_op jit(solution)/shard_map/dot_general | solution.py:17
  194.6 4.3 %fusion.10 = bf16[512,512]{1,0:T(8,128)(2,1)} fusion(bf16[2048,2304]{1,0:T(8,128)(2,1)} %constant_dynamic-update-slice_fusion.8, bf16[2048,2304]{1,0:T(8,128)(2,1)} %all-gather.2.cloned.1.call-done), kind=kOutput, calls=%fused_computation.7 | convolution fusion | flops 1074266112 | bytes 4718592 | tf_op jit(solution)/shard_map/dot_general | solution.py:17
  (3 shorter events, 0.1 us)
Async XLA Ops:
  7.2 167.7 %all-gather.2.cloned.1.call-start = ((), (), s32[]{:S(2)}) async-start(), calls=%async_computation | async-start | bytes 10027008 | tf_op jit(solution)/shard_map/all_gather | solution.py:73
  9.2 34.9 %collective-permute-start = (bf16[128,2304]{1,0:T(8,128)(2,1)S(1)}, bf16[128,2304]{1,0:T(8,128)(2,1)S(1)}, u32[]{:S(2)}, u32[]{:S(2)}) collective-permute-start(bf16[128,2304]{1,0:T(8,128)(2,1)S(1)} %constant_dynamic-update-slice_fusion), channel_id=1, source_target_pairs={{0,0},{16,1},{32,2},{48,3},{64,4},{80,5},{96,6},{112,7},{128,8},{1... | collective-permute-start | bytes 1769480 | tf_op jit(solution)/shard_map/ppermute | solution.py:72
  44.1 0.8 copy-start
  45.9 15.3 %collective-permute-start.1 = (bf16[128,2304]{1,0:T(8,128)(2,1)S(1)}, bf16[128,2304]{1,0:T(8,128)(2,1)S(1)}, u32[]{:S(2)}, u32[]{:S(2)}) collective-permute-start(bf16[128,2304]{1,0:T(8,128)(2,1)S(1)} %get-tuple-element.3), channel_id=1, source_target_pairs={{16,0},{0,16},{48,32},{32,48},{80,64},{64,80},{112,96},{96,112},{1... | collective-permute-start | bytes 1769480 | tf_op jit(solution)/shard_map/ppermute | solution.py:49
  61.2 27.2 %collective-permute-start.2 = (bf16[256,2304]{1,0:T(8,128)(2,1)S(1)}, bf16[256,2304]{1,0:T(8,128)(2,1)S(1)}, u32[]{:S(2)}, u32[]{:S(2)}) collective-permute-start(bf16[256,2304]{1,0:T(8,128)(2,1)S(1)} %pad_maximum_fusion), channel_id=1, source_target_pairs={{32,0},{48,16},{64,32},{80,48},{96,64},{112,80},{0,96},{16,112},{3... | collective-permute-start | bytes 3538952 | tf_op jit(solution)/shard_map/ppermute | solution.py:51
  61.3 28.5 %collective-permute-start.4 = (bf16[256,2304]{1,0:T(8,128)(2,1)S(1)}, bf16[256,2304]{1,0:T(8,128)(2,1)S(1)}, u32[]{:S(2)}, u32[]{:S(2)}) collective-permute-start(bf16[256,2304]{1,0:T(8,128)(2,1)S(1)} %pad_maximum_fusion), channel_id=1, source_target_pairs={{96,0},{112,16},{0,32},{16,48},{32,64},{48,80},{64,96},{80,112},{9... | collective-permute-start | bytes 3538952 | tf_op jit(solution)/shard_map/ppermute | solution.py:52
  88.5 13.8 %collective-permute-start.3 = (bf16[128,2304]{1,0:T(8,128)(2,1)S(1)}, bf16[128,2304]{1,0:T(8,128)(2,1)S(1)}, u32[]{:S(2)}, u32[]{:S(2)}) collective-permute-start(bf16[128,2304]{1,0:T(8,128)(2,1)S(1)} %slice.25), channel_id=1, source_target_pairs={{32,0},{48,16},{64,32},{80,48},{96,64},{112,80},{0,96},{16,112},{3... | collective-permute-start | bytes 1769480 | tf_op jit(solution)/shard_map/ppermute | solution.py:53
  89.9 15.0 %collective-permute-start.5 = (bf16[128,2304]{1,0:T(8,128)(2,1)S(1)}, bf16[128,2304]{1,0:T(8,128)(2,1)S(1)}, u32[]{:S(2)}, u32[]{:S(2)}) collective-permute-start(bf16[128,2304]{1,0:T(8,128)(2,1)S(1)} %slice.26), channel_id=1, source_target_pairs={{96,0},{112,16},{0,32},{16,48},{32,64},{48,80},{64,96},{80,112},{9... | collective-permute-start | bytes 1769480 | tf_op jit(solution)/shard_map/ppermute | solution.py:54
  106.9 10.0 %collective-permute-start.6 = (bf16[1024,2304]{1,0:T(8,128)(2,1)S(1)}, bf16[1024,2304]{1,0:T(8,128)(2,1)S(1)}, u32[]{:S(2)}, u32[]{:S(2)}) collective-permute-start(bf16[1024,2304]{1,0:T(8,128)(2,1)S(1)} %get-tuple-element.4), channel_id=1, source_target_pairs={{128,0},{0,128},{129,1},{1,129},{130,2},{2,130},{131,3},{3,131},{1... | collective-permute-start | bytes 14155784 | tf_op jit(solution)/shard_map/ppermute | solution.py:56
Sparse Core Ops, SparseCore 0:
  45.1 129.7 all-gather.1

commit v3 on v1

--- a/solution.py
+++ b/solution.py
@@ -4,6 +4,7 @@
 from jax.sharding import PartitionSpec as P
 
 ROWS = ("dp", "ctx")
+SIDE = 4
 
 
 def token_weights(tok_ids, domain_weights):
@@ -22,10 +23,40 @@
     return [(c * n_cols + r, r * n_cols + c) for r in range(n_rows) for c in range(n_cols)]
 
 
+def feat_shift(dx, dz):
+    pairs = []
+    for x in range(SIDE):
+        for z in range(SIDE):
+            pairs.append((((x + dx) % SIDE) * SIDE + (z + dz) % SIDE, x * SIDE + z))
+    return pairs
+
+
+def ring_gather(block, dx, dz):
+    half = block.shape[0] // 2
+    ahead = lax.ppermute(block, "feat", feat_shift(dx, dz))
+    behind = lax.ppermute(block, "feat", feat_shift(-dx, -dz))
+    far_a = lax.ppermute(ahead[:half], "feat", feat_shift(dx, dz))
+    far_b = lax.ppermute(behind[half:], "feat", feat_shift(-dx, -dz))
+    return [block, ahead, jnp.concatenate([far_a, far_b], axis=0), behind]
+
+
+def gather_rows(piece):
+    size = piece.shape[0]
+    f = lax.axis_index("feat")
+    x, z = f // SIDE, f % SIDE
+    line = jnp.concatenate(ring_gather(piece, 0, 1), axis=0)
+    rows = jnp.zeros((SIDE * SIDE * size, piece.shape[1]), piece.dtype)
+    for dx, block in enumerate(ring_gather(line, 1, 0)):
+        for dz in range(SIDE):
+            at = (((x + dx) % SIDE) * SIDE + (z + dz) % SIDE) * size
+            rows = lax.dynamic_update_slice(rows, block[dz * size:(dz + 1) * size], (at, 0))
+    return rows
+
+
 def local(out_grads, acts, domain_ids, domain_weights):
     n_rows = lax.axis_size(ROWS)
     n_cols = lax.axis_size("feat")
-    assert n_rows == n_cols
+    assert n_rows == n_cols and n_cols == SIDE * SIDE
     inv_count = 1.0 / (out_grads.shape[0] * n_rows)
     width_g = out_grads.shape[1]
     both = jnp.concatenate([out_grads, acts], axis=1)
@@ -33,7 +64,7 @@
     weighted = (tok_weight[:, None] * both.astype(jnp.float32)).astype(jnp.bfloat16)
     cols = lax.all_gather(weighted, ROWS, axis=0, tiled=True)
     swapped = lax.ppermute(both, ROWS + ("feat",), transpose_pairs(n_rows, n_cols))
-    rows = lax.all_gather(swapped, "feat", axis=0, tiled=True)
+    rows = gather_rows(swapped)
     grad_sum = contract_tokens(rows[:, :width_g], cols[:, :width_g])
     act_sum = contract_tokens(rows[:, width_g:], cols[:, width_g:])
     grad_factor = (grad_sum * inv_count).astype(jnp.bfloat16)

time: 253 us -> 257 us (1.016)
  the two profiles are of different devices: /device:TPU:41 before, /device:TPU:1 now
where the time goes in v3:
time: 257 us; the launch traced here: 256 us
  waiting for transfers between devices  130 us (51%)
  starting transfers between devices  57.9 us (23%)
  local copies, waits for them, and re-layouts  27.1 us (11%)
  matrix products  24.1 us (9%)
  between operations  14.1 us (5%)
  other arithmetic  2.62 us (1%)
    ppermute x2, waiting for transfers between devices, ring_gather(): ahead = lax.ppermute(block, 'feat', feat_shift(dx, dz))  67.8 us
    ppermute x2, starting transfers between devices, ring_gather(): ahead = lax.ppermute(block, 'feat', feat_shift(dx, dz))  45.2 us
    dot_general x2, matrix products, contract_tokens(): lax.dot_general(left, right, (((0,), (0,)), ((), ())), preferred_element_...  24.1 us
    ppermute x2, waiting for transfers between devices, ring_gather(): far_b = lax.ppermute(behind[half:], 'feat', feat_shift(-dx, -dz))  21.2 us
    ppermute x2, waiting for transfers between devices, ring_gather(): far_a = lax.ppermute(ahead[:half], 'feat', feat_shift(dx, dz))  19 us
    ppermute x2, waiting for transfers between devices, ring_gather(): behind = lax.ppermute(block, 'feat', feat_shift(-dx, -dz))  14.7 us
    dynamic_update_slice x12, local copies, waits for them, and re-layouts, gather_rows(): lax.dynamic_update_slice(rows, block[dz * size:(dz + 1) * size], (at, 0))  14.7 us
    ppermute x1, waiting for transfers between devices, local(): lax.ppermute(both, ROWS + ('feat',), transpose_pairs(n_rows, n_cols))  7.62 us
  transfers between devices with their start and end apart: 10, of which 7 were waited for; matrix products, arithmetic and copies ran while one was open for 10% of the time, Pallas kernels for 0%

profile of v3, /device:TPU:1, one launch (start us, length us, event | category | flops | bytes accessed | tf_op | source)
XLA Modules:
  0.0 256.1 jit_solution(14906174080535781519)
XLA Ops:
  7.2 0.0 all-gather.2.cloned.1.call-start
  7.2 1.0 constant_dynamic-update-slice_fusion.1
  8.3 0.8 select_reduce_fusion
  9.0 0.9 constant_dynamic-update-slice_fusion
  9.9 1.0 multiply_convert_fusion.1
  10.9 0.0 all-gather.2.cloned.1.call-update
  11.0 6.1 %collective-permute-start = (bf16[128,2304]{1,0:T(8,128)(2,1)S(1)}, bf16[128,2304]{1,0:T(8,128)(2,1)S(1)}, u32[]{:S(2)}, u32[]{:S(2)}) collective-permute-start(bf16[128,2304]{1,0:T(8,128)(2,1)S(1)} %constant_dynamic-update-slice_fusion), channel_id=1, source_target_pairs={{0,0},{16,1},{32,2},{48,3},{64,4},{80,5},{96,6},{112,7},{128,8},{1... | collective-permute-start | bytes 1769480 | tf_op jit(solution)/shard_map/ppermute | solution.py:66
  17.0 7.6 %collective-permute-done = bf16[128,2304]{1,0:T(8,128)(2,1)S(1)} collective-permute-done((bf16[128,2304]{1,0:T(8,128)(2,1)S(1)}, bf16[128,2304]{1,0:T(8,128)(2,1)S(1)}, u32[]{:S(2)}, u32[]{:S(2)}) %collective-permute-start) | collective-permute-done | bytes 589856 | tf_op jit(solution)/shard_map/ppermute | solution.py:66
  24.7 29.8 %collective-permute-start.1 = (bf16[128,2304]{1,0:T(8,128)(2,1)S(1)}, bf16[128,2304]{1,0:T(8,128)(2,1)S(1)}, u32[]{:S(2)}, u32[]{:S(2)}) collective-permute-start(bf16[128,2304]{1,0:T(8,128)(2,1)S(1)} %collective-permute-done), channel_id=1, source_target_pairs={{1,0},{2,1},{3,2},{0,3},{5,4},{6,5},{7,6},{4,7},{9,8},{10,9},{11,1... | collective-permute-start | bytes 1769480 | tf_op jit(solution)/shard_map/ppermute | solution.py:36
  54.4 0.0 collective-permute-start.3
  54.5 4.3 %broadcast_in_dim.19 = bf16[2048,2304]{1,0:T(8,128)(2,1)} broadcast(bf16[]{:T(256)} %constant.112.clone.1), dimensions={} | broadcast | bytes 9437186 | tf_op jit(solution)/shard_map/broadcast_in_dim | solution.py:48
  58.7 1.1 constant_dynamic-update-slice_fusion.6
  59.8 16.8 %collective-permute-done.1 = bf16[128,2304]{1,0:T(8,128)(2,1)S(1)} collective-permute-done((bf16[128,2304]{1,0:T(8,128)(2,1)S(1)}, bf16[128,2304]{1,0:T(8,128)(2,1)S(1)}, u32[]{:S(2)}, u32[]{:S(2)}) %collective-permute-start.1) | collective-permute-done | bytes 589856 | tf_op jit(solution)/shard_map/ppermute | solution.py:36
  76.7 4.1 %collective-permute-start.2 = (bf16[64,2304]{1,0:T(8,128)(2,1)S(1)}, bf16[64,2304]{1,0:T(8,128)(2,1)S(1)}, u32[]{:S(2)}, u32[]{:S(2)}) collective-permute-start(bf16[64,2304]{1,0:T(8,128)(2,1)S(1)} %slice.80), channel_id=1, source_target_pairs={{1,0},{2,1},{3,2},{0,3},{5,4},{6,5},{7,6},{4,7},{9,8},{10,9},{11,1... | collective-permute-start | bytes 884744 | tf_op jit(solution)/shard_map/ppermute | solution.py:38
  80.8 14.7 %collective-permute-done.3 = bf16[128,2304]{1,0:T(8,128)(2,1)S(1)} collective-permute-done((bf16[128,2304]{1,0:T(8,128)(2,1)S(1)}, bf16[128,2304]{1,0:T(8,128)(2,1)S(1)}, u32[]{:S(2)}, u32[]{:S(2)}) %collective-permute-start.3) | collective-permute-done | bytes 589856 | tf_op jit(solution)/shard_map/ppermute | solution.py:37
  95.5 0.1 collective-permute-start.4
  95.6 1.1 constant_dynamic-update-slice_fusion.5
  96.7 0.0 collective-permute-done.2
  96.7 0.7 constant_dynamic-update-slice_fusion.4
  97.4 19.0 %collective-permute-done.4 = bf16[64,2304]{1,0:T(8,128)(2,1)S(1)} collective-permute-done((bf16[64,2304]{1,0:T(8,128)(2,1)S(1)}, bf16[64,2304]{1,0:T(8,128)(2,1)S(1)}, u32[]{:S(2)}, u32[]{:S(2)}) %collective-permute-start.4) | collective-permute-done | bytes 294944 | tf_op jit(solution)/shard_map/ppermute | solution.py:39
  116.4 0.7 constant_dynamic-update-slice_fusion.3
  117.1 0.9 maximum_dynamic-update-slice_fusion
  118.0 1.1 constant_dynamic-update-slice_fusion.2
  119.1 15.4 %collective-permute-start.5 = (bf16[512,2304]{1,0:T(8,128)(2,1)}, bf16[512,2304]{1,0:T(8,128)(2,1)S(1)}, u32[]{:S(2)}, u32[]{:S(2)}) collective-permute-start(bf16[512,2304]{1,0:T(8,128)(2,1)} %get-tuple-element.2), channel_id=1, source_target_pairs={{4,0},{5,1},{6,2},{7,3},{8,4},{9,5},{10,6},{11,7},{12,8},{13,9},{1... | collective-permute-start | bytes 7077896 | tf_op jit(solution)/shard_map/ppermute | solution.py:36
  134.5 0.0 collective-permute-start.7
  134.5 51.0 %collective-permute-done.5 = bf16[512,2304]{1,0:T(8,128)(2,1)S(1)} collective-permute-done((bf16[512,2304]{1,0:T(8,128)(2,1)}, bf16[512,2304]{1,0:T(8,128)(2,1)S(1)}, u32[]{:S(2)}, u32[]{:S(2)}) %collective-permute-start.5) | collective-permute-done | bytes 2359328 | tf_op jit(solution)/shard_map/ppermute | solution.py:36
  185.5 0.1 slice.86
  185.6 2.2 collective-permute-start.6
  187.7 0.0 collective-permute-done.7
  187.7 1.3 slice.89
  189.1 0.3 collective-permute-start.8
  189.4 0.9 slice_dynamic-update-slice_fusion.11
  190.2 0.9 slice_dynamic-update-slice_fusion.10
  191.1 0.9 slice_dynamic-update-slice_fusion.9
  192.0 0.9 slice_dynamic-update-slice_fusion.8
  192.9 19.0 %collective-permute-done.6 = bf16[256,2304]{1,0:T(8,128)(2,1)S(1)} collective-permute-done((bf16[256,2304]{1,0:T(8,128)(2,1)S(1)}, bf16[256,2304]{1,0:T(8,128)(2,1)S(1)}, u32[]{:S(2)}, u32[]{:S(2)}) %collective-permute-start.6) | collective-permute-done | bytes 1179680 | tf_op jit(solution)/shard_map/ppermute | solution.py:38
  211.8 0.8 slice_dynamic-update-slice_fusion.7
  212.7 0.9 slice_dynamic-update-slice_fusion.6
  213.5 2.2 collective-permute-done.8
  215.7 0.9 slice_dynamic-update-slice_fusion.5
  216.6 0.9 slice_dynamic-update-slice_fusion.4
  217.5 1.9 slice_dynamic-update-slice_fusion.3
  219.4 1.9 slice_dynamic-update-slice_fusion.2
  221.3 1.9 slice_dynamic-update-slice_fusion.1
  223.3 1.9 slice_dynamic-update-slice_fusion
  225.2 0.0 all-gather.2.cloned.1.call-done
  225.2 19.7 %multiply_convert_fusion = bf16[1792,1792]{1,0:T(8,128)(2,1)} fusion(bf16[2048,2304]{1,0:T(8,128)(2,1)} %all-gather.2.cloned.1.call-done, bf16[2048,2304]{1,0:T(8,128)(2,1)} %slice_dynamic-update-slice_fusion), kind=kOutput, calls=%fused_computation | convolution fusion | flops 13159759872 | bytes 21102592 | tf_op jit(solution)/shard_map/dot_general | solution.py:17
  245.0 4.3 %fusion.10 = bf16[512,512]{1,0:T(8,128)(2,1)} fusion(bf16[2048,2304]{1,0:T(8,128)(2,1)} %all-gather.2.cloned.1.call-done, bf16[2048,2304]{1,0:T(8,128)(2,1)} %slice_dynamic-update-slice_fusion), kind=kOutput, calls=%fused_computation.7 | convolution fusion | flops 1074266112 | bytes 4718592 | tf_op jit(solution)/shard_map/dot_general | solution.py:17
  (3 shorter events, 0.0 us)
Async XLA Ops:
  7.2 218.0 %all-gather.2.cloned.1.call-start = ((), (), s32[]{:S(2)}) async-start(), calls=%async_computation | async-start | bytes 10027008 | tf_op jit(solution)/shard_map/all_gather | solution.py:65
  11.0 13.7 %collective-permute-start = (bf16[128,2304]{1,0:T(8,128)(2,1)S(1)}, bf16[128,2304]{1,0:T(8,128)(2,1)S(1)}, u32[]{:S(2)}, u32[]{:S(2)}) collective-permute-start(bf16[128,2304]{1,0:T(8,128)(2,1)S(1)} %constant_dynamic-update-slice_fusion), channel_id=1, source_target_pairs={{0,0},{16,1},{32,2},{48,3},{64,4},{80,5},{96,6},{112,7},{128,8},{1... | collective-permute-start | bytes 1769480 | tf_op jit(solution)/shard_map/ppermute | solution.py:66
  24.7 52.0 %collective-permute-start.1 = (bf16[128,2304]{1,0:T(8,128)(2,1)S(1)}, bf16[128,2304]{1,0:T(8,128)(2,1)S(1)}, u32[]{:S(2)}, u32[]{:S(2)}) collective-permute-start(bf16[128,2304]{1,0:T(8,128)(2,1)S(1)} %collective-permute-done), channel_id=1, source_target_pairs={{1,0},{2,1},{3,2},{0,3},{5,4},{6,5},{7,6},{4,7},{9,8},{10,9},{11,1... | collective-permute-start | bytes 1769480 | tf_op jit(solution)/shard_map/ppermute | solution.py:36
  54.4 41.0 %collective-permute-start.3 = (bf16[128,2304]{1,0:T(8,128)(2,1)S(1)}, bf16[128,2304]{1,0:T(8,128)(2,1)S(1)}, u32[]{:S(2)}, u32[]{:S(2)}) collective-permute-start(bf16[128,2304]{1,0:T(8,128)(2,1)S(1)} %collective-permute-done), channel_id=1, source_target_pairs={{3,0},{0,1},{1,2},{2,3},{7,4},{4,5},{5,6},{6,7},{11,8},{8,9},{9,10... | collective-permute-start | bytes 1769480 | tf_op jit(solution)/shard_map/ppermute | solution.py:37
  76.7 20.0 %collective-permute-start.2 = (bf16[64,2304]{1,0:T(8,128)(2,1)S(1)}, bf16[64,2304]{1,0:T(8,128)(2,1)S(1)}, u32[]{:S(2)}, u32[]{:S(2)}) collective-permute-start(bf16[64,2304]{1,0:T(8,128)(2,1)S(1)} %slice.80), channel_id=1, source_target_pairs={{1,0},{2,1},{3,2},{0,3},{5,4},{6,5},{7,6},{4,7},{9,8},{10,9},{11,1... | collective-permute-start | bytes 884744 | tf_op jit(solution)/shard_map/ppermute | solution.py:38
  95.5 20.9 %collective-permute-start.4 = (bf16[64,2304]{1,0:T(8,128)(2,1)S(1)}, bf16[64,2304]{1,0:T(8,128)(2,1)S(1)}, u32[]{:S(2)}, u32[]{:S(2)}) collective-permute-start(bf16[64,2304]{1,0:T(8,128)(2,1)S(1)} %slice.81), channel_id=1, source_target_pairs={{3,0},{0,1},{1,2},{2,3},{7,4},{4,5},{5,6},{6,7},{11,8},{8,9},{9,10... | collective-permute-start | bytes 884744 | tf_op jit(solution)/shard_map/ppermute | solution.py:39
  119.1 66.4 %collective-permute-start.5 = (bf16[512,2304]{1,0:T(8,128)(2,1)}, bf16[512,2304]{1,0:T(8,128)(2,1)S(1)}, u32[]{:S(2)}, u32[]{:S(2)}) collective-permute-start(bf16[512,2304]{1,0:T(8,128)(2,1)} %get-tuple-element.2), channel_id=1, source_target_pairs={{4,0},{5,1},{6,2},{7,3},{8,4},{9,5},{10,6},{11,7},{12,8},{13,9},{1... | collective-permute-start | bytes 7077896 | tf_op jit(solution)/shard_map/ppermute | solution.py:36
  134.5 53.2 %collective-permute-start.7 = (bf16[512,2304]{1,0:T(8,128)(2,1)}, bf16[512,2304]{1,0:T(8,128)(2,1)}, u32[]{:S(2)}, u32[]{:S(2)}) collective-permute-start(bf16[512,2304]{1,0:T(8,128)(2,1)} %get-tuple-element.2), channel_id=1, source_target_pairs={{12,0},{13,1},{14,2},{15,3},{0,4},{1,5},{2,6},{3,7},{4,8},{5,9},{6... | collective-permute-start | bytes 7077896 | tf_op jit(solution)/shard_map/ppermute | solution.py:37
  185.6 26.3 %collective-permute-start.6 = (bf16[256,2304]{1,0:T(8,128)(2,1)S(1)}, bf16[256,2304]{1,0:T(8,128)(2,1)S(1)}, u32[]{:S(2)}, u32[]{:S(2)}) collective-permute-start(bf16[256,2304]{1,0:T(8,128)(2,1)S(1)} %slice.86), channel_id=1, source_target_pairs={{4,0},{5,1},{6,2},{7,3},{8,4},{9,5},{10,6},{11,7},{12,8},{13,9},{1... | collective-permute-start | bytes 3538952 | tf_op jit(solution)/shard_map/ppermute | solution.py:38
  189.1 26.6 %collective-permute-start.8 = (bf16[256,2304]{1,0:T(8,128)(2,1)S(1)}, bf16[256,2304]{1,0:T(8,128)(2,1)S(1)}, u32[]{:S(2)}, u32[]{:S(2)}) collective-permute-start(bf16[256,2304]{1,0:T(8,128)(2,1)S(1)} %slice.89), channel_id=1, source_target_pairs={{12,0},{13,1},{14,2},{15,3},{0,4},{1,5},{2,6},{3,7},{4,8},{5,9},{6... | collective-permute-start | bytes 3538952 | tf_op jit(solution)/shard_map/ppermute | solution.py:39
Sparse Core Ops, SparseCore 0:
  11.1 111.7 all-gather.1

commit v4 on v2

--- a/solution.py
+++ b/solution.py
@@ -70,10 +70,12 @@
     tok_weight = token_weights(domain_ids, domain_weights)
     weighted = (tok_weight[:, None] * both.astype(jnp.float32)).astype(jnp.bfloat16)
     swapped = lax.ppermute(both, ROWS + ("feat",), transpose_pairs(n_rows, n_cols, n_dp, n_ring))
-    rows = lax.all_gather(swapped, "feat", axis=0, tiled=True)
+    rows_g = lax.all_gather(swapped[:, :width_g], "feat", axis=0, tiled=True)
+    rows_g, piece_a = lax.optimization_barrier((rows_g, swapped[:, width_g:]))
+    rows_a = lax.all_gather(piece_a, "feat", axis=0, tiled=True)
     cols = gather_columns(weighted, n_dp, n_ring)
-    grad_sum = contract_tokens(rows[:, :width_g], cols[:, :width_g])
-    act_sum = contract_tokens(rows[:, width_g:], cols[:, width_g:])
+    grad_sum = contract_tokens(rows_g, cols[:, :width_g])
+    act_sum = contract_tokens(rows_a, cols[:, width_g:])
     grad_factor = (grad_sum * inv_count).astype(jnp.bfloat16)
     act_factor = (act_sum * inv_count).astype(jnp.bfloat16)
     return (grad_factor, act_factor)

time: 206 us -> 227 us (1.10)
  waiting for transfers between devices: 139 us -> 151 us
  local copies, waits for them, and re-layouts: 11.2 us -> 18.4 us
    all_gather x1 -> x2, waiting for transfers between devices: 55.4 us -> 74 us  [the longest x1 39.7 us: local(): rows_g = lax.all_gather(swapped[:, :width_g], 'feat', axis=0, tiled=True)]
    ppermute x1, waiting for transfers between devices: 7.54 us -> 0.01 us  [gather_columns(): other = lax.ppermute(mine, 'dp', [(1, 0), (0, 1)])]
    unnamed x8 -> x10, local copies, waits for them, and re-layouts: 6.64 us -> 9.59 us
    concatenate x1, local copies, waits for them, and re-layouts: 2.42 us -> 5.19 us  [gather_columns(): return jnp.concatenate([mine, other], axis=0)]
  transfers between devices with their start and end apart: 8 -> 9, of which waited for: 7 -> 7; matrix products, arithmetic and copies ran while one was open for 5% -> 14% of each run, Pallas kernels for 0% -> 0%
where the time goes in v4:
time: 227 us; the launch traced here: 225 us
  waiting for transfers between devices  151 us (67%)
  matrix products  23.2 us (10%)
  local copies, waits for them, and re-layouts  18.4 us (8%)
  starting transfers between devices  16.3 us (7%)
  between operations  14.1 us (6%)
    all_gather x1, waiting for transfers between devices, local(): rows_g = lax.all_gather(swapped[:, :width_g], 'feat', axis=0, tiled=True)  39.7 us
    all_gather x1, waiting for transfers between devices, local(): rows_a = lax.all_gather(piece_a, 'feat', axis=0, tiled=True)  34.3 us
    ppermute x1, waiting for transfers between devices, gather_columns(): ahead = lax.ppermute(own, 'ctx', ctx_shift(n_ring, 1, 0))  25.6 us
    ppermute x1, waiting for transfers between devices, local(): lax.ppermute(both, ROWS + ('feat',), transpose_pairs(n_rows, n_cols, n_dp...  24.5 us
    dot_general x2, matrix products, contract_tokens(): lax.dot_general(left, right, (((0,), (0,)), ((), ())), preferred_element_...  23.2 us
    ppermute x1, waiting for transfers between devices, gather_columns(): near = lax.ppermute(block, 'ctx', ctx_shift(n_ring, 0, 1))  15.2 us
    ppermute x1, starting transfers between devices, local(): lax.ppermute(both, ROWS + ('feat',), transpose_pairs(n_rows, n_cols, n_dp...  10.4 us
    ppermute x1, waiting for transfers between devices, gather_columns(): far_a = lax.ppermute(ahead[:half], 'ctx', ctx_shift(n_ring, 1, 0))  10.1 us
  transfers between devices with their start and end apart: 9, of which 7 were waited for; matrix products, arithmetic and copies ran while one was open for 14% of the time, Pallas kernels for 0%

profile of v4, /device:TPU:41, one launch (start us, length us, event | category | flops | bytes accessed | tf_op | source)
XLA Modules:
  0.0 224.6 jit_solution(4767984604677345865)
XLA Ops:
  7.2 0.0 all-gather.3.cloned.1.call-start
  7.2 1.0 constant_dynamic-update-slice_fusion.1
  8.3 0.9 constant_dynamic-update-slice_fusion
  9.2 10.4 %collective-permute-start = (bf16[128,2304]{1,0:T(8,128)(2,1)S(1)}, bf16[128,2304]{1,0:T(8,128)(2,1)S(1)}, u32[]{:S(2)}, u32[]{:S(2)}) collective-permute-start(bf16[128,2304]{1,0:T(8,128)(2,1)S(1)} %constant_dynamic-update-slice_fusion), channel_id=1, source_target_pairs={{0,0},{16,1},{32,2},{48,3},{64,4},{80,5},{96,6},{112,7},{128,8},{1... | collective-permute-start | bytes 1769480 | tf_op jit(solution)/shard_map/ppermute | solution.py:72
  19.6 24.5 %collective-permute-done = bf16[128,2304]{1,0:T(8,128)(2,1)S(1)} collective-permute-done((bf16[128,2304]{1,0:T(8,128)(2,1)S(1)}, bf16[128,2304]{1,0:T(8,128)(2,1)S(1)}, u32[]{:S(2)}, u32[]{:S(2)}) %collective-permute-start) | collective-permute-done | bytes 589856 | tf_op jit(solution)/shard_map/ppermute | solution.py:72
  44.1 0.8 slice.24
  44.9 0.0 all-gather.3.cloned.1.call-update
  44.9 0.0 all-gather.5.cloned.1.call-start
  45.0 0.8 select_reduce_fusion
  45.7 1.0 constant_dynamic-update-slice_fusion.7
  46.7 0.0 collective-permute-start.1
  46.7 15.2 %collective-permute-done.1 = bf16[128,2304]{1,0:T(8,128)(2,1)S(1)} collective-permute-done((bf16[128,2304]{1,0:T(8,128)(2,1)S(1)}, bf16[128,2304]{1,0:T(8,128)(2,1)S(1)}, u32[]{:S(2)}, u32[]{:S(2)}) %collective-permute-start.1) | collective-permute-done | bytes 589856 | tf_op jit(solution)/shard_map/ppermute | solution.py:49
  61.9 0.1 pad_maximum_fusion
  62.0 0.1 collective-permute-start.2
  62.1 1.5 collective-permute-start.4
  63.6 25.6 %collective-permute-done.2 = bf16[256,2304]{1,0:T(8,128)(2,1)S(1)} collective-permute-done((bf16[256,2304]{1,0:T(8,128)(2,1)S(1)}, bf16[256,2304]{1,0:T(8,128)(2,1)S(1)}, u32[]{:S(2)}, u32[]{:S(2)}) %collective-permute-start.2) | collective-permute-done | bytes 1179680 | tf_op jit(solution)/shard_map/ppermute | solution.py:51
  89.2 0.4 collective-permute-start.3
  89.6 0.9 constant_dynamic-update-slice_fusion.6
  90.5 0.0 collective-permute-done.4
  90.6 1.2 collective-permute-start.5
  91.8 1.2 constant_dynamic-update-slice_fusion.5
  93.0 10.1 %collective-permute-done.3 = bf16[128,2304]{1,0:T(8,128)(2,1)S(1)} collective-permute-done((bf16[128,2304]{1,0:T(8,128)(2,1)S(1)}, bf16[128,2304]{1,0:T(8,128)(2,1)S(1)}, u32[]{:S(2)}, u32[]{:S(2)}) %collective-permute-start.3) | collective-permute-done | bytes 589856 | tf_op jit(solution)/shard_map/ppermute | solution.py:53
  103.0 0.9 constant_dynamic-update-slice_fusion.4
  103.9 1.4 collective-permute-done.5
  105.3 0.9 constant_dynamic-update-slice_fusion.3
  106.2 1.2 constant_dynamic-update-slice_fusion.2
  107.4 0.0 copy-start
  107.4 3.7 %copy-done = bf16[2048,2304]{1,0:T(8,128)(2,1)} copy-done((bf16[2048,2304]{1,0:T(8,128)(2,1)}, bf16[2048,2304]{1,0:T(8,128)(2,1)S(1)}, u32[]{:S(2)}) %copy-start) | copy-done | bytes 9437208
  111.0 2.6 %collective-permute-start.6 = (bf16[1024,2304]{1,0:T(8,128)(2,1)}, bf16[1024,2304]{1,0:T(8,128)(2,1)}, u32[]{:S(2)}, u32[]{:S(2)}) collective-permute-start(bf16[1024,2304]{1,0:T(8,128)(2,1)} %get-tuple-element.8), channel_id=1, source_target_pairs={{128,0},{0,128},{129,1},{1,129},{130,2},{2,130},{131,3},{3,131},{1... | collective-permute-start | bytes 14155784 | tf_op jit(solution)/shard_map/ppermute | solution.py:56
  113.7 0.7 slice.25
  114.3 39.7 %all-gather.3.cloned.1.call-done = bf16[2048,1792]{1,0:T(8,128)(2,1)} async-done(((bf16[128,1792]{1,0:T(8,128)(2,1)}), bf16[2048,1792]{1,0:T(8,128)(2,1)}) %all-gather.3.cloned.1.call-update) | async-done | bytes 7340048 | tf_op jit(solution)/shard_map/all_gather | solution.py:73
  154.0 0.0 all-gather.5.cloned.1.call-update
  154.0 0.0 collective-permute-done.6
  154.0 0.0 copy-start.1
  154.0 5.2 %constant_dynamic-update-slice_fusion.8 = bf16[2048,2304]{1,0:T(8,128)(2,1)} fusion(bf16[2048,2304]{1,0:T(8,128)(2,1)} %copy-done, bf16[1024,2304]{1,0:T(8,128)(2,1)} %collective-permute-done.6), kind=kLoop, calls=%fused_computation.16 | loop fusion | bytes 9437184 | tf_op jit(solution)/shard_map/concatenate | solution.py:57
  159.2 1.0 copy-done.1
  160.2 18.9 %multiply_convert_fusion = bf16[1792,1792]{1,0:T(8,128)(2,1)} fusion(bf16[2048,1792]{1,0:T(8,128)(2,1)S(1)} %copy-done.1, bf16[2048,2304]{1,0:T(8,128)(2,1)} %constant_dynamic-update-slice_fusion.8), kind=kOutput, calls=%fused_computation | convolution fusion | flops 13159759872 | bytes 21102592 | tf_op jit(solution)/shard_map/dot_general | solution.py:17
  179.1 34.3 %all-gather.5.cloned.1.call-done = bf16[2048,512]{1,0:T(8,128)(2,1)} async-done(((bf16[128,512]{1,0:T(8,128)(2,1)}), bf16[2048,512]{1,0:T(8,128)(2,1)}) %all-gather.5.cloned.1.call-update) | async-done | bytes 2097168 | tf_op jit(solution)/shard_map/all_gather | solution.py:75
  213.4 4.3 %fusion.6 = bf16[512,512]{1,0:T(8,128)(2,1)} fusion(bf16[2048,512]{1,0:T(8,128)(2,1)} %all-gather.5.cloned.1.call-done, bf16[2048,2304]{1,0:T(8,128)(2,1)} %constant_dynamic-update-slice_fusion.8), kind=kOutput, calls=%fused_computation.5 | convolution fusion | flops 1074266112 | bytes 4718592 | tf_op jit(solution)/shard_map/dot_general | solution.py:17
  (4 shorter events, 0.1 us)
Async XLA Ops:
  7.2 146.8 %all-gather.3.cloned.1.call-start = ((), (), s32[]{:S(2)}) async-start(), calls=%async_computation | async-start | bytes 7798784 | tf_op jit(solution)/shard_map/all_gather | solution.py:73
  9.2 34.9 %collective-permute-start = (bf16[128,2304]{1,0:T(8,128)(2,1)S(1)}, bf16[128,2304]{1,0:T(8,128)(2,1)S(1)}, u32[]{:S(2)}, u32[]{:S(2)}) collective-permute-start(bf16[128,2304]{1,0:T(8,128)(2,1)S(1)} %constant_dynamic-update-slice_fusion), channel_id=1, source_target_pairs={{0,0},{16,1},{32,2},{48,3},{64,4},{80,5},{96,6},{112,7},{128,8},{1... | collective-permute-start | bytes 1769480 | tf_op jit(solution)/shard_map/ppermute | solution.py:72
  44.9 168.5 %all-gather.5.cloned.1.call-start = ((), (), s32[]{:S(2)}) async-start(), calls=%async_computation.1 | async-start | bytes 2228224 | tf_op jit(solution)/shard_map/all_gather | solution.py:75
  46.7 15.2 %collective-permute-start.1 = (bf16[128,2304]{1,0:T(8,128)(2,1)S(1)}, bf16[128,2304]{1,0:T(8,128)(2,1)S(1)}, u32[]{:S(2)}, u32[]{:S(2)}) collective-permute-start(bf16[128,2304]{1,0:T(8,128)(2,1)S(1)} %get-tuple-element.7), channel_id=1, source_target_pairs={{16,0},{0,16},{48,32},{32,48},{80,64},{64,80},{112,96},{96,112},{1... | collective-permute-start | bytes 1769480 | tf_op jit(solution)/shard_map/ppermute | solution.py:49
  62.0 27.2 %collective-permute-start.2 = (bf16[256,2304]{1,0:T(8,128)(2,1)S(1)}, bf16[256,2304]{1,0:T(8,128)(2,1)S(1)}, u32[]{:S(2)}, u32[]{:S(2)}) collective-permute-start(bf16[256,2304]{1,0:T(8,128)(2,1)S(1)} %pad_maximum_fusion), channel_id=1, source_target_pairs={{32,0},{48,16},{64,32},{80,48},{96,64},{112,80},{0,96},{16,112},{3... | collective-permute-start | bytes 3538952 | tf_op jit(solution)/shard_map/ppermute | solution.py:51
  62.1 28.5 %collective-permute-start.4 = (bf16[256,2304]{1,0:T(8,128)(2,1)S(1)}, bf16[256,2304]{1,0:T(8,128)(2,1)S(1)}, u32[]{:S(2)}, u32[]{:S(2)}) collective-permute-start(bf16[256,2304]{1,0:T(8,128)(2,1)S(1)} %pad_maximum_fusion), channel_id=1, source_target_pairs={{96,0},{112,16},{0,32},{16,48},{32,64},{48,80},{64,96},{80,112},{9... | collective-permute-start | bytes 3538952 | tf_op jit(solution)/shard_map/ppermute | solution.py:52
  89.2 13.8 %collective-permute-start.3 = (bf16[128,2304]{1,0:T(8,128)(2,1)S(1)}, bf16[128,2304]{1,0:T(8,128)(2,1)S(1)}, u32[]{:S(2)}, u32[]{:S(2)}) collective-permute-start(bf16[128,2304]{1,0:T(8,128)(2,1)S(1)} %slice.26), channel_id=1, source_target_pairs={{32,0},{48,16},{64,32},{80,48},{96,64},{112,80},{0,96},{16,112},{3... | collective-permute-start | bytes 1769480 | tf_op jit(solution)/shard_map/ppermute | solution.py:53
  90.6 14.7 %collective-permute-start.5 = (bf16[128,2304]{1,0:T(8,128)(2,1)S(1)}, bf16[128,2304]{1,0:T(8,128)(2,1)S(1)}, u32[]{:S(2)}, u32[]{:S(2)}) collective-permute-start(bf16[128,2304]{1,0:T(8,128)(2,1)S(1)} %slice.27), channel_id=1, source_target_pairs={{96,0},{112,16},{0,32},{16,48},{32,64},{48,80},{64,96},{80,112},{9... | collective-permute-start | bytes 1769480 | tf_op jit(solution)/shard_map/ppermute | solution.py:54
  107.4 3.7 %copy-start = (bf16[2048,2304]{1,0:T(8,128)(2,1)}, bf16[2048,2304]{1,0:T(8,128)(2,1)S(1)}, u32[]{:S(2)}) copy-start(bf16[2048,2304]{1,0:T(8,128)(2,1)S(1)} %get-tuple-element.9) | copy-start | bytes 28311556
  111.0 43.0 %collective-permute-start.6 = (bf16[1024,2304]{1,0:T(8,128)(2,1)}, bf16[1024,2304]{1,0:T(8,128)(2,1)}, u32[]{:S(2)}, u32[]{:S(2)}) collective-permute-start(bf16[1024,2304]{1,0:T(8,128)(2,1)} %get-tuple-element.8), channel_id=1, source_target_pairs={{128,0},{0,128},{129,1},{1,129},{130,2},{2,130},{131,3},{3,131},{1... | collective-permute-start | bytes 14155784 | tf_op jit(solution)/shard_map/ppermute | solution.py:56
  154.0 6.2 %copy-start.1 = (bf16[2048,1792]{1,0:T(8,128)(2,1)S(1)}, bf16[2048,1792]{1,0:T(8,128)(2,1)}, u32[]{:S(2)}) copy-start(bf16[2048,1792]{1,0:T(8,128)(2,1)} %all-gather.3.cloned.1.call-done) | copy-start | bytes 22020100
Sparse Core Ops, SparseCore 0:
  45.0 108.9 all-gather.2
  156.4 56.9 all-gather.4

commit v5 on v1

v5 whole, which is shorter than its diff:
```python
import jax
import jax.numpy as jnp
from jax import lax
from jax.sharding import Mesh
from jax.sharding import PartitionSpec as P

AXES = ("dp", "y", "zlo", "x", "zhi")
ROWS = ("dp", "y", "zlo")
COLS = ("x", "zhi")


def token_weights(tok_ids, domain_weights):
    labels = jnp.arange(domain_weights.shape[0], dtype=jnp.int32)
    match = tok_ids[:, None] == labels[None, :]
    return jnp.sum(jnp.where(match, domain_weights[None, :], 0), axis=1).astype(jnp.float32)


def contract_tokens(left, right):
    return lax.dot_general(
        left, right, (((0,), (0,)), ((), ())), preferred_element_type=jnp.float32
    )


def row_coords(r, n_ring, n_lo):
    per_dp = n_ring * n_lo
    return r // per_dp, (r % per_dp) // n_lo, r % n_lo


def shifted_block(r, ddp, dy, dz, n_dp, n_ring, n_lo):
    dp, y, z = row_coords(r, n_ring, n_lo)
    return ((dp + ddp) % n_dp) * n_ring * n_lo + ((y + dy) % n_ring) * n_lo + (z + dz) % n_lo


def fetch_pairs(k, n_dp, n_ring, n_lo, n_x, n_zh):
    n_rows, n_cols = n_dp * n_ring * n_lo, n_x * n_zh
    pairs = []
    for r in range(n_rows):
        for x in range(n_x):
            for zh in range(n_zh):
                ddp, dz = divmod((k + zh) % (n_dp * n_lo), n_lo)
                s = shifted_block(r, ddp, x, dz, n_dp, n_ring, n_lo)
                pairs.append((s * n_cols + r, r * n_cols + x * n_zh + zh))
    return pairs


def ring_pairs(n_ring, n_lo, dy, dz):
    pairs = []
    for y in range(n_ring):
        for z in range(n_lo):
            pairs.append((((y + dy) % n_ring) * n_lo + (z + dz) % n_lo, y * n_lo + z))
    return pairs


def gather_columns(block, n_ring, n_lo):
    half = block.shape[0]
    near = lax.ppermute(block, ("y", "zlo"), ring_pairs(n_ring, n_lo, 0, 1))
    own = jnp.concatenate([block, near], axis=0)
    ahead = lax.ppermute(own, ("y", "zlo"), ring_pairs(n_ring, n_lo, 1, 0))
    behind = lax.ppermute(own, ("y", "zlo"), ring_pairs(n_ring, n_lo, -1, 0))
    far_a = lax.ppermute(ahead[:half], ("y", "zlo"), ring_pairs(n_ring, n_lo, 1, 0))
    far_b = lax.ppermute(behind[half:], ("y", "zlo"), ring_pairs(n_ring, n_lo, -1, 0))
    mine = jnp.concatenate([own, ahead, far_a, far_b, behind], axis=0)
    other = lax.ppermute(mine, "dp", [(1, 0), (0, 1)])
    width = 2 * half
    parts = []
    for dy in range(n_ring):
        parts += [mine[dy * width:(dy + 1) * width], other[dy * width:(dy + 1) * width]]
    return jnp.concatenate(parts, axis=0)


def local(out_grads, acts, domain_ids, domain_weights):
    n_dp, n_ring, n_lo = (lax.axis_size(a) for a in ROWS)
    n_x, n_zh = (lax.axis_size(a) for a in COLS)
    assert n_dp == 2 and n_lo == 2 and n_ring == n_x and n_dp * n_lo == n_zh
    n_rows = n_dp * n_ring * n_lo
    inv_count = 1.0 / (out_grads.shape[0] * n_rows)
    width_g = out_grads.shape[1]
    both = jnp.concatenate([out_grads, acts], axis=1)
    tok_weight = token_weights(domain_ids, domain_weights)
    weighted = (tok_weight[:, None] * both.astype(jnp.float32)).astype(jnp.bfloat16)
    got = jnp.stack([lax.ppermute(both, AXES, fetch_pairs(k, n_dp, n_ring, n_lo, n_x, n_zh))
                     for k in range(n_zh)])
    zh = lax.axis_index("zhi")
    order = (jnp.arange(n_zh) - zh) % n_zh
    piece = jnp.take(got, order, axis=0).reshape(n_zh * both.shape[0], both.shape[1])
    rows = lax.all_gather(piece, "x", axis=0, tiled=True)
    cols = gather_columns(weighted, n_ring, n_lo)
    grad_sum = contract_tokens(rows[:, :width_g], cols[:, :width_g])
    act_sum = contract_tokens(rows[:, width_g:], cols[:, width_g:])
    grad_factor = (grad_sum * inv_count).astype(jnp.bfloat16)
    act_factor = (act_sum * inv_count).astype(jnp.bfloat16)
    return (grad_factor, act_factor)


def solution(mesh):
    n_dp, n_ctx, n_feat = mesh.devices.shape
    split = Mesh(mesh.devices.reshape(n_dp, n_ctx // 2, 2, 4, n_feat // 4), AXES)
    in_specs = (P(ROWS, COLS), P(ROWS, COLS), P(ROWS), P())
    out_specs = (P(ROWS, COLS), P(ROWS, COLS))
    return jax.shard_map(local, mesh=split, in_specs=in_specs, out_specs=out_specs, check_vma=False)
```

time: 253 us -> 227 us (0.90)
  waiting for transfers between devices: 198 us -> 132 us
  starting transfers between devices: 10.5 us -> 34.1 us
  local copies, waits for them, and re-layouts: 2.79 us -> 15.6 us
  other arithmetic: 1.74 us -> 5.45 us
    all_gather x2 -> x1, waiting for transfers between devices: 165 us -> 34.3 us  [local(): rows = lax.all_gather(piece, 'x', axis=0, tiled=True)]
    ppermute x1 -> x10, waiting for transfers between devices: 33.9 us -> 97.7 us  [the longest x4 45.6 us: local(): lax.ppermute(both, AXES, fetch_pairs(k, n_dp, n_ring, n_lo, n_x, n_zh))]
    ppermute x1 -> x10, starting transfers between devices: 10.4 us -> 34 us  [the longest x4 26.3 us: local(): lax.ppermute(both, AXES, fetch_pairs(k, n_dp, n_ring, n_lo, n_x, n_zh))]
    unnamed x3 -> x23, local copies, waits for them, and re-layouts: 1.88 us -> 11.2 us
    select_n x0 -> x2, other arithmetic: none -> 3.38 us  [local(): jnp.take(got, order, axis=0).reshape(n_zh * both.shape[0], both.shape[1])]
  transfers between devices with their start and end apart: 3 -> 11, of which waited for: 3 -> 10; matrix products, arithmetic and copies ran while one was open for 0% -> 5% of each run, Pallas kernels for 0% -> 0%
where the time goes in v5:
time: 227 us; the launch traced here: 225 us
  waiting for transfers between devices  132 us (58%)
  starting transfers between devices  34.1 us (15%)
  matrix products  24.1 us (11%)
  local copies, waits for them, and re-layouts  15.6 us (7%)
  between operations  14.2 us (6%)
  other arithmetic  5.45 us (2%)
    ppermute x4, waiting for transfers between devices, local(): lax.ppermute(both, AXES, fetch_pairs(k, n_dp, n_ring, n_lo, n_x, n_zh))  45.6 us
    all_gather x1, waiting for transfers between devices, local(): rows = lax.all_gather(piece, 'x', axis=0, tiled=True)  34.3 us
    ppermute x4, starting transfers between devices, local(): lax.ppermute(both, AXES, fetch_pairs(k, n_dp, n_ring, n_lo, n_x, n_zh))  26.3 us
    dot_general x2, matrix products, contract_tokens(): lax.dot_general(left, right, (((0,), (0,)), ((), ())), preferred_element_...  24.1 us
    ppermute x1, waiting for transfers between devices, gather_columns(): ahead = lax.ppermute(own, ('y', 'zlo'), ring_pairs(n_ring, n_lo, 1, 0))  21.1 us
    ppermute x1, waiting for transfers between devices, gather_columns(): lax.ppermute(ahead[:half], ('y', 'zlo'), ring_pairs(n_ring, n_lo, 1, 0))  12.2 us
    unnamed x23, local copies, waits for them, and re-layouts  11.2 us
    ppermute x1, waiting for transfers between devices, gather_columns(): near = lax.ppermute(block, ('y', 'zlo'), ring_pairs(n_ring, n_lo, 0, 1))  9.6 us
  transfers between devices with their start and end apart: 11, of which 10 were waited for; matrix products, arithmetic and copies ran while one was open for 5% of the time, Pallas kernels for 0%

profile of v5, /device:TPU:41, one launch (start us, length us, event | category | flops | bytes accessed | tf_op | source)
XLA Modules:
  0.0 225.3 jit_solution(1827649593475652463)
XLA Ops:
  7.2 0.0 all-gather.2.cloned.1.call-start
  7.2 1.0 constant_dynamic-update-slice_fusion.1
  8.3 0.9 constant_dynamic-update-slice_fusion
  9.2 8.8 %collective-permute-start = (bf16[128,2304]{1,0:T(8,128)(2,1)S(1)}, bf16[128,2304]{1,0:T(8,128)(2,1)S(1)}, u32[]{:S(2)}, u32[]{:S(2)}) collective-permute-start(bf16[128,2304]{1,0:T(8,128)(2,1)S(1)} %constant_dynamic-update-slice_fusion), channel_id=1, source_target_pairs={{0,0},{16,1},{128,2},{144,3},{32,4},{48,5},{160,6},{176,7},{64,8},... | collective-permute-start | bytes 1769480 | tf_op jit(solution)/shard_map/ppermute | solution.py:81
  18.0 3.1 %collective-permute-start.1 = (bf16[128,2304]{1,0:T(8,128)(2,1)S(1)}, bf16[128,2304]{1,0:T(8,128)(2,1)S(1)}, u32[]{:S(2)}, u32[]{:S(2)}) collective-permute-start(bf16[128,2304]{1,0:T(8,128)(2,1)S(1)} %constant_dynamic-update-slice_fusion), channel_id=1, source_target_pairs={{16,0},{128,1},{144,2},{0,3},{48,4},{160,5},{176,6},{32,7},{80,8},... | collective-permute-start | bytes 1769480 | tf_op jit(solution)/shard_map/ppermute | solution.py:81
  21.1 5.5 %collective-permute-start.2 = (bf16[128,2304]{1,0:T(8,128)(2,1)S(1)}, bf16[128,2304]{1,0:T(8,128)(2,1)S(1)}, u32[]{:S(2)}, u32[]{:S(2)}) collective-permute-start(bf16[128,2304]{1,0:T(8,128)(2,1)S(1)} %constant_dynamic-update-slice_fusion), channel_id=1, source_target_pairs={{128,0},{144,1},{0,2},{16,3},{160,4},{176,5},{32,6},{48,7},{192,8}... | collective-permute-start | bytes 1769480 | tf_op jit(solution)/shard_map/ppermute | solution.py:81
  26.7 8.9 %collective-permute-start.3 = (bf16[128,2304]{1,0:T(8,128)(2,1)S(1)}, bf16[128,2304]{1,0:T(8,128)(2,1)S(1)}, u32[]{:S(2)}, u32[]{:S(2)}) collective-permute-start(bf16[128,2304]{1,0:T(8,128)(2,1)S(1)} %constant_dynamic-update-slice_fusion), channel_id=1, source_target_pairs={{144,0},{0,1},{16,2},{128,3},{176,4},{32,5},{48,6},{160,7},{208,8}... | collective-permute-start | bytes 1769480 | tf_op jit(solution)/shard_map/ppermute | solution.py:81
  35.6 0.1 broadcast_bitcast_fusion
  35.7 21.4 %collective-permute-done = bf16[128,2304]{1,0:T(8,128)(2,1)S(1)} collective-permute-done((bf16[128,2304]{1,0:T(8,128)(2,1)S(1)}, bf16[128,2304]{1,0:T(8,128)(2,1)S(1)}, u32[]{:S(2)}, u32[]{:S(2)}) %collective-permute-start) | collective-permute-done | bytes 589856 | tf_op jit(solution)/shard_map/ppermute | solution.py:81
  57.1 1.0 collective-permute-done.1
  58.1 0.0 copy-start
  58.1 23.2 %collective-permute-done.2 = bf16[128,2304]{1,0:T(8,128)(2,1)S(1)} collective-permute-done((bf16[128,2304]{1,0:T(8,128)(2,1)S(1)}, bf16[128,2304]{1,0:T(8,128)(2,1)S(1)}, u32[]{:S(2)}, u32[]{:S(2)}) %collective-permute-start.2) | collective-permute-done | bytes 589856 | tf_op jit(solution)/shard_map/ppermute | solution.py:81
  81.3 0.0 copy-start.1
  81.3 0.0 collective-permute-done.3
  81.3 0.0 copy-start.2
  81.3 0.0 copy-done
  81.3 0.8 copy-done.1
  82.1 0.2 copy-done.2
  82.3 1.7 pad_maximum_fusion
  84.0 2.1 gather_fusion
  86.1 0.0 copy-start.3
  86.1 0.0 copy-start.4
  86.1 3.4 %bitcast_select_fusion = bf16[512,2304]{1,0:T(8,128)(2,1)} fusion(bf16[4,128,2304]{2,1,0:T(8,128)(2,1)} %gather_fusion, pred[512]{0:T(512)(128)(4,1)S(1)} %broadcast_bitcast_fusion), kind=kLoop, calls=%fused_computation.5 | loop fusion | flops 1179648 | bytes 4719104 | tf_op jit(solution)/shard_map/jit(_take)/select_n | solution.py:85
  89.5 0.0 all-gather.2.cloned.1.call-update
  89.5 0.0 copy-done.3
  89.5 0.0 copy-done.4
  89.5 0.1 select_reduce_fusion
  89.6 0.2 constant_dynamic-update-slice_fusion.7
  89.8 0.1 collective-permute-start.4
  89.9 9.6 %collective-permute-done.4 = bf16[128,2304]{1,0:T(8,128)(2,1)S(1)} collective-permute-done((bf16[128,2304]{1,0:T(8,128)(2,1)S(1)}, bf16[128,2304]{1,0:T(8,128)(2,1)S(1)}, u32[]{:S(2)}, u32[]{:S(2)}) %collective-permute-start.4) | collective-permute-done | bytes 589856 | tf_op jit(solution)/shard_map/ppermute | solution.py:56
  99.5 0.1 pad_maximum_fusion.1
  99.5 0.1 collective-permute-start.5
  99.6 2.1 collective-permute-start.7
  101.8 0.8 constant_dynamic-update-slice_fusion.13
  102.6 21.1 %collective-permute-done.5 = bf16[256,2304]{1,0:T(8,128)(2,1)S(1)} collective-permute-done((bf16[256,2304]{1,0:T(8,128)(2,1)S(1)}, bf16[256,2304]{1,0:T(8,128)(2,1)S(1)}, u32[]{:S(2)}, u32[]{:S(2)}) %collective-permute-start.5) | collective-permute-done | bytes 1179680 | tf_op jit(solution)/shard_map/ppermute | solution.py:58
  123.8 0.1 collective-permute-start.6
  123.9 0.9 constant_dynamic-update-slice_fusion.6
  124.8 1.2 collective-permute-done.7
  126.1 3.7 %collective-permute-start.8 = (bf16[128,2304]{1,0:T(8,128)(2,1)S(1)}, bf16[128,2304]{1,0:T(8,128)(2,1)S(1)}, u32[]{:S(2)}, u32[]{:S(2)}) collective-permute-start(bf16[128,2304]{1,0:T(8,128)(2,1)S(1)} %slice.46), channel_id=1, source_target_pairs={{96,0},{112,16},{0,32},{16,48},{32,64},{48,80},{64,96},{80,112},{9... | collective-permute-start | bytes 1769480 | tf_op jit(solution)/shard_map/ppermute | solution.py:61
  129.8 0.1 constant_dynamic-update-slice_fusion.5
  129.9 12.2 %collective-permute-done.6 = bf16[128,2304]{1,0:T(8,128)(2,1)S(1)} collective-permute-done((bf16[128,2304]{1,0:T(8,128)(2,1)S(1)}, bf16[128,2304]{1,0:T(8,128)(2,1)S(1)}, u32[]{:S(2)}, u32[]{:S(2)}) %collective-permute-start.6) | collective-permute-done | bytes 589856 | tf_op jit(solution)/shard_map/ppermute | solution.py:60
  142.1 0.4 collective-permute-done.8
  142.6 0.1 constant_dynamic-update-slice_fusion.2
  142.6 1.6 collective-permute-start.9
  144.2 7.5 %collective-permute-done.9 = bf16[1024,2304]{1,0:T(8,128)(2,1)S(1)} collective-permute-done((bf16[1024,2304]{1,0:T(8,128)(2,1)S(1)}, bf16[1024,2304]{1,0:T(8,128)(2,1)S(1)}, u32[]{:S(2)}, u32[]{:S(2)}) %collective-permute-start.9) | collective-permute-done | bytes 4718624 | tf_op jit(solution)/shard_map/ppermute | solution.py:63
  151.8 1.1 slice_dynamic-update-slice_fusion.3
  152.9 1.1 constant_dynamic-update-slice_fusion.11
  154.0 1.1 slice_dynamic-update-slice_fusion.2
  155.1 0.9 constant_dynamic-update-slice_fusion.10
  156.0 0.8 constant_dynamic-update-slice_fusion.9
  156.8 1.1 slice_dynamic-update-slice_fusion.1
  157.9 1.1 constant_dynamic-update-slice_fusion.8
  159.0 1.1 slice_dynamic-update-slice_fusion
  160.2 34.3 %all-gather.2.cloned.1.call-done = bf16[2048,2304]{1,0:T(8,128)(2,1)} async-done(((bf16[512,2304]{1,0:T(8,128)(2,1)}), bf16[2048,2304]{1,0:T(8,128)(2,1)}) %all-gather.2.cloned.1.call-update) | async-done | bytes 9437200 | tf_op jit(solution)/shard_map/all_gather | solution.py:86
  194.4 19.8 %multiply_convert_fusion = bf16[1792,1792]{1,0:T(8,128)(2,1)} fusion(bf16[2048,2304]{1,0:T(8,128)(2,1)} %slice_dynamic-update-slice_fusion, bf16[2048,2304]{1,0:T(8,128)(2,1)} %all-gather.2.cloned.1.call-done), kind=kOutput, calls=%fused_computation.1 | convolution fusion | flops 13159759872 | bytes 21102592 | tf_op jit(solution)/shard_map/dot_general | solution.py:19
  214.2 4.3 %fusion.10 = bf16[512,512]{1,0:T(8,128)(2,1)} fusion(bf16[2048,2304]{1,0:T(8,128)(2,1)} %slice_dynamic-update-slice_fusion, bf16[2048,2304]{1,0:T(8,128)(2,1)} %all-gather.2.cloned.1.call-done), kind=kOutput, calls=%fused_computation.10 | convolution fusion | flops 1074266112 | bytes 4718592 | tf_op jit(solution)/shard_map/dot_general | solution.py:19
  (8 shorter events, 0.2 us)
Async XLA Ops:
  7.2 187.3 %all-gather.2.cloned.1.call-start = ((), (), s32[]{:S(2)}) async-start(), calls=%async_computation | async-start | bytes 11796480 | tf_op jit(solution)/shard_map/all_gather | solution.py:86
  9.2 47.9 %collective-permute-start = (bf16[128,2304]{1,0:T(8,128)(2,1)S(1)}, bf16[128,2304]{1,0:T(8,128)(2,1)S(1)}, u32[]{:S(2)}, u32[]{:S(2)}) collective-permute-start(bf16[128,2304]{1,0:T(8,128)(2,1)S(1)} %constant_dynamic-update-slice_fusion), channel_id=1, source_target_pairs={{0,0},{16,1},{128,2},{144,3},{32,4},{48,5},{160,6},{176,7},{64,8},... | collective-permute-start | bytes 1769480 | tf_op jit(solution)/shard_map/ppermute | solution.py:81
  18.0 40.0 %collective-permute-start.1 = (bf16[128,2304]{1,0:T(8,128)(2,1)S(1)}, bf16[128,2304]{1,0:T(8,128)(2,1)S(1)}, u32[]{:S(2)}, u32[]{:S(2)}) collective-permute-start(bf16[128,2304]{1,0:T(8,128)(2,1)S(1)} %constant_dynamic-update-slice_fusion), channel_id=1, source_target_pairs={{16,0},{128,1},{144,2},{0,3},{48,4},{160,5},{176,6},{32,7},{80,8},... | collective-permute-start | bytes 1769480 | tf_op jit(solution)/shard_map/ppermute | solution.py:81
  21.1 60.1 %collective-permute-start.2 = (bf16[128,2304]{1,0:T(8,128)(2,1)S(1)}, bf16[128,2304]{1,0:T(8,128)(2,1)S(1)}, u32[]{:S(2)}, u32[]{:S(2)}) collective-permute-start(bf16[128,2304]{1,0:T(8,128)(2,1)S(1)} %constant_dynamic-update-slice_fusion), channel_id=1, source_target_pairs={{128,0},{144,1},{0,2},{16,3},{160,4},{176,5},{32,6},{48,7},{192,8}... | collective-permute-start | bytes 1769480 | tf_op jit(solution)/shard_map/ppermute | solution.py:81
  26.7 54.6 %collective-permute-start.3 = (bf16[128,2304]{1,0:T(8,128)(2,1)S(1)}, bf16[128,2304]{1,0:T(8,128)(2,1)S(1)}, u32[]{:S(2)}, u32[]{:S(2)}) collective-permute-start(bf16[128,2304]{1,0:T(8,128)(2,1)S(1)} %constant_dynamic-update-slice_fusion), channel_id=1, source_target_pairs={{144,0},{0,1},{16,2},{128,3},{176,4},{32,5},{48,6},{160,7},{208,8}... | collective-permute-start | bytes 1769480 | tf_op jit(solution)/shard_map/ppermute | solution.py:81
  58.1 23.2 %copy-start = (bf16[128,2304]{1,0:T(8,128)(2,1)}, bf16[128,2304]{1,0:T(8,128)(2,1)S(1)}, u32[]{:S(2)}) copy-start(bf16[128,2304]{1,0:T(8,128)(2,1)S(1)} %collective-permute-done.1) | copy-start | bytes 1769476
  81.3 0.8 copy-start.1
  81.3 1.0 copy-start.2
  86.1 3.4 %copy-start.3 = (s32[8]{0:T(128)S(1)}, s32[8]{0:T(128)}, u32[]{:S(2)}) copy-start(s32[8]{0:T(128)} %param.7) | copy-start | bytes 100
  86.1 3.4 %copy-start.4 = (s32[128]{0:T(128)S(1)}, s32[128]{0:T(128)}, u32[]{:S(2)}) copy-start(s32[128]{0:T(128)} %param.6) | copy-start | bytes 1540
  89.8 9.7 %collective-permute-start.4 = (bf16[128,2304]{1,0:T(8,128)(2,1)S(1)}, bf16[128,2304]{1,0:T(8,128)(2,1)S(1)}, u32[]{:S(2)}, u32[]{:S(2)}) collective-permute-start(bf16[128,2304]{1,0:T(8,128)(2,1)S(1)} %get-tuple-element.3), channel_id=1, source_target_pairs={{16,0},{0,16},{48,32},{32,48},{80,64},{64,80},{112,96},{96,112},{1... | collective-permute-start | bytes 1769480 | tf_op jit(solution)/shard_map/ppermute | solution.py:56
  99.5 24.2 %collective-permute-start.5 = (bf16[256,2304]{1,0:T(8,128)(2,1)S(1)}, bf16[256,2304]{1,0:T(8,128)(2,1)S(1)}, u32[]{:S(2)}, u32[]{:S(2)}) collective-permute-start(bf16[256,2304]{1,0:T(8,128)(2,1)S(1)} %pad_maximum_fusion.1), channel_id=1, source_target_pairs={{32,0},{48,16},{64,32},{80,48},{96,64},{112,80},{0,96},{16,112},{3... | collective-permute-start | bytes 3538952 | tf_op jit(solution)/shard_map/ppermute | solution.py:58
  99.6 26.4 %collective-permute-start.7 = (bf16[256,2304]{1,0:T(8,128)(2,1)S(1)}, bf16[256,2304]{1,0:T(8,128)(2,1)S(1)}, u32[]{:S(2)}, u32[]{:S(2)}) collective-permute-start(bf16[256,2304]{1,0:T(8,128)(2,1)S(1)} %pad_maximum_fusion.1), channel_id=1, source_target_pairs={{96,0},{112,16},{0,32},{16,48},{32,64},{48,80},{64,96},{80,112},{9... | collective-permute-start | bytes 3538952 | tf_op jit(solution)/shard_map/ppermute | solution.py:59
  123.8 18.2 %collective-permute-start.6 = (bf16[128,2304]{1,0:T(8,128)(2,1)S(1)}, bf16[128,2304]{1,0:T(8,128)(2,1)S(1)}, u32[]{:S(2)}, u32[]{:S(2)}) collective-permute-start(bf16[128,2304]{1,0:T(8,128)(2,1)S(1)} %slice.45), channel_id=1, source_target_pairs={{32,0},{48,16},{64,32},{80,48},{96,64},{112,80},{0,96},{16,112},{3... | collective-permute-start | bytes 1769480 | tf_op jit(solution)/shard_map/ppermute | solution.py:60
  126.1 16.4 %collective-permute-start.8 = (bf16[128,2304]{1,0:T(8,128)(2,1)S(1)}, bf16[128,2304]{1,0:T(8,128)(2,1)S(1)}, u32[]{:S(2)}, u32[]{:S(2)}) collective-permute-start(bf16[128,2304]{1,0:T(8,128)(2,1)S(1)} %slice.46), channel_id=1, source_target_pairs={{96,0},{112,16},{0,32},{16,48},{32,64},{48,80},{64,96},{80,112},{9... | collective-permute-start | bytes 1769480 | tf_op jit(solution)/shard_map/ppermute | solution.py:61
  142.6 9.1 %collective-permute-start.9 = (bf16[1024,2304]{1,0:T(8,128)(2,1)S(1)}, bf16[1024,2304]{1,0:T(8,128)(2,1)S(1)}, u32[]{:S(2)}, u32[]{:S(2)}) collective-permute-start(bf16[1024,2304]{1,0:T(8,128)(2,1)S(1)} %constant_dynamic-update-slice_fusion.2), channel_id=1, source_target_pairs={{128,0},{0,128},{129,1},{1,129},{130,2},{2,130},{131,3},{3,131},{1... | collective-permute-start | bytes 14155784 | tf_op jit(solution)/shard_map/ppermute | solution.py:63
Sparse Core Ops, SparseCore 0:
  89.6 104.8 all-gather.1

commit v6 on v4

--- a/solution.py
+++ b/solution.py
@@ -57,6 +57,11 @@
     return jnp.concatenate([mine, other], axis=0)
 
 
+def fetch_pairs(k, n_rows, n_cols, n_dp, n_ring):
+    return [(token_block(r, (k + c) % n_cols, n_dp, n_ring) * n_cols + r, r * n_cols + c)
+            for r in range(n_rows) for c in range(n_cols)]
+
+
 def local(out_grads, acts, domain_ids, domain_weights):
     n_dp = lax.axis_size("dp")
     n_ctx = lax.axis_size("ctx")
@@ -69,10 +74,12 @@
     both = jnp.concatenate([out_grads, acts], axis=1)
     tok_weight = token_weights(domain_ids, domain_weights)
     weighted = (tok_weight[:, None] * both.astype(jnp.float32)).astype(jnp.bfloat16)
-    swapped = lax.ppermute(both, ROWS + ("feat",), transpose_pairs(n_rows, n_cols, n_dp, n_ring))
-    rows_g = lax.all_gather(swapped[:, :width_g], "feat", axis=0, tiled=True)
-    rows_g, piece_a = lax.optimization_barrier((rows_g, swapped[:, width_g:]))
-    rows_a = lax.all_gather(piece_a, "feat", axis=0, tiled=True)
+    swapped = lax.ppermute(out_grads, ROWS + ("feat",), transpose_pairs(n_rows, n_cols, n_dp, n_ring))
+    rows_g = lax.all_gather(swapped, "feat", axis=0, tiled=True)
+    got = jnp.stack([lax.ppermute(acts, ROWS + ("feat",), fetch_pairs(k, n_rows, n_cols, n_dp, n_ring))
+                     for k in range(n_cols)])
+    order = (jnp.arange(n_cols) - lax.axis_index("feat")) % n_cols
+    rows_a = jnp.take(got, order, axis=0).reshape(n_cols * acts.shape[0], acts.shape[1])
     cols = gather_columns(weighted, n_dp, n_ring)
     grad_sum = contract_tokens(rows_g, cols[:, :width_g])
     act_sum = contract_tokens(rows_a, cols[:, width_g:])

time: 227 us -> 261 us (1.15)
  starting transfers between devices: 16.3 us -> 113 us
  waiting for transfers between devices: 151 us -> 67.9 us
  local copies, waits for them, and re-layouts: 18.4 us -> 36.1 us
  other arithmetic: 1.82 us -> 4.57 us
    ppermute x1 -> x17, starting transfers between devices: 10.4 us -> 106 us  [the longest x16 95.6 us: local(): lax.ppermute(acts, ROWS + ('feat',), fetch_pairs(k, n_rows, n_cols, n_dp,...]
    all_gather x2 -> x1, waiting for transfers between devices: 74 us -> 0.01 us  [local(): rows_g = lax.all_gather(swapped, 'feat', axis=0, tiled=True)]
    unnamed x10 -> x25, local copies, waits for them, and re-layouts: 9.59 us -> 27.1 us
    ppermute x1, waiting for transfers between devices: 25.6 us -> 8.77 us  [gather_columns(): ahead = lax.ppermute(own, 'ctx', ctx_shift(n_ring, 1, 0))]
    ppermute x1 -> x17, waiting for transfers between devices: 24.5 us -> 31.8 us  [the longest x1 19.1 us: local(): lax.ppermute(out_grads, ROWS + ('feat',), transpose_pairs(n_rows, n_cols,...]
  transfers between devices with their start and end apart: 9 -> 24, of which waited for: 7 -> 7; matrix products, arithmetic and copies ran while one was open for 14% -> 13% of each run, Pallas kernels for 0% -> 0%
where the time goes in v6:
time: 261 us; the launch traced here: 259 us
  starting transfers between devices  113 us (43%)
  waiting for transfers between devices  67.9 us (26%)
  local copies, waits for them, and re-layouts  36.1 us (14%)
  matrix products  23.5 us (9%)
  between operations  14.3 us (5%)
  other arithmetic  4.57 us (2%)
    ppermute x16, starting transfers between devices, local(): lax.ppermute(acts, ROWS + ('feat',), fetch_pairs(k, n_rows, n_cols, n_dp,...  95.6 us
    unnamed x25, local copies, waits for them, and re-layouts  27.1 us
    dot_general x2, matrix products, contract_tokens(): lax.dot_general(left, right, (((0,), (0,)), ((), ())), preferred_element_...  23.5 us
    ppermute x1, waiting for transfers between devices, local(): lax.ppermute(out_grads, ROWS + ('feat',), transpose_pairs(n_rows, n_cols,...  19.1 us
    ppermute x1, waiting for transfers between devices, gather_columns(): near = lax.ppermute(block, 'ctx', ctx_shift(n_ring, 0, 1))  16.2 us
    ppermute x16, waiting for transfers between devices, local(): lax.ppermute(acts, ROWS + ('feat',), fetch_pairs(k, n_rows, n_cols, n_dp,...  12.6 us
    ppermute x1, waiting for transfers between devices, gather_columns(): far_a = lax.ppermute(ahead[:half], 'ctx', ctx_shift(n_ring, 1, 0))  11.2 us
    ppermute x1, starting transfers between devices, local(): lax.ppermute(out_grads, ROWS + ('feat',), transpose_pairs(n_rows, n_cols,...  10.4 us
  transfers between devices with their start and end apart: 24, of which 7 were waited for; matrix products, arithmetic and copies ran while one was open for 13% of the time, Pallas kernels for 0%

profile of v6, /device:TPU:41, one launch (start us, length us, event | category | flops | bytes accessed | tf_op | source)
XLA Modules:
  0.0 259.2 jit_solution(4302463827620492322)
XLA Ops:
  7.2 0.0 all-gather.2.cloned.1.call-start
  7.2 10.4 %collective-permute-start.6 = (bf16[128,1792]{1,0:T(8,128)(2,1)}, bf16[128,1792]{1,0:T(8,128)(2,1)S(1)}, u32[]{:S(2)}, u32[]{:S(2)}) collective-permute-start(bf16[128,1792]{1,0:T(8,128)(2,1)} %param.4), channel_id=1, source_target_pairs={{0,0},{16,1},{32,2},{48,3},{64,4},{80,5},{96,6},{112,7},{128,8},{1... | collective-permute-start | bytes 1376264 | tf_op jit(solution)/shard_map/ppermute | solution.py:77
  17.6 19.1 %collective-permute-done.6 = bf16[128,1792]{1,0:T(8,128)(2,1)S(1)} collective-permute-done((bf16[128,1792]{1,0:T(8,128)(2,1)}, bf16[128,1792]{1,0:T(8,128)(2,1)S(1)}, u32[]{:S(2)}, u32[]{:S(2)}) %collective-permute-start.6) | collective-permute-done | bytes 458784 | tf_op jit(solution)/shard_map/ppermute | solution.py:77
  36.7 0.8 copy-done
  37.5 0.0 all-gather.2.cloned.1.call-update
  37.5 0.8 select_reduce_fusion
  38.3 2.1 constant_dynamic-update-slice_fusion.5
  40.3 0.0 collective-permute-start
  40.3 16.2 %collective-permute-done = bf16[128,2304]{1,0:T(8,128)(2,1)S(1)} collective-permute-done((bf16[128,2304]{1,0:T(8,128)(2,1)S(1)}, bf16[128,2304]{1,0:T(8,128)(2,1)S(1)}, u32[]{:S(2)}, u32[]{:S(2)}) %collective-permute-start) | collective-permute-done | bytes 589856 | tf_op jit(solution)/shard_map/ppermute | solution.py:49
  56.6 1.1 pad_maximum_fusion
  57.7 1.5 collective-permute-start.3
  59.1 15.1 %collective-permute-start.7 = (bf16[128,512]{1,0:T(8,128)(2,1)}, bf16[128,512]{1,0:T(8,128)(2,1)}, u32[]{:S(2)}, u32[]{:S(2)}) collective-permute-start(bf16[128,512]{1,0:T(8,128)(2,1)} %param.5), channel_id=1, source_target_pairs={{0,0},{16,1},{32,2},{48,3},{64,4},{80,5},{96,6},{112,7},{128,8},{1... | collective-permute-start | bytes 393224 | tf_op jit(solution)/shard_map/ppermute | solution.py:79
  74.2 1.9 collective-permute-start.8
  76.1 1.9 collective-permute-start.9
  78.1 8.8 %collective-permute-done.1 = bf16[256,2304]{1,0:T(8,128)(2,1)S(1)} collective-permute-done((bf16[256,2304]{1,0:T(8,128)(2,1)}, bf16[256,2304]{1,0:T(8,128)(2,1)S(1)}, u32[]{:S(2)}, u32[]{:S(2)}) %collective-permute-start.1) | collective-permute-done | bytes 1179680 | tf_op jit(solution)/shard_map/ppermute | solution.py:51
  86.9 1.7 collective-permute-start.2
  88.6 0.9 constant_dynamic-update-slice_fusion.4
  89.5 0.1 collective-permute-start.4
  89.6 1.2 constant_dynamic-update-slice_fusion.3
  90.8 11.2 %collective-permute-done.2 = bf16[128,2304]{1,0:T(8,128)(2,1)S(1)} collective-permute-done((bf16[128,2304]{1,0:T(8,128)(2,1)S(1)}, bf16[128,2304]{1,0:T(8,128)(2,1)S(1)}, u32[]{:S(2)}, u32[]{:S(2)}) %collective-permute-start.2) | collective-permute-done | bytes 589856 | tf_op jit(solution)/shard_map/ppermute | solution.py:53
  102.0 1.9 collective-permute-start.10
  103.9 0.9 constant_dynamic-update-slice_fusion.2
  104.8 0.9 constant_dynamic-update-slice_fusion.1
  105.7 1.2 constant_dynamic-update-slice_fusion
  106.8 3.6 %collective-permute-start.5 = (bf16[1024,2304]{1,0:T(8,128)(2,1)}, bf16[1024,2304]{1,0:T(8,128)(2,1)}, u32[]{:S(2)}, u32[]{:S(2)}) collective-permute-start(bf16[1024,2304]{1,0:T(8,128)(2,1)} %get-tuple-element.8), channel_id=1, source_target_pairs={{128,0},{0,128},{129,1},{1,129},{130,2},{2,130},{131,3},{3,131},{1... | collective-permute-start | bytes 14155784 | tf_op jit(solution)/shard_map/ppermute | solution.py:56
  110.4 0.1 broadcast_bitcast_fusion
  110.5 0.0 collective-permute-done.7
  110.6 12.9 %collective-permute-start.11 = (bf16[128,512]{1,0:T(8,128)(2,1)}, bf16[128,512]{1,0:T(8,128)(2,1)S(1)}, u32[]{:S(2)}, u32[]{:S(2)}) collective-permute-start(bf16[128,512]{1,0:T(8,128)(2,1)} %param.5), channel_id=1, source_target_pairs={{64,0},{80,1},{96,2},{112,3},{128,4},{144,5},{160,6},{176,7},{192,... | collective-permute-start | bytes 393224 | tf_op jit(solution)/shard_map/ppermute | solution.py:79
  123.5 1.6 bitcast_dynamic-update-slice_fusion.15
  125.1 3.7 %collective-permute-start.12 = (bf16[128,512]{1,0:T(8,128)(2,1)}, bf16[128,512]{1,0:T(8,128)(2,1)S(1)}, u32[]{:S(2)}, u32[]{:S(2)}) collective-permute-start(bf16[128,512]{1,0:T(8,128)(2,1)} %param.5), channel_id=1, source_target_pairs={{80,0},{96,1},{112,2},{128,3},{144,4},{160,5},{176,6},{192,7},{208... | collective-permute-start | bytes 393224 | tf_op jit(solution)/shard_map/ppermute | solution.py:79
  128.8 1.6 bitcast_dynamic-update-slice_fusion.14
  130.3 1.9 collective-permute-start.13
  132.3 1.6 bitcast_dynamic-update-slice_fusion.13
  133.8 13.6 %collective-permute-start.14 = (bf16[128,512]{1,0:T(8,128)(2,1)}, bf16[128,512]{1,0:T(8,128)(2,1)S(1)}, u32[]{:S(2)}, u32[]{:S(2)}) collective-permute-start(bf16[128,512]{1,0:T(8,128)(2,1)} %param.5), channel_id=1, source_target_pairs={{112,0},{128,1},{144,2},{160,3},{176,4},{192,5},{208,6},{224,7},{2... | collective-permute-start | bytes 393224 | tf_op jit(solution)/shard_map/ppermute | solution.py:79
  147.5 0.7 bitcast_dynamic-update-slice_fusion.12
  148.1 3.5 %collective-permute-start.15 = (bf16[128,512]{1,0:T(8,128)(2,1)}, bf16[128,512]{1,0:T(8,128)(2,1)S(1)}, u32[]{:S(2)}, u32[]{:S(2)}) collective-permute-start(bf16[128,512]{1,0:T(8,128)(2,1)} %param.5), channel_id=1, source_target_pairs={{128,0},{144,1},{160,2},{176,3},{192,4},{208,5},{224,6},{240,7},{0... | collective-permute-start | bytes 393224 | tf_op jit(solution)/shard_map/ppermute | solution.py:79
  151.7 0.7 bitcast_dynamic-update-slice_fusion.11
  152.3 0.9 collective-permute-done.12
  153.2 3.6 %collective-permute-start.16 = (bf16[128,512]{1,0:T(8,128)(2,1)}, bf16[128,512]{1,0:T(8,128)(2,1)S(1)}, u32[]{:S(2)}, u32[]{:S(2)}) collective-permute-start(bf16[128,512]{1,0:T(8,128)(2,1)} %param.5), channel_id=1, source_target_pairs={{144,0},{160,1},{176,2},{192,3},{208,4},{224,5},{240,6},{0,7},{16,... | collective-permute-start | bytes 393224 | tf_op jit(solution)/shard_map/ppermute | solution.py:79
  156.8 0.7 bitcast_dynamic-update-slice_fusion.10
  157.5 0.5 collective-permute-done.13
  158.0 2.2 collective-permute-start.17
  160.2 0.7 bitcast_dynamic-update-slice_fusion.9
  160.9 13.4 %collective-permute-start.18 = (bf16[128,512]{1,0:T(8,128)(2,1)}, bf16[128,512]{1,0:T(8,128)(2,1)S(1)}, u32[]{:S(2)}, u32[]{:S(2)}) collective-permute-start(bf16[128,512]{1,0:T(8,128)(2,1)} %param.5), channel_id=1, source_target_pairs={{176,0},{192,1},{208,2},{224,3},{240,4},{0,5},{16,6},{32,7},{48,8}... | collective-permute-start | bytes 393224 | tf_op jit(solution)/shard_map/ppermute | solution.py:79
  174.3 0.7 bitcast_dynamic-update-slice_fusion.8
  174.9 6.3 %collective-permute-start.19 = (bf16[128,512]{1,0:T(8,128)(2,1)}, bf16[128,512]{1,0:T(8,128)(2,1)S(1)}, u32[]{:S(2)}, u32[]{:S(2)}) collective-permute-start(bf16[128,512]{1,0:T(8,128)(2,1)} %param.5), channel_id=1, source_target_pairs={{192,0},{208,1},{224,2},{240,3},{0,4},{16,5},{32,6},{48,7},{64,8},... | collective-permute-start | bytes 393224 | tf_op jit(solution)/shard_map/ppermute | solution.py:79
  181.3 0.7 bitcast_dynamic-update-slice_fusion.7
  181.9 9.3 %collective-permute-start.20 = (bf16[128,512]{1,0:T(8,128)(2,1)}, bf16[128,512]{1,0:T(8,128)(2,1)S(1)}, u32[]{:S(2)}, u32[]{:S(2)}) collective-permute-start(bf16[128,512]{1,0:T(8,128)(2,1)} %param.5), channel_id=1, source_target_pairs={{208,0},{224,1},{240,2},{0,3},{16,4},{32,5},{48,6},{64,7},{80,8},{... | collective-permute-start | bytes 393224 | tf_op jit(solution)/shard_map/ppermute | solution.py:79
  191.2 0.7 bitcast_dynamic-update-slice_fusion.6
  191.9 1.9 collective-permute-start.21
  193.8 0.7 bitcast_dynamic-update-slice_fusion.5
  194.5 2.4 collective-permute-start.22
  196.9 0.7 bitcast_dynamic-update-slice_fusion.4
  197.5 0.7 bitcast_dynamic-update-slice_fusion.3
  198.2 0.7 bitcast_dynamic-update-slice_fusion.2
  198.9 11.2 %collective-permute-done.21 = bf16[128,512]{1,0:T(8,128)(2,1)S(1)} collective-permute-done((bf16[128,512]{1,0:T(8,128)(2,1)}, bf16[128,512]{1,0:T(8,128)(2,1)S(1)}, u32[]{:S(2)}, u32[]{:S(2)}) %collective-permute-start.21) | collective-permute-done | bytes 131104 | tf_op jit(solution)/shard_map/ppermute | solution.py:79
  210.1 0.7 bitcast_dynamic-update-slice_fusion.1
  210.7 0.7 bitcast_dynamic-update-slice_fusion
  211.4 2.3 gather_fusion
  213.7 0.6 bitcast_select_fusion
  214.3 4.8 %constant_dynamic-update-slice_fusion.6 = bf16[2048,2304]{1,0:T(8,128)(2,1)} fusion(bf16[2048,2304]{1,0:T(8,128)(2,1)} %copy-done.1, bf16[1024,2304]{1,0:T(8,128)(2,1)} %collective-permute-done.5), kind=kLoop, calls=%fused_computation.33 | loop fusion | bytes 9437184 | tf_op jit(solution)/shard_map/concatenate | solution.py:57
  219.1 3.7 %fusion.9 = bf16[512,512]{1,0:T(8,128)(2,1)} fusion(bf16[2048,512]{1,0:T(8,128)(2,1)S(1)} %bitcast_select_fusion, bf16[2048,2304]{1,0:T(8,128)(2,1)} %constant_dynamic-update-slice_fusion.6), kind=kOutput, calls=%fused_computation.8 | convolution fusion | flops 1074266112 | bytes 4718592 | tf_op jit(solution)/shard_map/dot_general | solution.py:17
  222.8 19.8 %fusion.1 = bf16[1792,1792]{0,1:T(8,128)(2,1)} fusion(bf16[2048,1792]{1,0:T(8,128)(2,1)} %all-gather.2.cloned.1.call-done, bf16[2048,2304]{1,0:T(8,128)(2,1)} %constant_dynamic-update-slice_fusion.6), kind=kOutput, calls=%fused_computation.3 | convolution fusion | flops 13159759872 | bytes 21102592 | tf_op jit(solution)/shard_map/dot_general | solution.py:17
  242.6 9.8 %copy.7 = bf16[1792,1792]{1,0:T(8,128)(2,1)} copy(bf16[1792,1792]{0,1:T(8,128)(2,1)} %fusion.1) | data formatting | bytes 12845056
  (27 shorter events, 0.2 us)
Async XLA Ops:
  7.2 215.6 %all-gather.2.cloned.1.call-start = ((), (), s32[]{:S(2)}) async-start(), calls=%async_computation | async-start | bytes 7798784 | tf_op jit(solution)/shard_map/all_gather | solution.py:78
  7.2 29.5 %collective-permute-start.6 = (bf16[128,1792]{1,0:T(8,128)(2,1)}, bf16[128,1792]{1,0:T(8,128)(2,1)S(1)}, u32[]{:S(2)}, u32[]{:S(2)}) collective-permute-start(bf16[128,1792]{1,0:T(8,128)(2,1)} %param.4), channel_id=1, source_target_pairs={{0,0},{16,1},{32,2},{48,3},{64,4},{80,5},{96,6},{112,7},{128,8},{1... | collective-permute-start | bytes 1376264 | tf_op jit(solution)/shard_map/ppermute | solution.py:77
  36.7 0.8 copy-start
  40.3 16.2 %collective-permute-start = (bf16[128,2304]{1,0:T(8,128)(2,1)S(1)}, bf16[128,2304]{1,0:T(8,128)(2,1)S(1)}, u32[]{:S(2)}, u32[]{:S(2)}) collective-permute-start(bf16[128,2304]{1,0:T(8,128)(2,1)S(1)} %get-tuple-element.7), channel_id=1, source_target_pairs={{16,0},{0,16},{48,32},{32,48},{80,64},{64,80},{112,96},{96,112},{1... | collective-permute-start | bytes 1769480 | tf_op jit(solution)/shard_map/ppermute | solution.py:49
  57.7 29.2 %collective-permute-start.1 = (bf16[256,2304]{1,0:T(8,128)(2,1)}, bf16[256,2304]{1,0:T(8,128)(2,1)S(1)}, u32[]{:S(2)}, u32[]{:S(2)}) collective-permute-start(bf16[256,2304]{1,0:T(8,128)(2,1)} %pad_maximum_fusion), channel_id=1, source_target_pairs={{32,0},{48,16},{64,32},{80,48},{96,64},{112,80},{0,96},{16,112},{3... | collective-permute-start | bytes 3538952 | tf_op jit(solution)/shard_map/ppermute | solution.py:51
  57.7 31.8 %collective-permute-start.3 = (bf16[256,2304]{1,0:T(8,128)(2,1)}, bf16[256,2304]{1,0:T(8,128)(2,1)S(1)}, u32[]{:S(2)}, u32[]{:S(2)}) collective-permute-start(bf16[256,2304]{1,0:T(8,128)(2,1)} %pad_maximum_fusion), channel_id=1, source_target_pairs={{96,0},{112,16},{0,32},{16,48},{32,64},{48,80},{64,96},{80,112},{9... | collective-permute-start | bytes 3538952 | tf_op jit(solution)/shard_map/ppermute | solution.py:52
  59.1 51.4 %collective-permute-start.7 = (bf16[128,512]{1,0:T(8,128)(2,1)}, bf16[128,512]{1,0:T(8,128)(2,1)}, u32[]{:S(2)}, u32[]{:S(2)}) collective-permute-start(bf16[128,512]{1,0:T(8,128)(2,1)} %param.5), channel_id=1, source_target_pairs={{0,0},{16,1},{32,2},{48,3},{64,4},{80,5},{96,6},{112,7},{128,8},{1... | collective-permute-start | bytes 393224 | tf_op jit(solution)/shard_map/ppermute | solution.py:79
  74.2 50.9 %collective-permute-start.8 = (bf16[128,512]{1,0:T(8,128)(2,1)}, bf16[128,512]{1,0:T(8,128)(2,1)}, u32[]{:S(2)}, u32[]{:S(2)}) collective-permute-start(bf16[128,512]{1,0:T(8,128)(2,1)} %param.5), channel_id=1, source_target_pairs={{16,0},{32,1},{48,2},{64,3},{80,4},{96,5},{112,6},{128,7},{144,8},... | collective-permute-start | bytes 393224 | tf_op jit(solution)/shard_map/ppermute | solution.py:79
  76.1 54.2 %collective-permute-start.9 = (bf16[128,512]{1,0:T(8,128)(2,1)}, bf16[128,512]{1,0:T(8,128)(2,1)}, u32[]{:S(2)}, u32[]{:S(2)}) collective-permute-start(bf16[128,512]{1,0:T(8,128)(2,1)} %param.5), channel_id=1, source_target_pairs={{32,0},{48,1},{64,2},{80,3},{96,4},{112,5},{128,6},{144,7},{160,8}... | collective-permute-start | bytes 393224 | tf_op jit(solution)/shard_map/ppermute | solution.py:79
  86.9 15.0 %collective-permute-start.2 = (bf16[128,2304]{1,0:T(8,128)(2,1)S(1)}, bf16[128,2304]{1,0:T(8,128)(2,1)S(1)}, u32[]{:S(2)}, u32[]{:S(2)}) collective-permute-start(bf16[128,2304]{1,0:T(8,128)(2,1)S(1)} %slice.18), channel_id=1, source_target_pairs={{32,0},{48,16},{64,32},{80,48},{96,64},{112,80},{0,96},{16,112},{3... | collective-permute-start | bytes 1769480 | tf_op jit(solution)/shard_map/ppermute | solution.py:53
  89.5 15.3 %collective-permute-start.4 = (bf16[128,2304]{1,0:T(8,128)(2,1)S(1)}, bf16[128,2304]{1,0:T(8,128)(2,1)S(1)}, u32[]{:S(2)}, u32[]{:S(2)}) collective-permute-start(bf16[128,2304]{1,0:T(8,128)(2,1)S(1)} %slice.19), channel_id=1, source_target_pairs={{96,0},{112,16},{0,32},{16,48},{32,64},{48,80},{64,96},{80,112},{9... | collective-permute-start | bytes 1769480 | tf_op jit(solution)/shard_map/ppermute | solution.py:54
  102.0 31.9 %collective-permute-start.10 = (bf16[128,512]{1,0:T(8,128)(2,1)}, bf16[128,512]{1,0:T(8,128)(2,1)S(1)}, u32[]{:S(2)}, u32[]{:S(2)}) collective-permute-start(bf16[128,512]{1,0:T(8,128)(2,1)} %param.5), channel_id=1, source_target_pairs={{48,0},{64,1},{80,2},{96,3},{112,4},{128,5},{144,6},{160,7},{176,8... | collective-permute-start | bytes 393224 | tf_op jit(solution)/shard_map/ppermute | solution.py:79
  106.8 103.9 %copy-start.1 = (bf16[2048,2304]{1,0:T(8,128)(2,1)}, bf16[2048,2304]{1,0:T(8,128)(2,1)S(1)}, u32[]{:S(2)}) copy-start(bf16[2048,2304]{1,0:T(8,128)(2,1)S(1)} %get-tuple-element.9) | copy-start | bytes 28311556
  106.8 107.4 %collective-permute-start.5 = (bf16[1024,2304]{1,0:T(8,128)(2,1)}, bf16[1024,2304]{1,0:T(8,128)(2,1)}, u32[]{:S(2)}, u32[]{:S(2)}) collective-permute-start(bf16[1024,2304]{1,0:T(8,128)(2,1)} %get-tuple-element.8), channel_id=1, source_target_pairs={{128,0},{0,128},{129,1},{1,129},{130,2},{2,130},{131,3},{3,131},{1... | collective-permute-start | bytes 14155784 | tf_op jit(solution)/shard_map/ppermute | solution.py:56
  110.6 37.6 %collective-permute-start.11 = (bf16[128,512]{1,0:T(8,128)(2,1)}, bf16[128,512]{1,0:T(8,128)(2,1)S(1)}, u32[]{:S(2)}, u32[]{:S(2)}) collective-permute-start(bf16[128,512]{1,0:T(8,128)(2,1)} %param.5), channel_id=1, source_target_pairs={{64,0},{80,1},{96,2},{112,3},{128,4},{144,5},{160,6},{176,7},{192,... | collective-permute-start | bytes 393224 | tf_op jit(solution)/shard_map/ppermute | solution.py:79
  125.1 28.1 %collective-permute-start.12 = (bf16[128,512]{1,0:T(8,128)(2,1)}, bf16[128,512]{1,0:T(8,128)(2,1)S(1)}, u32[]{:S(2)}, u32[]{:S(2)}) collective-permute-start(bf16[128,512]{1,0:T(8,128)(2,1)} %param.5), channel_id=1, source_target_pairs={{80,0},{96,1},{112,2},{128,3},{144,4},{160,5},{176,6},{192,7},{208... | collective-permute-start | bytes 393224 | tf_op jit(solution)/shard_map/ppermute | solution.py:79
  130.3 27.7 %collective-permute-start.13 = (bf16[128,512]{1,0:T(8,128)(2,1)}, bf16[128,512]{1,0:T(8,128)(2,1)S(1)}, u32[]{:S(2)}, u32[]{:S(2)}) collective-permute-start(bf16[128,512]{1,0:T(8,128)(2,1)} %param.5), channel_id=1, source_target_pairs={{96,0},{112,1},{128,2},{144,3},{160,4},{176,5},{192,6},{208,7},{22... | collective-permute-start | bytes 393224 | tf_op jit(solution)/shard_map/ppermute | solution.py:79
  133.8 27.0 %collective-permute-start.14 = (bf16[128,512]{1,0:T(8,128)(2,1)}, bf16[128,512]{1,0:T(8,128)(2,1)S(1)}, u32[]{:S(2)}, u32[]{:S(2)}) collective-permute-start(bf16[128,512]{1,0:T(8,128)(2,1)} %param.5), channel_id=1, source_target_pairs={{112,0},{128,1},{144,2},{160,3},{176,4},{192,5},{208,6},{224,7},{2... | collective-permute-start | bytes 393224 | tf_op jit(solution)/shard_map/ppermute | solution.py:79
  148.1 26.8 %collective-permute-start.15 = (bf16[128,512]{1,0:T(8,128)(2,1)}, bf16[128,512]{1,0:T(8,128)(2,1)S(1)}, u32[]{:S(2)}, u32[]{:S(2)}) collective-permute-start(bf16[128,512]{1,0:T(8,128)(2,1)} %param.5), channel_id=1, source_target_pairs={{128,0},{144,1},{160,2},{176,3},{192,4},{208,5},{224,6},{240,7},{0... | collective-permute-start | bytes 393224 | tf_op jit(solution)/shard_map/ppermute | solution.py:79
  153.2 28.7 %collective-permute-start.16 = (bf16[128,512]{1,0:T(8,128)(2,1)}, bf16[128,512]{1,0:T(8,128)(2,1)S(1)}, u32[]{:S(2)}, u32[]{:S(2)}) collective-permute-start(bf16[128,512]{1,0:T(8,128)(2,1)} %param.5), channel_id=1, source_target_pairs={{144,0},{160,1},{176,2},{192,3},{208,4},{224,5},{240,6},{0,7},{16,... | collective-permute-start | bytes 393224 | tf_op jit(solution)/shard_map/ppermute | solution.py:79
  158.0 33.9 %collective-permute-start.17 = (bf16[128,512]{1,0:T(8,128)(2,1)}, bf16[128,512]{1,0:T(8,128)(2,1)S(1)}, u32[]{:S(2)}, u32[]{:S(2)}) collective-permute-start(bf16[128,512]{1,0:T(8,128)(2,1)} %param.5), channel_id=1, source_target_pairs={{160,0},{176,1},{192,2},{208,3},{224,4},{240,5},{0,6},{16,7},{32,8... | collective-permute-start | bytes 393224 | tf_op jit(solution)/shard_map/ppermute | solution.py:79
  160.9 33.6 %collective-permute-start.18 = (bf16[128,512]{1,0:T(8,128)(2,1)}, bf16[128,512]{1,0:T(8,128)(2,1)S(1)}, u32[]{:S(2)}, u32[]{:S(2)}) collective-permute-start(bf16[128,512]{1,0:T(8,128)(2,1)} %param.5), channel_id=1, source_target_pairs={{176,0},{192,1},{208,2},{224,3},{240,4},{0,5},{16,6},{32,7},{48,8}... | collective-permute-start | bytes 393224 | tf_op jit(solution)/shard_map/ppermute | solution.py:79
  174.9 22.6 %collective-permute-start.19 = (bf16[128,512]{1,0:T(8,128)(2,1)}, bf16[128,512]{1,0:T(8,128)(2,1)S(1)}, u32[]{:S(2)}, u32[]{:S(2)}) collective-permute-start(bf16[128,512]{1,0:T(8,128)(2,1)} %param.5), channel_id=1, source_target_pairs={{192,0},{208,1},{224,2},{240,3},{0,4},{16,5},{32,6},{48,7},{64,8},... | collective-permute-start | bytes 393224 | tf_op jit(solution)/shard_map/ppermute | solution.py:79
  181.9 16.3 %collective-permute-start.20 = (bf16[128,512]{1,0:T(8,128)(2,1)}, bf16[128,512]{1,0:T(8,128)(2,1)S(1)}, u32[]{:S(2)}, u32[]{:S(2)}) collective-permute-start(bf16[128,512]{1,0:T(8,128)(2,1)} %param.5), channel_id=1, source_target_pairs={{208,0},{224,1},{240,2},{0,3},{16,4},{32,5},{48,6},{64,7},{80,8},{... | collective-permute-start | bytes 393224 | tf_op jit(solution)/shard_map/ppermute | solution.py:79
  191.9 18.2 %collective-permute-start.21 = (bf16[128,512]{1,0:T(8,128)(2,1)}, bf16[128,512]{1,0:T(8,128)(2,1)S(1)}, u32[]{:S(2)}, u32[]{:S(2)}) collective-permute-start(bf16[128,512]{1,0:T(8,128)(2,1)} %param.5), channel_id=1, source_target_pairs={{224,0},{240,1},{0,2},{16,3},{32,4},{48,5},{64,6},{80,7},{96,8},{1... | collective-permute-start | bytes 393224 | tf_op jit(solution)/shard_map/ppermute | solution.py:79
  194.5 16.3 %collective-permute-start.22 = (bf16[128,512]{1,0:T(8,128)(2,1)}, bf16[128,512]{1,0:T(8,128)(2,1)S(1)}, u32[]{:S(2)}, u32[]{:S(2)}) collective-permute-start(bf16[128,512]{1,0:T(8,128)(2,1)} %param.5), channel_id=1, source_target_pairs={{240,0},{0,1},{16,2},{32,3},{48,4},{64,5},{80,6},{96,7},{112,8},{1... | collective-permute-start | bytes 393224 | tf_op jit(solution)/shard_map/ppermute | solution.py:79
Sparse Core Ops, SparseCore 0:
  37.6 137.0 all-gather.1

commit v7 on v2

--- a/solution.py
+++ b/solution.py
@@ -69,7 +69,10 @@
     both = jnp.concatenate([out_grads, acts], axis=1)
     tok_weight = token_weights(domain_ids, domain_weights)
     weighted = (tok_weight[:, None] * both.astype(jnp.float32)).astype(jnp.bfloat16)
-    swapped = lax.ppermute(both, ROWS + ("feat",), transpose_pairs(n_rows, n_cols, n_dp, n_ring))
+    pairs = transpose_pairs(n_rows, n_cols, n_dp, n_ring)
+    step = both.shape[0] // 4
+    swapped = jnp.concatenate([lax.ppermute(both[i * step:(i + 1) * step], ROWS + ("feat",), pairs)
+                               for i in range(4)], axis=0)
     rows = lax.all_gather(swapped, "feat", axis=0, tiled=True)
     cols = gather_columns(weighted, n_dp, n_ring)
     grad_sum = contract_tokens(rows[:, :width_g], cols[:, :width_g])

time: 206 us -> 206 us (level)
  waiting for transfers between devices: 139 us -> 122 us
  starting transfers between devices: 16.2 us -> 32.8 us
    ppermute x1 -> x4, starting transfers between devices: 10.4 us -> 26.5 us  [local(): lax.ppermute(both[i * step:(i + 1) * step], ROWS + ('feat',), pairs)]
    ppermute x1 -> x4, waiting for transfers between devices: 24.5 us -> 11.6 us  [local(): lax.ppermute(both[i * step:(i + 1) * step], ROWS + ('feat',), pairs)]
    all_gather x1, waiting for transfers between devices: 55.4 us -> 45.7 us  [local(): rows = lax.all_gather(swapped, 'feat', axis=0, tiled=True)]
    ppermute x1, starting transfers between devices: 0.4 us -> 4.55 us  [gather_columns(): far_a = lax.ppermute(ahead[:half], 'ctx', ctx_shift(n_ring, 1, 0))]
    ppermute x1, waiting for transfers between devices: 1.68 us -> 4.25 us  [gather_columns(): far_b = lax.ppermute(behind[half:], 'ctx', ctx_shift(n_ring, -1, 0))]
    ppermute x1, starting transfers between devices: 2.51 us -> 0.01 us  [gather_columns(): other = lax.ppermute(mine, 'dp', [(1, 0), (0, 1)])]
    ppermute x1, waiting for transfers between devices: 15.2 us -> 17.4 us  [gather_columns(): near = lax.ppermute(block, 'ctx', ctx_shift(n_ring, 0, 1))]
    unnamed x8 -> x6, local copies, waits for them, and re-layouts: 6.64 us -> 5.8 us
  transfers between devices with their start and end apart: 8 -> 11, of which waited for: 7 -> 8; matrix products, arithmetic and copies ran while one was open for 5% -> 5% of each run, Pallas kernels for 0% -> 0%
where the time goes in v7:
time: 206 us; the launch traced here: 205 us
  waiting for transfers between devices  122 us (59%)
  starting transfers between devices  32.8 us (16%)
  matrix products  24.1 us (12%)
  between operations  14.1 us (7%)
  local copies, waits for them, and re-layouts  10.4 us (5%)
    all_gather x1, waiting for transfers between devices, local(): rows = lax.all_gather(swapped, 'feat', axis=0, tiled=True)  45.7 us
    ppermute x4, starting transfers between devices, local(): lax.ppermute(both[i * step:(i + 1) * step], ROWS + ('feat',), pairs)  26.5 us
    ppermute x1, waiting for transfers between devices, gather_columns(): ahead = lax.ppermute(own, 'ctx', ctx_shift(n_ring, 1, 0))  24.6 us
    dot_general x2, matrix products, contract_tokens(): lax.dot_general(left, right, (((0,), (0,)), ((), ())), preferred_element_...  24.1 us
    ppermute x1, waiting for transfers between devices, gather_columns(): near = lax.ppermute(block, 'ctx', ctx_shift(n_ring, 0, 1))  17.4 us
    ppermute x4, waiting for transfers between devices, local(): lax.ppermute(both[i * step:(i + 1) * step], ROWS + ('feat',), pairs)  11.6 us
    ppermute x1, waiting for transfers between devices, gather_columns(): far_a = lax.ppermute(ahead[:half], 'ctx', ctx_shift(n_ring, 1, 0))  10.2 us
    ppermute x1, waiting for transfers between devices, gather_columns(): other = lax.ppermute(mine, 'dp', [(1, 0), (0, 1)])  7.91 us
  transfers between devices with their start and end apart: 11, of which 8 were waited for; matrix products, arithmetic and copies ran while one was open for 5% of the time, Pallas kernels for 0%

profile of v7, /device:TPU:41, one launch (start us, length us, event | category | flops | bytes accessed | tf_op | source)
XLA Modules:
  0.0 205.0 jit_solution(2120940594506322037)
XLA Ops:
  7.2 0.0 all-gather.2.cloned.1.call-start
  7.2 1.0 constant_dynamic-update-slice_fusion.1
  8.3 0.9 constant_dynamic-update-slice_fusion
  9.2 10.4 %collective-permute-start = (bf16[32,2304]{1,0:T(8,128)(2,1)S(1)}, bf16[32,2304]{1,0:T(8,128)(2,1)S(1)}, u32[]{:S(2)}, u32[]{:S(2)}) collective-permute-start(bf16[32,2304]{1,0:T(8,128)(2,1)S(1)} %get-tuple-element.8), channel_id=1, source_target_pairs={{0,0},{16,1},{32,2},{48,3},{64,4},{80,5},{96,6},{112,7},{128,8},{1... | collective-permute-start | bytes 442376 | tf_op jit(solution)/shard_map/ppermute | solution.py:74
  19.6 4.0 %collective-permute-start.1 = (bf16[32,2304]{1,0:T(8,128)(2,1)S(1)}, bf16[32,2304]{1,0:T(8,128)(2,1)S(1)}, u32[]{:S(2)}, u32[]{:S(2)}) collective-permute-start(bf16[32,2304]{1,0:T(8,128)(2,1)S(1)} %get-tuple-element.11), channel_id=1, source_target_pairs={{0,0},{16,1},{32,2},{48,3},{64,4},{80,5},{96,6},{112,7},{128,8},{1... | collective-permute-start | bytes 442376 | tf_op jit(solution)/shard_map/ppermute | solution.py:74
  23.6 2.9 %collective-permute-start.2 = (bf16[32,2304]{1,0:T(8,128)(2,1)S(1)}, bf16[32,2304]{1,0:T(8,128)(2,1)S(1)}, u32[]{:S(2)}, u32[]{:S(2)}) collective-permute-start(bf16[32,2304]{1,0:T(8,128)(2,1)S(1)} %get-tuple-element.10), channel_id=1, source_target_pairs={{0,0},{16,1},{32,2},{48,3},{64,4},{80,5},{96,6},{112,7},{128,8},{1... | collective-permute-start | bytes 442376 | tf_op jit(solution)/shard_map/ppermute | solution.py:74
  26.6 9.1 %collective-permute-start.3 = (bf16[32,2304]{1,0:T(8,128)(2,1)S(1)}, bf16[32,2304]{1,0:T(8,128)(2,1)S(1)}, u32[]{:S(2)}, u32[]{:S(2)}) collective-permute-start(bf16[32,2304]{1,0:T(8,128)(2,1)S(1)} %get-tuple-element.9), channel_id=1, source_target_pairs={{0,0},{16,1},{32,2},{48,3},{64,4},{80,5},{96,6},{112,7},{128,8},{1... | collective-permute-start | bytes 442376 | tf_op jit(solution)/shard_map/ppermute | solution.py:74
  35.7 0.0 collective-permute-done
  35.7 0.0 collective-permute-done.1
  35.8 5.2 %collective-permute-done.2 = bf16[32,2304]{1,0:T(8,128)(2,1)S(1)} collective-permute-done((bf16[32,2304]{1,0:T(8,128)(2,1)S(1)}, bf16[32,2304]{1,0:T(8,128)(2,1)S(1)}, u32[]{:S(2)}, u32[]{:S(2)}) %collective-permute-start.2) | collective-permute-done | bytes 147488 | tf_op jit(solution)/shard_map/ppermute | solution.py:74
  41.0 6.4 %collective-permute-done.3 = bf16[32,2304]{1,0:T(8,128)(2,1)S(1)} collective-permute-done((bf16[32,2304]{1,0:T(8,128)(2,1)S(1)}, bf16[32,2304]{1,0:T(8,128)(2,1)S(1)}, u32[]{:S(2)}, u32[]{:S(2)}) %collective-permute-start.3) | collective-permute-done | bytes 147488 | tf_op jit(solution)/shard_map/ppermute | solution.py:74
  47.3 0.9 pad_maximum_fusion.1
  48.2 0.0 all-gather.2.cloned.1.call-update
  48.2 0.8 select_reduce_fusion
  49.0 0.2 constant_dynamic-update-slice_fusion.7
  49.1 0.1 collective-permute-start.4
  49.2 17.4 %collective-permute-done.4 = bf16[128,2304]{1,0:T(8,128)(2,1)S(1)} collective-permute-done((bf16[128,2304]{1,0:T(8,128)(2,1)S(1)}, bf16[128,2304]{1,0:T(8,128)(2,1)S(1)}, u32[]{:S(2)}, u32[]{:S(2)}) %collective-permute-start.4) | collective-permute-done | bytes 589856 | tf_op jit(solution)/shard_map/ppermute | solution.py:49
  66.7 0.1 pad_maximum_fusion
  66.7 0.1 collective-permute-start.5
  66.8 1.5 collective-permute-start.7
  68.3 0.8 constant_dynamic-update-slice_fusion.14
  69.1 24.6 %collective-permute-done.5 = bf16[256,2304]{1,0:T(8,128)(2,1)S(1)} collective-permute-done((bf16[256,2304]{1,0:T(8,128)(2,1)S(1)}, bf16[256,2304]{1,0:T(8,128)(2,1)S(1)}, u32[]{:S(2)}, u32[]{:S(2)}) %collective-permute-start.5) | collective-permute-done | bytes 1179680 | tf_op jit(solution)/shard_map/ppermute | solution.py:51
  93.8 4.5 %collective-permute-start.6 = (bf16[128,2304]{1,0:T(8,128)(2,1)S(1)}, bf16[128,2304]{1,0:T(8,128)(2,1)S(1)}, u32[]{:S(2)}, u32[]{:S(2)}) collective-permute-start(bf16[128,2304]{1,0:T(8,128)(2,1)S(1)} %slice.45), channel_id=1, source_target_pairs={{32,0},{48,16},{64,32},{80,48},{96,64},{112,80},{0,96},{16,112},{3... | collective-permute-start | bytes 1769480 | tf_op jit(solution)/shard_map/ppermute | solution.py:53
  98.4 0.9 constant_dynamic-update-slice_fusion.6
  99.3 0.0 collective-permute-done.7
  99.3 0.1 collective-permute-start.8
  99.4 1.2 constant_dynamic-update-slice_fusion.5
  100.6 10.2 %collective-permute-done.6 = bf16[128,2304]{1,0:T(8,128)(2,1)S(1)} collective-permute-done((bf16[128,2304]{1,0:T(8,128)(2,1)S(1)}, bf16[128,2304]{1,0:T(8,128)(2,1)S(1)}, u32[]{:S(2)}, u32[]{:S(2)}) %collective-permute-start.6) | collective-permute-done | bytes 589856 | tf_op jit(solution)/shard_map/ppermute | solution.py:53
  110.8 0.9 constant_dynamic-update-slice_fusion.4
  111.7 4.3 %collective-permute-done.8 = bf16[128,2304]{1,0:T(8,128)(2,1)S(1)} collective-permute-done((bf16[128,2304]{1,0:T(8,128)(2,1)S(1)}, bf16[128,2304]{1,0:T(8,128)(2,1)S(1)}, u32[]{:S(2)}, u32[]{:S(2)}) %collective-permute-start.8) | collective-permute-done | bytes 589856 | tf_op jit(solution)/shard_map/ppermute | solution.py:54
  116.0 0.9 constant_dynamic-update-slice_fusion.3
  116.9 1.2 constant_dynamic-update-slice_fusion.2
  118.0 0.0 collective-permute-start.9
  118.1 7.9 %collective-permute-done.9 = bf16[1024,2304]{1,0:T(8,128)(2,1)S(1)} collective-permute-done((bf16[1024,2304]{1,0:T(8,128)(2,1)S(1)}, bf16[1024,2304]{1,0:T(8,128)(2,1)S(1)}, u32[]{:S(2)}, u32[]{:S(2)}) %collective-permute-start.9) | collective-permute-done | bytes 4718624 | tf_op jit(solution)/shard_map/ppermute | solution.py:56
  126.0 2.4 %constant_dynamic-update-slice_fusion.8 = bf16[2048,2304]{1,0:T(8,128)(2,1)} fusion(bf16[2048,2304]{1,0:T(8,128)(2,1)} %get-tuple-element.5, bf16[1024,2304]{1,0:T(8,128)(2,1)S(1)} %collective-permute-done.9), kind=kLoop, calls=%fused_computation.19 | loop fusion | bytes 9437184 | tf_op jit(solution)/shard_map/concatenate | solution.py:57
  128.4 45.7 %all-gather.2.cloned.1.call-done = bf16[2048,2304]{1,0:T(8,128)(2,1)} async-done(((bf16[128,2304]{1,0:T(8,128)(2,1)}), bf16[2048,2304]{1,0:T(8,128)(2,1)}) %all-gather.2.cloned.1.call-update) | async-done | bytes 9437200 | tf_op jit(solution)/shard_map/all_gather | solution.py:76
  174.1 4.3 %fusion.10 = bf16[512,512]{1,0:T(8,128)(2,1)} fusion(bf16[2048,2304]{1,0:T(8,128)(2,1)} %constant_dynamic-update-slice_fusion.8, bf16[2048,2304]{1,0:T(8,128)(2,1)} %all-gather.2.cloned.1.call-done), kind=kOutput, calls=%fused_computation.7 | convolution fusion | flops 1074266112 | bytes 4718592 | tf_op jit(solution)/shard_map/dot_general | solution.py:17
  178.4 19.7 %multiply_convert_fusion = bf16[1792,1792]{1,0:T(8,128)(2,1)} fusion(bf16[2048,2304]{1,0:T(8,128)(2,1)} %constant_dynamic-update-slice_fusion.8, bf16[2048,2304]{1,0:T(8,128)(2,1)} %all-gather.2.cloned.1.call-done), kind=kOutput, calls=%fused_computation | convolution fusion | flops 13159759872 | bytes 21102592 | tf_op jit(solution)/shard_map/dot_general | solution.py:17
  (4 shorter events, 0.1 us)
Async XLA Ops:
  7.2 167.0 %all-gather.2.cloned.1.call-start = ((), (), s32[]{:S(2)}) async-start(), calls=%async_computation | async-start | bytes 10027008 | tf_op jit(solution)/shard_map/all_gather | solution.py:76
  9.2 26.5 %collective-permute-start = (bf16[32,2304]{1,0:T(8,128)(2,1)S(1)}, bf16[32,2304]{1,0:T(8,128)(2,1)S(1)}, u32[]{:S(2)}, u32[]{:S(2)}) collective-permute-start(bf16[32,2304]{1,0:T(8,128)(2,1)S(1)} %get-tuple-element.8), channel_id=1, source_target_pairs={{0,0},{16,1},{32,2},{48,3},{64,4},{80,5},{96,6},{112,7},{128,8},{1... | collective-permute-start | bytes 442376 | tf_op jit(solution)/shard_map/ppermute | solution.py:74
  19.6 16.1 %collective-permute-start.1 = (bf16[32,2304]{1,0:T(8,128)(2,1)S(1)}, bf16[32,2304]{1,0:T(8,128)(2,1)S(1)}, u32[]{:S(2)}, u32[]{:S(2)}) collective-permute-start(bf16[32,2304]{1,0:T(8,128)(2,1)S(1)} %get-tuple-element.11), channel_id=1, source_target_pairs={{0,0},{16,1},{32,2},{48,3},{64,4},{80,5},{96,6},{112,7},{128,8},{1... | collective-permute-start | bytes 442376 | tf_op jit(solution)/shard_map/ppermute | solution.py:74
  23.6 17.3 %collective-permute-start.2 = (bf16[32,2304]{1,0:T(8,128)(2,1)S(1)}, bf16[32,2304]{1,0:T(8,128)(2,1)S(1)}, u32[]{:S(2)}, u32[]{:S(2)}) collective-permute-start(bf16[32,2304]{1,0:T(8,128)(2,1)S(1)} %get-tuple-element.10), channel_id=1, source_target_pairs={{0,0},{16,1},{32,2},{48,3},{64,4},{80,5},{96,6},{112,7},{128,8},{1... | collective-permute-start | bytes 442376 | tf_op jit(solution)/shard_map/ppermute | solution.py:74
  26.6 20.7 %collective-permute-start.3 = (bf16[32,2304]{1,0:T(8,128)(2,1)S(1)}, bf16[32,2304]{1,0:T(8,128)(2,1)S(1)}, u32[]{:S(2)}, u32[]{:S(2)}) collective-permute-start(bf16[32,2304]{1,0:T(8,128)(2,1)S(1)} %get-tuple-element.9), channel_id=1, source_target_pairs={{0,0},{16,1},{32,2},{48,3},{64,4},{80,5},{96,6},{112,7},{128,8},{1... | collective-permute-start | bytes 442376 | tf_op jit(solution)/shard_map/ppermute | solution.py:74
  49.1 17.5 %collective-permute-start.4 = (bf16[128,2304]{1,0:T(8,128)(2,1)S(1)}, bf16[128,2304]{1,0:T(8,128)(2,1)S(1)}, u32[]{:S(2)}, u32[]{:S(2)}) collective-permute-start(bf16[128,2304]{1,0:T(8,128)(2,1)S(1)} %get-tuple-element.3), channel_id=1, source_target_pairs={{16,0},{0,16},{48,32},{32,48},{80,64},{64,80},{112,96},{96,112},{1... | collective-permute-start | bytes 1769480 | tf_op jit(solution)/shard_map/ppermute | solution.py:49
  66.7 27.0 %collective-permute-start.5 = (bf16[256,2304]{1,0:T(8,128)(2,1)S(1)}, bf16[256,2304]{1,0:T(8,128)(2,1)S(1)}, u32[]{:S(2)}, u32[]{:S(2)}) collective-permute-start(bf16[256,2304]{1,0:T(8,128)(2,1)S(1)} %pad_maximum_fusion), channel_id=1, source_target_pairs={{32,0},{48,16},{64,32},{80,48},{96,64},{112,80},{0,96},{16,112},{3... | collective-permute-start | bytes 3538952 | tf_op jit(solution)/shard_map/ppermute | solution.py:51
  66.8 32.5 %collective-permute-start.7 = (bf16[256,2304]{1,0:T(8,128)(2,1)S(1)}, bf16[256,2304]{1,0:T(8,128)(2,1)S(1)}, u32[]{:S(2)}, u32[]{:S(2)}) collective-permute-start(bf16[256,2304]{1,0:T(8,128)(2,1)S(1)} %pad_maximum_fusion), channel_id=1, source_target_pairs={{96,0},{112,16},{0,32},{16,48},{32,64},{48,80},{64,96},{80,112},{9... | collective-permute-start | bytes 3538952 | tf_op jit(solution)/shard_map/ppermute | solution.py:52
  93.8 17.0 %collective-permute-start.6 = (bf16[128,2304]{1,0:T(8,128)(2,1)S(1)}, bf16[128,2304]{1,0:T(8,128)(2,1)S(1)}, u32[]{:S(2)}, u32[]{:S(2)}) collective-permute-start(bf16[128,2304]{1,0:T(8,128)(2,1)S(1)} %slice.45), channel_id=1, source_target_pairs={{32,0},{48,16},{64,32},{80,48},{96,64},{112,80},{0,96},{16,112},{3... | collective-permute-start | bytes 1769480 | tf_op jit(solution)/shard_map/ppermute | solution.py:53
  99.3 16.6 %collective-permute-start.8 = (bf16[128,2304]{1,0:T(8,128)(2,1)S(1)}, bf16[128,2304]{1,0:T(8,128)(2,1)S(1)}, u32[]{:S(2)}, u32[]{:S(2)}) collective-permute-start(bf16[128,2304]{1,0:T(8,128)(2,1)S(1)} %slice.46), channel_id=1, source_target_pairs={{96,0},{112,16},{0,32},{16,48},{32,64},{48,80},{64,96},{80,112},{9... | collective-permute-start | bytes 1769480 | tf_op jit(solution)/shard_map/ppermute | solution.py:54
  118.0 7.9 %collective-permute-start.9 = (bf16[1024,2304]{1,0:T(8,128)(2,1)S(1)}, bf16[1024,2304]{1,0:T(8,128)(2,1)S(1)}, u32[]{:S(2)}, u32[]{:S(2)}) collective-permute-start(bf16[1024,2304]{1,0:T(8,128)(2,1)S(1)} %get-tuple-element.4), channel_id=1, source_target_pairs={{128,0},{0,128},{129,1},{1,129},{130,2},{2,130},{131,3},{3,131},{1... | collective-permute-start | bytes 14155784 | tf_op jit(solution)/shard_map/ppermute | solution.py:56
Sparse Core Ops, SparseCore 0:
  48.3 125.7 all-gather.1

commit v8 on v2

--- a/solution.py
+++ b/solution.py
@@ -69,7 +69,9 @@
     both = jnp.concatenate([out_grads, acts], axis=1)
     tok_weight = token_weights(domain_ids, domain_weights)
     weighted = (tok_weight[:, None] * both.astype(jnp.float32)).astype(jnp.bfloat16)
-    swapped = lax.ppermute(both, ROWS + ("feat",), transpose_pairs(n_rows, n_cols, n_dp, n_ring))
+    pairs = transpose_pairs(n_rows, n_cols, n_dp, n_ring)
+    swapped = jnp.concatenate([lax.ppermute(out_grads, ROWS + ("feat",), pairs),
+                               lax.ppermute(acts, ROWS + ("feat",), pairs)], axis=1)
     rows = lax.all_gather(swapped, "feat", axis=0, tiled=True)
     cols = gather_columns(weighted, n_dp, n_ring)
     grad_sum = contract_tokens(rows[:, :width_g], cols[:, :width_g])

time: 206 us -> 205 us (level)
  waiting for transfers between devices: 139 us -> 134 us
  starting transfers between devices: 16.2 us -> 20.7 us
  local copies, waits for them, and re-layouts: 11.2 us -> 8.45 us
    ppermute x1 -> x2, starting transfers between devices: 10.4 us -> 14.4 us  [the longest x1 10.4 us: local(): lax.ppermute(out_grads, ROWS + ('feat',), pairs)]
    ppermute x1 -> x2, waiting for transfers between devices: 24.5 us -> 20.7 us  [the longest x1 20.7 us: local(): lax.ppermute(acts, ROWS + ('feat',), pairs)]
    unnamed x8 -> x5, local copies, waits for them, and re-layouts: 6.64 us -> 4.78 us
  transfers between devices with their start and end apart: 8 -> 9, of which waited for: 7 -> 7; matrix products, arithmetic and copies ran while one was open for 5% -> 5% of each run, Pallas kernels for 0% -> 0%
where the time goes in v8:
time: 205 us; the launch traced here: 204 us
  waiting for transfers between devices  134 us (65%)
  matrix products  24.1 us (12%)
  starting transfers between devices  20.7 us (10%)
  between operations  14.1 us (7%)
  local copies, waits for them, and re-layouts  8.45 us (4%)
  other arithmetic  2.95 us (1%)
    all_gather x1, waiting for transfers between devices, local(): rows = lax.all_gather(swapped, 'feat', axis=0, tiled=True)  54.9 us
    ppermute x1, waiting for transfers between devices, gather_columns(): ahead = lax.ppermute(own, 'ctx', ctx_shift(n_ring, 1, 0))  24.8 us
    dot_general x2, matrix products, contract_tokens(): lax.dot_general(left, right, (((0,), (0,)), ((), ())), preferred_element_...  24.1 us
    ppermute x1, waiting for transfers between devices, local(): lax.ppermute(acts, ROWS + ('feat',), pairs)  20.7 us
    ppermute x1, waiting for transfers between devices, gather_columns(): near = lax.ppermute(block, 'ctx', ctx_shift(n_ring, 0, 1))  15.2 us
    ppermute x1, starting transfers between devices, local(): lax.ppermute(out_grads, ROWS + ('feat',), pairs)  10.4 us
    ppermute x1, waiting for transfers between devices, gather_columns(): far_a = lax.ppermute(ahead[:half], 'ctx', ctx_shift(n_ring, 1, 0))  10 us
    ppermute x1, waiting for transfers between devices, gather_columns(): other = lax.ppermute(mine, 'dp', [(1, 0), (0, 1)])  7.54 us
  transfers between devices with their start and end apart: 9, of which 7 were waited for; matrix products, arithmetic and copies ran while one was open for 5% of the time, Pallas kernels for 0%

profile of v8, /device:TPU:41, one launch (start us, length us, event | category | flops | bytes accessed | tf_op | source)
XLA Modules:
  0.0 204.3 jit_solution(9633336941681814869)
XLA Ops:
  7.2 0.0 all-gather.2.cloned.1.call-start
  7.2 10.4 %collective-permute-start = (bf16[128,1792]{1,0:T(8,128)(2,1)}, bf16[128,1792]{1,0:T(8,128)(2,1)S(1)}, u32[]{:S(2)}, u32[]{:S(2)}) collective-permute-start(bf16[128,1792]{1,0:T(8,128)(2,1)} %param.4), channel_id=1, source_target_pairs={{0,0},{16,1},{32,2},{48,3},{64,4},{80,5},{96,6},{112,7},{128,8},{1... | collective-permute-start | bytes 1376264 | tf_op jit(solution)/shard_map/ppermute | solution.py:73
  17.6 4.0 %collective-permute-start.1 = (bf16[128,512]{1,0:T(8,128)(2,1)}, bf16[128,512]{1,0:T(8,128)(2,1)S(1)}, u32[]{:S(2)}, u32[]{:S(2)}) collective-permute-start(bf16[128,512]{1,0:T(8,128)(2,1)} %param.5), channel_id=1, source_target_pairs={{0,0},{16,1},{32,2},{48,3},{64,4},{80,5},{96,6},{112,7},{128,8},{1... | collective-permute-start | bytes 393224 | tf_op jit(solution)/shard_map/ppermute | solution.py:74
  21.6 20.7 %collective-permute-done.1 = bf16[128,512]{1,0:T(8,128)(2,1)S(1)} collective-permute-done((bf16[128,512]{1,0:T(8,128)(2,1)}, bf16[128,512]{1,0:T(8,128)(2,1)S(1)}, u32[]{:S(2)}, u32[]{:S(2)}) %collective-permute-start.1) | collective-permute-done | bytes 131104 | tf_op jit(solution)/shard_map/ppermute | solution.py:74
  42.3 0.0 collective-permute-done
  42.3 0.9 pad_maximum_fusion.1
  43.2 0.0 all-gather.2.cloned.1.call-update
  43.2 0.8 select_reduce_fusion
  44.0 1.3 constant_dynamic-update-slice_fusion.5
  45.2 0.1 collective-permute-start.2
  45.3 15.2 %collective-permute-done.2 = bf16[128,2304]{1,0:T(8,128)(2,1)S(1)} collective-permute-done((bf16[128,2304]{1,0:T(8,128)(2,1)S(1)}, bf16[128,2304]{1,0:T(8,128)(2,1)S(1)}, u32[]{:S(2)}, u32[]{:S(2)}) %collective-permute-start.2) | collective-permute-done | bytes 589856 | tf_op jit(solution)/shard_map/ppermute | solution.py:49
  60.5 0.1 pad_maximum_fusion
  60.6 0.1 collective-permute-start.3
  60.7 1.5 collective-permute-start.5
  62.1 0.9 constant_dynamic-update-slice_fusion.12
  63.0 24.8 %collective-permute-done.3 = bf16[256,2304]{1,0:T(8,128)(2,1)S(1)} collective-permute-done((bf16[256,2304]{1,0:T(8,128)(2,1)S(1)}, bf16[256,2304]{1,0:T(8,128)(2,1)S(1)}, u32[]{:S(2)}, u32[]{:S(2)}) %collective-permute-start.3) | collective-permute-done | bytes 1179680 | tf_op jit(solution)/shard_map/ppermute | solution.py:51
  87.9 0.4 collective-permute-start.4
  88.3 0.9 constant_dynamic-update-slice_fusion.4
  89.2 0.0 collective-permute-done.5
  89.2 1.2 collective-permute-start.6
  90.5 1.2 constant_dynamic-update-slice_fusion.3
  91.6 10.0 %collective-permute-done.4 = bf16[128,2304]{1,0:T(8,128)(2,1)S(1)} collective-permute-done((bf16[128,2304]{1,0:T(8,128)(2,1)S(1)}, bf16[128,2304]{1,0:T(8,128)(2,1)S(1)}, u32[]{:S(2)}, u32[]{:S(2)}) %collective-permute-start.4) | collective-permute-done | bytes 589856 | tf_op jit(solution)/shard_map/ppermute | solution.py:53
  101.6 0.9 constant_dynamic-update-slice_fusion.2
  102.5 0.9 collective-permute-done.6
  103.5 0.9 constant_dynamic-update-slice_fusion.1
  104.4 1.2 constant_dynamic-update-slice_fusion
  105.5 3.0 %collective-permute-start.7 = (bf16[1024,2304]{1,0:T(8,128)(2,1)S(1)}, bf16[1024,2304]{1,0:T(8,128)(2,1)S(1)}, u32[]{:S(2)}, u32[]{:S(2)}) collective-permute-start(bf16[1024,2304]{1,0:T(8,128)(2,1)S(1)} %get-tuple-element.4), channel_id=1, source_target_pairs={{128,0},{0,128},{129,1},{1,129},{130,2},{2,130},{131,3},{3,131},{1... | collective-permute-start | bytes 14155784 | tf_op jit(solution)/shard_map/ppermute | solution.py:56
  108.6 7.5 %collective-permute-done.7 = bf16[1024,2304]{1,0:T(8,128)(2,1)S(1)} collective-permute-done((bf16[1024,2304]{1,0:T(8,128)(2,1)S(1)}, bf16[1024,2304]{1,0:T(8,128)(2,1)S(1)}, u32[]{:S(2)}, u32[]{:S(2)}) %collective-permute-start.7) | collective-permute-done | bytes 4718624 | tf_op jit(solution)/shard_map/ppermute | solution.py:56
  116.1 2.4 %constant_dynamic-update-slice_fusion.6 = bf16[2048,2304]{1,0:T(8,128)(2,1)} fusion(bf16[2048,2304]{1,0:T(8,128)(2,1)} %get-tuple-element.5, bf16[1024,2304]{1,0:T(8,128)(2,1)S(1)} %collective-permute-done.7), kind=kLoop, calls=%fused_computation.17 | loop fusion | bytes 9437184 | tf_op jit(solution)/shard_map/concatenate | solution.py:57
  118.5 54.9 %all-gather.2.cloned.1.call-done = bf16[2048,2304]{1,0:T(8,128)(2,1)} async-done(((bf16[128,2304]{1,0:T(8,128)(2,1)}), bf16[2048,2304]{1,0:T(8,128)(2,1)}) %all-gather.2.cloned.1.call-update) | async-done | bytes 9437200 | tf_op jit(solution)/shard_map/all_gather | solution.py:75
  173.4 19.7 %multiply_convert_fusion = bf16[1792,1792]{1,0:T(8,128)(2,1)} fusion(bf16[2048,2304]{1,0:T(8,128)(2,1)} %constant_dynamic-update-slice_fusion.6, bf16[2048,2304]{1,0:T(8,128)(2,1)} %all-gather.2.cloned.1.call-done), kind=kOutput, calls=%fused_computation | convolution fusion | flops 13159759872 | bytes 21102592 | tf_op jit(solution)/shard_map/dot_general | solution.py:17
  193.2 4.3 %fusion.10 = bf16[512,512]{1,0:T(8,128)(2,1)} fusion(bf16[2048,2304]{1,0:T(8,128)(2,1)} %constant_dynamic-update-slice_fusion.6, bf16[2048,2304]{1,0:T(8,128)(2,1)} %all-gather.2.cloned.1.call-done), kind=kOutput, calls=%fused_computation.7 | convolution fusion | flops 1074266112 | bytes 4718592 | tf_op jit(solution)/shard_map/dot_general | solution.py:17
  (3 shorter events, 0.1 us)
Async XLA Ops:
  7.2 166.3 %all-gather.2.cloned.1.call-start = ((), (), s32[]{:S(2)}) async-start(), calls=%async_computation | async-start | bytes 10027008 | tf_op jit(solution)/shard_map/all_gather | solution.py:75
  7.2 35.1 %collective-permute-start = (bf16[128,1792]{1,0:T(8,128)(2,1)}, bf16[128,1792]{1,0:T(8,128)(2,1)S(1)}, u32[]{:S(2)}, u32[]{:S(2)}) collective-permute-start(bf16[128,1792]{1,0:T(8,128)(2,1)} %param.4), channel_id=1, source_target_pairs={{0,0},{16,1},{32,2},{48,3},{64,4},{80,5},{96,6},{112,7},{128,8},{1... | collective-permute-start | bytes 1376264 | tf_op jit(solution)/shard_map/ppermute | solution.py:73
  17.6 24.7 %collective-permute-start.1 = (bf16[128,512]{1,0:T(8,128)(2,1)}, bf16[128,512]{1,0:T(8,128)(2,1)S(1)}, u32[]{:S(2)}, u32[]{:S(2)}) collective-permute-start(bf16[128,512]{1,0:T(8,128)(2,1)} %param.5), channel_id=1, source_target_pairs={{0,0},{16,1},{32,2},{48,3},{64,4},{80,5},{96,6},{112,7},{128,8},{1... | collective-permute-start | bytes 393224 | tf_op jit(solution)/shard_map/ppermute | solution.py:74
  45.2 15.3 %collective-permute-start.2 = (bf16[128,2304]{1,0:T(8,128)(2,1)S(1)}, bf16[128,2304]{1,0:T(8,128)(2,1)S(1)}, u32[]{:S(2)}, u32[]{:S(2)}) collective-permute-start(bf16[128,2304]{1,0:T(8,128)(2,1)S(1)} %get-tuple-element.3), channel_id=1, source_target_pairs={{16,0},{0,16},{48,32},{32,48},{80,64},{64,80},{112,96},{96,112},{1... | collective-permute-start | bytes 1769480 | tf_op jit(solution)/shard_map/ppermute | solution.py:49
  60.6 27.2 %collective-permute-start.3 = (bf16[256,2304]{1,0:T(8,128)(2,1)S(1)}, bf16[256,2304]{1,0:T(8,128)(2,1)S(1)}, u32[]{:S(2)}, u32[]{:S(2)}) collective-permute-start(bf16[256,2304]{1,0:T(8,128)(2,1)S(1)} %pad_maximum_fusion), channel_id=1, source_target_pairs={{32,0},{48,16},{64,32},{80,48},{96,64},{112,80},{0,96},{16,112},{3... | collective-permute-start | bytes 3538952 | tf_op jit(solution)/shard_map/ppermute | solution.py:51
  60.7 28.5 %collective-permute-start.5 = (bf16[256,2304]{1,0:T(8,128)(2,1)S(1)}, bf16[256,2304]{1,0:T(8,128)(2,1)S(1)}, u32[]{:S(2)}, u32[]{:S(2)}) collective-permute-start(bf16[256,2304]{1,0:T(8,128)(2,1)S(1)} %pad_maximum_fusion), channel_id=1, source_target_pairs={{96,0},{112,16},{0,32},{16,48},{32,64},{48,80},{64,96},{80,112},{9... | collective-permute-start | bytes 3538952 | tf_op jit(solution)/shard_map/ppermute | solution.py:52
  87.9 13.8 %collective-permute-start.4 = (bf16[128,2304]{1,0:T(8,128)(2,1)S(1)}, bf16[128,2304]{1,0:T(8,128)(2,1)S(1)}, u32[]{:S(2)}, u32[]{:S(2)}) collective-permute-start(bf16[128,2304]{1,0:T(8,128)(2,1)S(1)} %slice.25), channel_id=1, source_target_pairs={{32,0},{48,16},{64,32},{80,48},{96,64},{112,80},{0,96},{16,112},{3... | collective-permute-start | bytes 1769480 | tf_op jit(solution)/shard_map/ppermute | solution.py:53
  89.2 14.2 %collective-permute-start.6 = (bf16[128,2304]{1,0:T(8,128)(2,1)S(1)}, bf16[128,2304]{1,0:T(8,128)(2,1)S(1)}, u32[]{:S(2)}, u32[]{:S(2)}) collective-permute-start(bf16[128,2304]{1,0:T(8,128)(2,1)S(1)} %slice.26), channel_id=1, source_target_pairs={{96,0},{112,16},{0,32},{16,48},{32,64},{48,80},{64,96},{80,112},{9... | collective-permute-start | bytes 1769480 | tf_op jit(solution)/shard_map/ppermute | solution.py:54
  105.5 10.6 %collective-permute-start.7 = (bf16[1024,2304]{1,0:T(8,128)(2,1)S(1)}, bf16[1024,2304]{1,0:T(8,128)(2,1)S(1)}, u32[]{:S(2)}, u32[]{:S(2)}) collective-permute-start(bf16[1024,2304]{1,0:T(8,128)(2,1)S(1)} %get-tuple-element.4), channel_id=1, source_target_pairs={{128,0},{0,128},{129,1},{1,129},{130,2},{2,130},{131,3},{3,131},{1... | collective-permute-start | bytes 14155784 | tf_op jit(solution)/shard_map/ppermute | solution.py:56
Sparse Core Ops, SparseCore 0:
  43.3 130.0 all-gather.1

commit v9 on v8

v9 whole, which is shorter than its diff:
```python
import jax
import jax.numpy as jnp
from jax import lax
from jax.sharding import Mesh
from jax.sharding import PartitionSpec as P

AXES = ("dp", "y", "zlo", "x", "zhi")
ROWS = ("dp", "y", "zlo")
COLS = ("x", "zhi")
CTX = ("y", "zlo")
PAIR = 2
SIDE = 4


def token_weights(tok_ids, domain_weights):
    labels = jnp.arange(domain_weights.shape[0], dtype=jnp.int32)
    match = tok_ids[:, None] == labels[None, :]
    return jnp.sum(jnp.where(match, domain_weights[None, :], 0), axis=1).astype(jnp.float32)


def contract_tokens(left, right):
    return lax.dot_general(
        left, right, (((0,), (0,)), ((), ())), preferred_element_type=jnp.float32
    )


def split_row(r, n_ring):
    per_dp = n_ring * PAIR
    return r // per_dp, (r % per_dp) // PAIR, r % PAIR


def token_block(r, p, n_dp, n_ring):
    dp, y, z = split_row(r, n_ring)
    ddp, dy, dz = split_row(p, n_ring)
    return ((dp + ddp) % n_dp) * n_ring * PAIR + ((y + dy) % n_ring) * PAIR + (z + dz) % PAIR


def transpose_pairs(n_rows, n_cols, n_dp, n_ring):
    def place(c):
        return (c % SIDE) * SIDE + c // SIDE
    return [(token_block(r, place(c), n_dp, n_ring) * n_cols + r, r * n_cols + c)
            for r in range(n_rows) for c in range(n_cols)]


def ctx_shift(n_ring, dy, dz):
    pairs = []
    for y in range(n_ring):
        for z in range(PAIR):
            src = ((y + dy) % n_ring) * PAIR + (z + dz) % PAIR
            pairs.append((src, y * PAIR + z))
    return pairs


def gather_columns(block, n_dp, n_ring):
    half = block.shape[0]
    near = lax.ppermute(block, CTX, ctx_shift(n_ring, 0, 1))
    own = jnp.concatenate([block, near], axis=0)
    ahead = lax.ppermute(own, CTX, ctx_shift(n_ring, 1, 0))
    behind = lax.ppermute(own, CTX, ctx_shift(n_ring, -1, 0))
    far_a = lax.ppermute(ahead[:half], CTX, ctx_shift(n_ring, 1, 0))
    far_b = lax.ppermute(behind[half:], CTX, ctx_shift(n_ring, -1, 0))
    mine = jnp.concatenate([own, ahead, far_a, far_b, behind], axis=0)
    other = lax.ppermute(mine, "dp", [(1, 0), (0, 1)])
    return jnp.concatenate([mine, other], axis=0)


def local(out_grads, acts, domain_ids, domain_weights):
    n_dp = lax.axis_size("dp")
    n_ctx = lax.axis_size(CTX)
    n_rows = n_dp * n_ctx
    n_cols = lax.axis_size(COLS)
    assert lax.axis_size("x") == SIDE and lax.axis_size("zhi") == SIDE
    n_ring = n_ctx // PAIR
    assert n_rows == n_cols and n_dp == 2 and n_ring == 4 and n_ctx % PAIR == 0
    inv_count = 1.0 / (out_grads.shape[0] * n_rows)
    width_g = out_grads.shape[1]
    both = jnp.concatenate([out_grads, acts], axis=1)
    tok_weight = token_weights(domain_ids, domain_weights)
    weighted = (tok_weight[:, None] * both.astype(jnp.float32)).astype(jnp.bfloat16)
    pairs = transpose_pairs(n_rows, n_cols, n_dp, n_ring)
    swapped = jnp.concatenate([lax.ppermute(out_grads, AXES, pairs),
                               lax.ppermute(acts, AXES, pairs)], axis=1)
    rows = lax.all_gather(swapped, ("zhi", "x"), axis=0, tiled=True)
    cols = gather_columns(weighted, n_dp, n_ring)
    grad_sum = contract_tokens(rows[:, :width_g], cols[:, :width_g])
    act_sum = contract_tokens(rows[:, width_g:], cols[:, width_g:])
    grad_factor = (grad_sum * inv_count).astype(jnp.bfloat16)
    act_factor = (act_sum * inv_count).astype(jnp.bfloat16)
    return (grad_factor, act_factor)


def solution(mesh):
    n_dp, n_ctx, n_feat = mesh.devices.shape
    split = Mesh(mesh.devices.reshape(n_dp, n_ctx // PAIR, PAIR, n_feat // SIDE, SIDE), AXES)
    in_specs = (P(ROWS, COLS), P(ROWS, COLS), P(ROWS), P())
    out_specs = (P(ROWS, COLS), P(ROWS, COLS))
    return jax.shard_map(local, mesh=split, in_specs=in_specs, out_specs=out_specs, check_vma=False)
```

time: 205 us -> 208 us (1.015)
  waiting for transfers between devices: 134 us -> 137 us
    ppermute x7, waiting for transfers between devices: 71.6 us -> 74.3 us  [the longest x1 24.9 us: gather_columns(): ahead = lax.ppermute(own, CTX, ctx_shift(n_ring, 1, 0))]
where the time goes in v9:
time: 208 us; the launch traced here: 207 us
  waiting for transfers between devices  137 us (66%)
  matrix products  24 us (12%)
  starting transfers between devices  20.5 us (10%)
  between operations  14.1 us (7%)
  local copies, waits for them, and re-layouts  8.45 us (4%)
  other arithmetic  2.95 us (1%)
    all_gather x1, waiting for transfers between devices, local(): rows = lax.all_gather(swapped, ('zhi', 'x'), axis=0, tiled=True)  55.5 us
    ppermute x1, waiting for transfers between devices, gather_columns(): ahead = lax.ppermute(own, CTX, ctx_shift(n_ring, 1, 0))  24.9 us
    dot_general x2, matrix products, contract_tokens(): lax.dot_general(left, right, (((0,), (0,)), ((), ())), preferred_element_...  24 us
    ppermute x1, waiting for transfers between devices, local(): lax.ppermute(acts, AXES, pairs)  21.2 us
    ppermute x1, waiting for transfers between devices, gather_columns(): near = lax.ppermute(block, CTX, ctx_shift(n_ring, 0, 1))  14.6 us
    ppermute x1, waiting for transfers between devices, gather_columns(): far_a = lax.ppermute(ahead[:half], CTX, ctx_shift(n_ring, 1, 0))  11 us
    ppermute x1, starting transfers between devices, local(): lax.ppermute(out_grads, AXES, pairs)  10.1 us
    ppermute x1, waiting for transfers between devices, gather_columns(): other = lax.ppermute(mine, 'dp', [(1, 0), (0, 1)])  7.54 us
  transfers between devices with their start and end apart: 9, of which 7 were waited for; matrix products, arithmetic and copies ran while one was open for 5% of the time, Pallas kernels for 0%

profile of v9, /device:TPU:41, one launch (start us, length us, event | category | flops | bytes accessed | tf_op | source)
XLA Modules:
  0.0 207.4 jit_solution(2630165964258691037)
XLA Ops:
  7.2 0.0 all-gather.2.cloned.1.call-start
  7.2 10.1 %collective-permute-start = (bf16[128,1792]{1,0:T(8,128)(2,1)}, bf16[128,1792]{1,0:T(8,128)(2,1)S(1)}, u32[]{:S(2)}, u32[]{:S(2)}) collective-permute-start(bf16[128,1792]{1,0:T(8,128)(2,1)} %param.4), channel_id=1, source_target_pairs={{0,0},{64,1},{128,2},{192,3},{16,4},{80,5},{144,6},{208,7},{32,8},... | collective-permute-start | bytes 1376264 | tf_op jit(solution)/shard_map/ppermute | solution.py:81
  17.3 4.6 %collective-permute-start.1 = (bf16[128,512]{1,0:T(8,128)(2,1)}, bf16[128,512]{1,0:T(8,128)(2,1)S(1)}, u32[]{:S(2)}, u32[]{:S(2)}) collective-permute-start(bf16[128,512]{1,0:T(8,128)(2,1)} %param.5), channel_id=1, source_target_pairs={{0,0},{64,1},{128,2},{192,3},{16,4},{80,5},{144,6},{208,7},{32,8},... | collective-permute-start | bytes 393224 | tf_op jit(solution)/shard_map/ppermute | solution.py:82
  22.0 21.2 %collective-permute-done.1 = bf16[128,512]{1,0:T(8,128)(2,1)S(1)} collective-permute-done((bf16[128,512]{1,0:T(8,128)(2,1)}, bf16[128,512]{1,0:T(8,128)(2,1)S(1)}, u32[]{:S(2)}, u32[]{:S(2)}) %collective-permute-start.1) | collective-permute-done | bytes 131104 | tf_op jit(solution)/shard_map/ppermute | solution.py:82
  43.1 0.0 collective-permute-done
  43.1 0.9 pad_maximum_fusion.1
  44.0 0.0 all-gather.2.cloned.1.call-update
  44.0 0.8 select_reduce_fusion
  44.8 1.3 constant_dynamic-update-slice_fusion.5
  46.0 0.1 collective-permute-start.2
  46.1 14.6 %collective-permute-done.2 = bf16[128,2304]{1,0:T(8,128)(2,1)S(1)} collective-permute-done((bf16[128,2304]{1,0:T(8,128)(2,1)S(1)}, bf16[128,2304]{1,0:T(8,128)(2,1)S(1)}, u32[]{:S(2)}, u32[]{:S(2)}) %collective-permute-start.2) | collective-permute-done | bytes 589856 | tf_op jit(solution)/shard_map/ppermute | solution.py:56
  60.7 0.1 pad_maximum_fusion
  60.8 0.1 collective-permute-start.3
  60.9 1.5 collective-permute-start.5
  62.4 0.9 constant_dynamic-update-slice_fusion.12
  63.2 24.9 %collective-permute-done.3 = bf16[256,2304]{1,0:T(8,128)(2,1)S(1)} collective-permute-done((bf16[256,2304]{1,0:T(8,128)(2,1)S(1)}, bf16[256,2304]{1,0:T(8,128)(2,1)S(1)}, u32[]{:S(2)}, u32[]{:S(2)}) %collective-permute-start.3) | collective-permute-done | bytes 1179680 | tf_op jit(solution)/shard_map/ppermute | solution.py:58
  88.2 2.0 collective-permute-start.4
  90.2 0.9 constant_dynamic-update-slice_fusion.4
  91.1 0.0 collective-permute-done.5
  91.1 0.4 collective-permute-start.6
  91.6 1.2 constant_dynamic-update-slice_fusion.3
  92.8 11.0 %collective-permute-done.4 = bf16[128,2304]{1,0:T(8,128)(2,1)S(1)} collective-permute-done((bf16[128,2304]{1,0:T(8,128)(2,1)S(1)}, bf16[128,2304]{1,0:T(8,128)(2,1)S(1)}, u32[]{:S(2)}, u32[]{:S(2)}) %collective-permute-start.4) | collective-permute-done | bytes 589856 | tf_op jit(solution)/shard_map/ppermute | solution.py:60
  103.7 0.9 constant_dynamic-update-slice_fusion.2
  104.6 2.7 %collective-permute-done.6 = bf16[128,2304]{1,0:T(8,128)(2,1)S(1)} collective-permute-done((bf16[128,2304]{1,0:T(8,128)(2,1)S(1)}, bf16[128,2304]{1,0:T(8,128)(2,1)S(1)}, u32[]{:S(2)}, u32[]{:S(2)}) %collective-permute-start.6) | collective-permute-done | bytes 589856 | tf_op jit(solution)/shard_map/ppermute | solution.py:61
  107.3 0.9 constant_dynamic-update-slice_fusion.1
  108.2 1.2 constant_dynamic-update-slice_fusion
  109.4 1.6 collective-permute-start.7
  111.0 7.5 %collective-permute-done.7 = bf16[1024,2304]{1,0:T(8,128)(2,1)S(1)} collective-permute-done((bf16[1024,2304]{1,0:T(8,128)(2,1)S(1)}, bf16[1024,2304]{1,0:T(8,128)(2,1)S(1)}, u32[]{:S(2)}, u32[]{:S(2)}) %collective-permute-start.7) | collective-permute-done | bytes 4718624 | tf_op jit(solution)/shard_map/ppermute | solution.py:63
  118.5 2.4 %constant_dynamic-update-slice_fusion.6 = bf16[2048,2304]{1,0:T(8,128)(2,1)} fusion(bf16[2048,2304]{1,0:T(8,128)(2,1)} %get-tuple-element.5, bf16[1024,2304]{1,0:T(8,128)(2,1)S(1)} %collective-permute-done.7), kind=kLoop, calls=%fused_computation.17 | loop fusion | bytes 9437184 | tf_op jit(solution)/shard_map/concatenate | solution.py:64
  121.0 55.5 %all-gather.2.cloned.1.call-done = bf16[2048,2304]{1,0:T(8,128)(2,1)} async-done(((bf16[128,2304]{1,0:T(8,128)(2,1)}), bf16[2048,2304]{1,0:T(8,128)(2,1)}) %all-gather.2.cloned.1.call-update) | async-done | bytes 9437200 | tf_op jit(solution)/shard_map/all_gather | solution.py:83
  176.5 19.7 %multiply_convert_fusion = bf16[1792,1792]{1,0:T(8,128)(2,1)} fusion(bf16[2048,2304]{1,0:T(8,128)(2,1)} %constant_dynamic-update-slice_fusion.6, bf16[2048,2304]{1,0:T(8,128)(2,1)} %all-gather.2.cloned.1.call-done), kind=kOutput, calls=%fused_computation | convolution fusion | flops 13159759872 | bytes 21102592 | tf_op jit(solution)/shard_map/dot_general | solution.py:22
  196.2 4.3 %fusion.10 = bf16[512,512]{1,0:T(8,128)(2,1)} fusion(bf16[2048,2304]{1,0:T(8,128)(2,1)} %constant_dynamic-update-slice_fusion.6, bf16[2048,2304]{1,0:T(8,128)(2,1)} %all-gather.2.cloned.1.call-done), kind=kOutput, calls=%fused_computation.7 | convolution fusion | flops 1074266112 | bytes 4718592 | tf_op jit(solution)/shard_map/dot_general | solution.py:22
  (3 shorter events, 0.1 us)
Async XLA Ops:
  7.2 169.3 %all-gather.2.cloned.1.call-start = ((), (), s32[]{:S(2)}) async-start(), calls=%async_computation | async-start | bytes 10027008 | tf_op jit(solution)/shard_map/all_gather | solution.py:83
  7.2 35.9 %collective-permute-start = (bf16[128,1792]{1,0:T(8,128)(2,1)}, bf16[128,1792]{1,0:T(8,128)(2,1)S(1)}, u32[]{:S(2)}, u32[]{:S(2)}) collective-permute-start(bf16[128,1792]{1,0:T(8,128)(2,1)} %param.4), channel_id=1, source_target_pairs={{0,0},{64,1},{128,2},{192,3},{16,4},{80,5},{144,6},{208,7},{32,8},... | collective-permute-start | bytes 1376264 | tf_op jit(solution)/shard_map/ppermute | solution.py:81
  17.3 25.8 %collective-permute-start.1 = (bf16[128,512]{1,0:T(8,128)(2,1)}, bf16[128,512]{1,0:T(8,128)(2,1)S(1)}, u32[]{:S(2)}, u32[]{:S(2)}) collective-permute-start(bf16[128,512]{1,0:T(8,128)(2,1)} %param.5), channel_id=1, source_target_pairs={{0,0},{64,1},{128,2},{192,3},{16,4},{80,5},{144,6},{208,7},{32,8},... | collective-permute-start | bytes 393224 | tf_op jit(solution)/shard_map/ppermute | solution.py:82
  46.0 14.7 %collective-permute-start.2 = (bf16[128,2304]{1,0:T(8,128)(2,1)S(1)}, bf16[128,2304]{1,0:T(8,128)(2,1)S(1)}, u32[]{:S(2)}, u32[]{:S(2)}) collective-permute-start(bf16[128,2304]{1,0:T(8,128)(2,1)S(1)} %get-tuple-element.3), channel_id=1, source_target_pairs={{16,0},{0,16},{48,32},{32,48},{80,64},{64,80},{112,96},{96,112},{1... | collective-permute-start | bytes 1769480 | tf_op jit(solution)/shard_map/ppermute | solution.py:56
  60.8 27.3 %collective-permute-start.3 = (bf16[256,2304]{1,0:T(8,128)(2,1)S(1)}, bf16[256,2304]{1,0:T(8,128)(2,1)S(1)}, u32[]{:S(2)}, u32[]{:S(2)}) collective-permute-start(bf16[256,2304]{1,0:T(8,128)(2,1)S(1)} %pad_maximum_fusion), channel_id=1, source_target_pairs={{32,0},{48,16},{64,32},{80,48},{96,64},{112,80},{0,96},{16,112},{3... | collective-permute-start | bytes 3538952 | tf_op jit(solution)/shard_map/ppermute | solution.py:58
  60.9 30.2 %collective-permute-start.5 = (bf16[256,2304]{1,0:T(8,128)(2,1)S(1)}, bf16[256,2304]{1,0:T(8,128)(2,1)S(1)}, u32[]{:S(2)}, u32[]{:S(2)}) collective-permute-start(bf16[256,2304]{1,0:T(8,128)(2,1)S(1)} %pad_maximum_fusion), channel_id=1, source_target_pairs={{96,0},{112,16},{0,32},{16,48},{32,64},{48,80},{64,96},{80,112},{9... | collective-permute-start | bytes 3538952 | tf_op jit(solution)/shard_map/ppermute | solution.py:59
  88.2 15.5 %collective-permute-start.4 = (bf16[128,2304]{1,0:T(8,128)(2,1)S(1)}, bf16[128,2304]{1,0:T(8,128)(2,1)S(1)}, u32[]{:S(2)}, u32[]{:S(2)}) collective-permute-start(bf16[128,2304]{1,0:T(8,128)(2,1)S(1)} %slice.25), channel_id=1, source_target_pairs={{32,0},{48,16},{64,32},{80,48},{96,64},{112,80},{0,96},{16,112},{3... | collective-permute-start | bytes 1769480 | tf_op jit(solution)/shard_map/ppermute | solution.py:60
  91.1 16.1 %collective-permute-start.6 = (bf16[128,2304]{1,0:T(8,128)(2,1)S(1)}, bf16[128,2304]{1,0:T(8,128)(2,1)S(1)}, u32[]{:S(2)}, u32[]{:S(2)}) collective-permute-start(bf16[128,2304]{1,0:T(8,128)(2,1)S(1)} %slice.26), channel_id=1, source_target_pairs={{96,0},{112,16},{0,32},{16,48},{32,64},{48,80},{64,96},{80,112},{9... | collective-permute-start | bytes 1769480 | tf_op jit(solution)/shard_map/ppermute | solution.py:61
  109.4 9.2 %collective-permute-start.7 = (bf16[1024,2304]{1,0:T(8,128)(2,1)S(1)}, bf16[1024,2304]{1,0:T(8,128)(2,1)S(1)}, u32[]{:S(2)}, u32[]{:S(2)}) collective-permute-start(bf16[1024,2304]{1,0:T(8,128)(2,1)S(1)} %get-tuple-element.4), channel_id=1, source_target_pairs={{128,0},{0,128},{129,1},{1,129},{130,2},{2,130},{131,3},{3,131},{1... | collective-permute-start | bytes 14155784 | tf_op jit(solution)/shard_map/ppermute | solution.py:63
Sparse Core Ops, SparseCore 0:
  44.1 132.2 all-gather.1

commit v10 on v8

--- a/solution.py
+++ b/solution.py
@@ -70,12 +70,21 @@
     tok_weight = token_weights(domain_ids, domain_weights)
     weighted = (tok_weight[:, None] * both.astype(jnp.float32)).astype(jnp.bfloat16)
     pairs = transpose_pairs(n_rows, n_cols, n_dp, n_ring)
-    swapped = jnp.concatenate([lax.ppermute(out_grads, ROWS + ("feat",), pairs),
-                               lax.ppermute(acts, ROWS + ("feat",), pairs)], axis=1)
-    rows = lax.all_gather(swapped, "feat", axis=0, tiled=True)
-    cols = gather_columns(weighted, n_dp, n_ring)
-    grad_sum = contract_tokens(rows[:, :width_g], cols[:, :width_g])
-    act_sum = contract_tokens(rows[:, width_g:], cols[:, width_g:])
+    swapped = lax.ppermute(out_grads, ROWS + ("feat",), pairs)
+    rows_g = lax.all_gather(swapped, "feat", axis=0, tiled=True)
+    cols = gather_columns(jnp.concatenate([weighted, acts], axis=1), n_dp, n_ring)
+    width = both.shape[1]
+    plain = [(c * n_cols + r, r * n_cols + c) for r in range(n_rows) for c in range(n_cols)]
+    got = lax.ppermute(cols[:, width:], ROWS + ("feat",), plain)
+    r_dp, r_y, r_z = split_row(lax.axis_index(ROWS), n_ring)
+    c_dp, c_y, c_z = split_row(lax.axis_index("feat"), n_ring)
+    ddp, dy, dz = split_row(jnp.arange(n_rows), n_ring)
+    src = (((r_dp - c_dp + ddp) % n_dp) * n_ring * PAIR + ((r_y - c_y + dy) % n_ring) * PAIR
+           + (r_z - c_z + dz) % PAIR)
+    block = acts.shape[0]
+    rows_a = jnp.take(got.reshape(n_rows, block, acts.shape[1]), src, axis=0).reshape(got.shape)
+    grad_sum = contract_tokens(rows_g, cols[:, :width_g])
+    act_sum = contract_tokens(rows_a, cols[:, width_g:width])
     grad_factor = (grad_sum * inv_count).astype(jnp.bfloat16)
     act_factor = (act_sum * inv_count).astype(jnp.bfloat16)
     return (grad_factor, act_factor)

time: 205 us -> 295 us (1.44)
  waiting for transfers between devices: 134 us -> 204 us
  local copies, waits for them, and re-layouts: 8.45 us -> 27.5 us
    ppermute x2, waiting for transfers between devices: 20.7 us -> 133 us  [the longest x1 119 us: local(): got = lax.ppermute(cols[:, width:], ROWS + ('feat',), plain)]
    all_gather x1, waiting for transfers between devices: 54.9 us -> 0.01 us  [local(): rows_g = lax.all_gather(swapped, 'feat', axis=0, tiled=True)]
    unnamed x5 -> x9, local copies, waits for them, and re-layouts: 4.78 us -> 17.3 us
    ppermute x1, waiting for transfers between devices: 24.8 us -> 32.1 us  [gather_columns(): ahead = lax.ppermute(own, 'ctx', ctx_shift(n_ring, 1, 0))]
    slice x0 -> x1, local copies, waits for them, and re-layouts: none -> 3.04 us  [local(): got = lax.ppermute(cols[:, width:], ROWS + ('feat',), plain)]
  transfers between devices with their start and end apart: 9 -> 9, of which waited for: 7 -> 7; matrix products, arithmetic and copies ran while one was open for 5% -> 9% of each run, Pallas kernels for 0% -> 0%
where the time goes in v10:
time: 295 us; the launch traced here: 293 us
  waiting for transfers between devices  204 us (69%)
  local copies, waits for them, and re-layouts  27.5 us (9%)
  matrix products  23.4 us (8%)
  starting transfers between devices  18.3 us (6%)
  between operations  14.2 us (5%)
  other arithmetic  5.82 us (2%)
    ppermute x1, waiting for transfers between devices, local(): got = lax.ppermute(cols[:, width:], ROWS + ('feat',), plain)  119 us
    ppermute x1, waiting for transfers between devices, gather_columns(): ahead = lax.ppermute(own, 'ctx', ctx_shift(n_ring, 1, 0))  32.1 us
    dot_general x2, matrix products, contract_tokens(): lax.dot_general(left, right, (((0,), (0,)), ((), ())), preferred_element_...  23.4 us
    unnamed x9, local copies, waits for them, and re-layouts  17.3 us
    ppermute x1, waiting for transfers between devices, gather_columns(): near = lax.ppermute(block, 'ctx', ctx_shift(n_ring, 0, 1))  14.1 us
    ppermute x1, waiting for transfers between devices, local(): swapped = lax.ppermute(out_grads, ROWS + ('feat',), pairs)  13.8 us
    ppermute x1, waiting for transfers between devices, gather_columns(): far_a = lax.ppermute(ahead[:half], 'ctx', ctx_shift(n_ring, 1, 0))  12.8 us
    ppermute x1, starting transfers between devices, local(): swapped = lax.ppermute(out_grads, ROWS + ('feat',), pairs)  10.4 us
  transfers between devices with their start and end apart: 9, of which 7 were waited for; matrix products, arithmetic and copies ran while one was open for 9% of the time, Pallas kernels for 0%

profile of v10, /device:TPU:41, one launch (start us, length us, event | category | flops | bytes accessed | tf_op | source)
XLA Modules:
  0.0 293.4 jit_solution(3323621109216540799)
XLA Ops:
  7.2 0.0 all-gather.2.cloned.1.call-start
  7.2 10.4 %collective-permute-start.6 = (bf16[128,1792]{1,0:T(8,128)(2,1)}, bf16[128,1792]{1,0:T(8,128)(2,1)S(1)}, u32[]{:S(2)}, u32[]{:S(2)}) collective-permute-start(bf16[128,1792]{1,0:T(8,128)(2,1)} %param.4), channel_id=1, source_target_pairs={{0,0},{16,1},{32,2},{48,3},{64,4},{80,5},{96,6},{112,7},{128,8},{1... | collective-permute-start | bytes 1376264 | tf_op jit(solution)/shard_map/ppermute | solution.py:73
  17.6 0.8 select_reduce_fusion
  18.4 1.3 multiply_convert_fusion.1
  19.6 2.2 constant_dynamic-update-slice_fusion.5
  21.8 1.2 collective-permute-start
  22.9 13.8 %collective-permute-done.6 = bf16[128,1792]{1,0:T(8,128)(2,1)S(1)} collective-permute-done((bf16[128,1792]{1,0:T(8,128)(2,1)}, bf16[128,1792]{1,0:T(8,128)(2,1)S(1)}, u32[]{:S(2)}, u32[]{:S(2)}) %collective-permute-start.6) | collective-permute-done | bytes 458784 | tf_op jit(solution)/shard_map/ppermute | solution.py:73
  36.8 0.0 copy-start.1
  36.8 0.8 copy-done.1
  37.6 0.0 all-gather.2.cloned.1.call-update
  37.6 14.1 %collective-permute-done = bf16[128,2816]{1,0:T(8,128)(2,1)S(1)} collective-permute-done((bf16[128,2816]{1,0:T(8,128)(2,1)S(1)}, bf16[128,2816]{1,0:T(8,128)(2,1)S(1)}, u32[]{:S(2)}, u32[]{:S(2)}) %collective-permute-start) | collective-permute-done | bytes 720928 | tf_op jit(solution)/shard_map/ppermute | solution.py:49
  51.7 1.0 pad_maximum_fusion
  52.7 0.1 collective-permute-start.1
  52.8 1.5 collective-permute-start.3
  54.2 32.1 %collective-permute-done.1 = bf16[256,2816]{1,0:T(8,128)(2,1)S(1)} collective-permute-done((bf16[256,2816]{1,0:T(8,128)(2,1)S(1)}, bf16[256,2816]{1,0:T(8,128)(2,1)S(1)}, u32[]{:S(2)}, u32[]{:S(2)}) %collective-permute-start.1) | collective-permute-done | bytes 1441824 | tf_op jit(solution)/shard_map/ppermute | solution.py:51
  86.4 1.1 collective-permute-start.2
  87.5 1.2 constant_dynamic-update-slice_fusion.4
  88.7 0.0 collective-permute-done.3
  88.7 0.5 collective-permute-start.4
  89.3 1.8 constant_dynamic-update-slice_fusion.3
  91.0 12.8 %collective-permute-done.2 = bf16[128,2816]{1,0:T(8,128)(2,1)S(1)} collective-permute-done((bf16[128,2816]{1,0:T(8,128)(2,1)S(1)}, bf16[128,2816]{1,0:T(8,128)(2,1)S(1)}, u32[]{:S(2)}, u32[]{:S(2)}) %collective-permute-start.2) | collective-permute-done | bytes 720928 | tf_op jit(solution)/shard_map/ppermute | solution.py:53
  103.8 1.2 constant_dynamic-update-slice_fusion.2
  105.0 2.9 collective-permute-done.4
  107.9 1.2 constant_dynamic-update-slice_fusion.1
  109.1 1.8 constant_dynamic-update-slice_fusion
  110.9 1.5 collective-permute-start.5
  112.4 9.2 %collective-permute-done.5 = bf16[1024,2816]{1,0:T(8,128)(2,1)S(1)} collective-permute-done((bf16[1024,2816]{1,0:T(8,128)(2,1)}, bf16[1024,2816]{1,0:T(8,128)(2,1)S(1)}, u32[]{:S(2)}, u32[]{:S(2)}) %collective-permute-start.5) | collective-permute-done | bytes 5767200 | tf_op jit(solution)/shard_map/ppermute | solution.py:56
  121.7 2.9 constant_dynamic-update-slice_fusion.6
  124.6 3.0 %slice.25 = bf16[2048,512]{1,0:T(8,128)(2,1)} slice(bf16[2048,2816]{1,0:T(8,128)(2,1)} %constant_dynamic-update-slice_fusion.6), slice={[0:2048], [2304:2816]} | slice | bytes 4194304 | tf_op jit(solution)/shard_map/slice | solution.py:78
  127.6 2.1 collective-permute-start.7
  129.9 0.1 broadcast_bitcast_fusion
  130.0 119.1 %collective-permute-done.7 = bf16[2048,512]{1,0:T(8,128)(2,1)S(1)} collective-permute-done((bf16[2048,512]{1,0:T(8,128)(2,1)}, bf16[2048,512]{1,0:T(8,128)(2,1)S(1)}, u32[]{:S(2)}, u32[]{:S(2)}) %collective-permute-start.7) | collective-permute-done | bytes 2097184 | tf_op jit(solution)/shard_map/ppermute | solution.py:78
  249.1 0.0 copy-start
  249.1 1.3 copy-done
  250.4 2.3 gather_fusion
  252.7 0.6 bitcast_select_fusion
  253.3 3.7 %fusion.9 = bf16[512,512]{1,0:T(8,128)(2,1)} fusion(bf16[2048,512]{1,0:T(8,128)(2,1)S(1)} %bitcast_select_fusion, bf16[2048,2816]{1,0:T(8,128)(2,1)} %constant_dynamic-update-slice_fusion.6), kind=kOutput, calls=%fused_computation.9 | convolution fusion | flops 1074266112 | bytes 4718592 | tf_op jit(solution)/shard_map/dot_general | solution.py:17
  257.0 0.0 all-gather.2.cloned.1.call-done
  257.0 19.8 %fusion.1 = bf16[1792,1792]{0,1:T(8,128)(2,1)} fusion(bf16[2048,1792]{1,0:T(8,128)(2,1)} %all-gather.2.cloned.1.call-done, bf16[2048,2816]{1,0:T(8,128)(2,1)} %constant_dynamic-update-slice_fusion.6), kind=kOutput, calls=%fused_computation.3 | convolution fusion | flops 13159759872 | bytes 21102592 | tf_op jit(solution)/shard_map/dot_general | solution.py:17
  276.7 9.8 %copy.7 = bf16[1792,1792]{1,0:T(8,128)(2,1)} copy(bf16[1792,1792]{0,1:T(8,128)(2,1)} %fusion.1) | data formatting | bytes 12845056
  (6 shorter events, 0.2 us)
Async XLA Ops:
  7.2 249.8 %all-gather.2.cloned.1.call-start = ((), (), s32[]{:S(2)}) async-start(), calls=%async_computation | async-start | bytes 7798784 | tf_op jit(solution)/shard_map/all_gather | solution.py:74
  7.2 29.6 %collective-permute-start.6 = (bf16[128,1792]{1,0:T(8,128)(2,1)}, bf16[128,1792]{1,0:T(8,128)(2,1)S(1)}, u32[]{:S(2)}, u32[]{:S(2)}) collective-permute-start(bf16[128,1792]{1,0:T(8,128)(2,1)} %param.4), channel_id=1, source_target_pairs={{0,0},{16,1},{32,2},{48,3},{64,4},{80,5},{96,6},{112,7},{128,8},{1... | collective-permute-start | bytes 1376264 | tf_op jit(solution)/shard_map/ppermute | solution.py:73
  21.8 29.9 %collective-permute-start = (bf16[128,2816]{1,0:T(8,128)(2,1)S(1)}, bf16[128,2816]{1,0:T(8,128)(2,1)S(1)}, u32[]{:S(2)}, u32[]{:S(2)}) collective-permute-start(bf16[128,2816]{1,0:T(8,128)(2,1)S(1)} %get-tuple-element.18), channel_id=1, source_target_pairs={{16,0},{0,16},{48,32},{32,48},{80,64},{64,80},{112,96},{96,112},{1... | collective-permute-start | bytes 2162696 | tf_op jit(solution)/shard_map/ppermute | solution.py:49
  36.8 0.8 copy-start.1
  52.7 33.6 %collective-permute-start.1 = (bf16[256,2816]{1,0:T(8,128)(2,1)S(1)}, bf16[256,2816]{1,0:T(8,128)(2,1)S(1)}, u32[]{:S(2)}, u32[]{:S(2)}) collective-permute-start(bf16[256,2816]{1,0:T(8,128)(2,1)S(1)} %pad_maximum_fusion), channel_id=1, source_target_pairs={{32,0},{48,16},{64,32},{80,48},{96,64},{112,80},{0,96},{16,112},{3... | collective-permute-start | bytes 4325384 | tf_op jit(solution)/shard_map/ppermute | solution.py:51
  52.8 35.9 %collective-permute-start.3 = (bf16[256,2816]{1,0:T(8,128)(2,1)S(1)}, bf16[256,2816]{1,0:T(8,128)(2,1)S(1)}, u32[]{:S(2)}, u32[]{:S(2)}) collective-permute-start(bf16[256,2816]{1,0:T(8,128)(2,1)S(1)} %pad_maximum_fusion), channel_id=1, source_target_pairs={{96,0},{112,16},{0,32},{16,48},{32,64},{48,80},{64,96},{80,112},{9... | collective-permute-start | bytes 4325384 | tf_op jit(solution)/shard_map/ppermute | solution.py:52
  86.4 17.4 %collective-permute-start.2 = (bf16[128,2816]{1,0:T(8,128)(2,1)S(1)}, bf16[128,2816]{1,0:T(8,128)(2,1)S(1)}, u32[]{:S(2)}, u32[]{:S(2)}) collective-permute-start(bf16[128,2816]{1,0:T(8,128)(2,1)S(1)} %slice.22), channel_id=1, source_target_pairs={{32,0},{48,16},{64,32},{80,48},{96,64},{112,80},{0,96},{16,112},{3... | collective-permute-start | bytes 2162696 | tf_op jit(solution)/shard_map/ppermute | solution.py:53
  88.7 19.2 %collective-permute-start.4 = (bf16[128,2816]{1,0:T(8,128)(2,1)S(1)}, bf16[128,2816]{1,0:T(8,128)(2,1)S(1)}, u32[]{:S(2)}, u32[]{:S(2)}) collective-permute-start(bf16[128,2816]{1,0:T(8,128)(2,1)S(1)} %slice.23), channel_id=1, source_target_pairs={{96,0},{112,16},{0,32},{16,48},{32,64},{48,80},{64,96},{80,112},{9... | collective-permute-start | bytes 2162696 | tf_op jit(solution)/shard_map/ppermute | solution.py:54
  110.9 10.7 %collective-permute-start.5 = (bf16[1024,2816]{1,0:T(8,128)(2,1)}, bf16[1024,2816]{1,0:T(8,128)(2,1)S(1)}, u32[]{:S(2)}, u32[]{:S(2)}) collective-permute-start(bf16[1024,2816]{1,0:T(8,128)(2,1)} %get-tuple-element.6), channel_id=1, source_target_pairs={{128,0},{0,128},{129,1},{1,129},{130,2},{2,130},{131,3},{3,131},{1... | collective-permute-start | bytes 17301512 | tf_op jit(solution)/shard_map/ppermute | solution.py:56
  127.6 121.5 %collective-permute-start.7 = (bf16[2048,512]{1,0:T(8,128)(2,1)}, bf16[2048,512]{1,0:T(8,128)(2,1)S(1)}, u32[]{:S(2)}, u32[]{:S(2)}) collective-permute-start(bf16[2048,512]{1,0:T(8,128)(2,1)} %slice.25), channel_id=1, source_target_pairs={{0,0},{16,1},{32,2},{48,3},{64,4},{80,5},{96,6},{112,7},{128,8},{1... | collective-permute-start | bytes 6291464 | tf_op jit(solution)/shard_map/ppermute | solution.py:78
  249.1 1.3 copy-start
Sparse Core Ops, SparseCore 0:
  37.7 165.2 all-gather.1

commit v11 on v8

--- a/solution.py
+++ b/solution.py
@@ -75,7 +75,7 @@
     rows = lax.all_gather(swapped, "feat", axis=0, tiled=True)
     cols = gather_columns(weighted, n_dp, n_ring)
     grad_sum = contract_tokens(rows[:, :width_g], cols[:, :width_g])
-    act_sum = contract_tokens(rows[:, width_g:], cols[:, width_g:])
+    act_sum = contract_tokens(rows[:, width_g:], lax.optimization_barrier(cols[:, width_g:]))
     grad_factor = (grad_sum * inv_count).astype(jnp.bfloat16)
     act_factor = (act_sum * inv_count).astype(jnp.bfloat16)
     return (grad_factor, act_factor)

time: 205 us -> 205 us (level)
  local copies, waits for them, and re-layouts: 8.45 us -> 4.76 us
  waiting for transfers between devices: 134 us -> 137 us
    concatenate x1, local copies, waits for them, and re-layouts: 2.42 us -> 0.3 us  [gather_columns(): return jnp.concatenate([mine, other], axis=0)]
    unnamed x5 -> x7, local copies, waits for them, and re-layouts: 4.78 us -> 4.06 us
  transfers between devices with their start and end apart: 9 -> 9, of which waited for: 7 -> 7; matrix products, arithmetic and copies ran while one was open for 5% -> 2% of each run, Pallas kernels for 0% -> 0%
where the time goes in v11:
time: 205 us; the launch traced here: 204 us
  waiting for transfers between devices  137 us (67%)
  matrix products  23.5 us (11%)
  starting transfers between devices  21 us (10%)
  between operations  14.1 us (7%)
  local copies, waits for them, and re-layouts  4.76 us (2%)
  other arithmetic  2.95 us (1%)
    all_gather x1, waiting for transfers between devices, local(): rows = lax.all_gather(swapped, 'feat', axis=0, tiled=True)  55.6 us
    ppermute x1, waiting for transfers between devices, gather_columns(): ahead = lax.ppermute(own, 'ctx', ctx_shift(n_ring, 1, 0))  25.6 us
    dot_general x2, matrix products, contract_tokens(): lax.dot_general(left, right, (((0,), (0,)), ((), ())), preferred_element_...  23.5 us
    ppermute x1, waiting for transfers between devices, local(): lax.ppermute(acts, ROWS + ('feat',), pairs)  20.7 us
    ppermute x1, waiting for transfers between devices, gather_columns(): near = lax.ppermute(block, 'ctx', ctx_shift(n_ring, 0, 1))  15.2 us
    ppermute x1, waiting for transfers between devices, gather_columns(): far_a = lax.ppermute(ahead[:half], 'ctx', ctx_shift(n_ring, 1, 0))  11.9 us
    ppermute x1, starting transfers between devices, local(): lax.ppermute(out_grads, ROWS + ('feat',), pairs)  10.4 us
    ppermute x1, waiting for transfers between devices, gather_columns(): other = lax.ppermute(mine, 'dp', [(1, 0), (0, 1)])  7.54 us
  transfers between devices with their start and end apart: 9, of which 7 were waited for; matrix products, arithmetic and copies ran while one was open for 2% of the time, Pallas kernels for 0%

profile of v11, /device:TPU:41, one launch (start us, length us, event | category | flops | bytes accessed | tf_op | source)
XLA Modules:
  0.0 203.8 jit_solution(8906525784769521334)
XLA Ops:
  7.2 0.0 all-gather.2.cloned.1.call-start
  7.2 10.4 %collective-permute-start = (bf16[128,1792]{1,0:T(8,128)(2,1)}, bf16[128,1792]{1,0:T(8,128)(2,1)S(1)}, u32[]{:S(2)}, u32[]{:S(2)}) collective-permute-start(bf16[128,1792]{1,0:T(8,128)(2,1)} %param.4), channel_id=1, source_target_pairs={{0,0},{16,1},{32,2},{48,3},{64,4},{80,5},{96,6},{112,7},{128,8},{1... | collective-permute-start | bytes 1376264 | tf_op jit(solution)/shard_map/ppermute | solution.py:73
  17.6 4.0 %collective-permute-start.1 = (bf16[128,512]{1,0:T(8,128)(2,1)}, bf16[128,512]{1,0:T(8,128)(2,1)S(1)}, u32[]{:S(2)}, u32[]{:S(2)}) collective-permute-start(bf16[128,512]{1,0:T(8,128)(2,1)} %param.5), channel_id=1, source_target_pairs={{0,0},{16,1},{32,2},{48,3},{64,4},{80,5},{96,6},{112,7},{128,8},{1... | collective-permute-start | bytes 393224 | tf_op jit(solution)/shard_map/ppermute | solution.py:74
  21.6 20.7 %collective-permute-done.1 = bf16[128,512]{1,0:T(8,128)(2,1)S(1)} collective-permute-done((bf16[128,512]{1,0:T(8,128)(2,1)}, bf16[128,512]{1,0:T(8,128)(2,1)S(1)}, u32[]{:S(2)}, u32[]{:S(2)}) %collective-permute-start.1) | collective-permute-done | bytes 131104 | tf_op jit(solution)/shard_map/ppermute | solution.py:74
  42.3 0.0 collective-permute-done
  42.3 0.9 pad_maximum_fusion.1
  43.2 0.0 all-gather.2.cloned.1.call-update
  43.2 0.8 select_reduce_fusion
  44.0 1.3 constant_dynamic-update-slice_fusion.5
  45.2 0.1 collective-permute-start.2
  45.3 15.2 %collective-permute-done.2 = bf16[128,2304]{1,0:T(8,128)(2,1)S(1)} collective-permute-done((bf16[128,2304]{1,0:T(8,128)(2,1)S(1)}, bf16[128,2304]{1,0:T(8,128)(2,1)S(1)}, u32[]{:S(2)}, u32[]{:S(2)}) %collective-permute-start.2) | collective-permute-done | bytes 589856 | tf_op jit(solution)/shard_map/ppermute | solution.py:49
  60.5 0.1 pad_maximum_fusion
  60.6 0.1 collective-permute-start.3
  60.7 1.5 collective-permute-start.5
  62.2 25.6 %collective-permute-done.3 = bf16[256,2304]{1,0:T(8,128)(2,1)S(1)} collective-permute-done((bf16[256,2304]{1,0:T(8,128)(2,1)S(1)}, bf16[256,2304]{1,0:T(8,128)(2,1)S(1)}, u32[]{:S(2)}, u32[]{:S(2)}) %collective-permute-start.3) | collective-permute-done | bytes 1179680 | tf_op jit(solution)/shard_map/ppermute | solution.py:51
  87.9 0.4 collective-permute-start.4
  88.3 0.1 constant_dynamic-update-slice_fusion.4
  88.3 0.0 collective-permute-done.5
  88.4 1.2 collective-permute-start.6
  89.6 0.2 constant_dynamic-update-slice_fusion.3
  89.8 11.9 %collective-permute-done.4 = bf16[128,2304]{1,0:T(8,128)(2,1)S(1)} collective-permute-done((bf16[128,2304]{1,0:T(8,128)(2,1)S(1)}, bf16[128,2304]{1,0:T(8,128)(2,1)S(1)}, u32[]{:S(2)}, u32[]{:S(2)}) %collective-permute-start.4) | collective-permute-done | bytes 589856 | tf_op jit(solution)/shard_map/ppermute | solution.py:53
  101.6 0.1 constant_dynamic-update-slice_fusion.2
  101.7 0.9 collective-permute-done.6
  102.6 0.1 constant_dynamic-update-slice_fusion.1
  102.7 0.2 constant_dynamic-update-slice_fusion
  102.9 3.3 %collective-permute-start.7 = (bf16[1024,2304]{1,0:T(8,128)(2,1)S(1)}, bf16[1024,2304]{1,0:T(8,128)(2,1)S(1)}, u32[]{:S(2)}, u32[]{:S(2)}) collective-permute-start(bf16[1024,2304]{1,0:T(8,128)(2,1)S(1)} %get-tuple-element.4), channel_id=1, source_target_pairs={{128,0},{0,128},{129,1},{1,129},{130,2},{2,130},{131,3},{3,131},{1... | collective-permute-start | bytes 14155784 | tf_op jit(solution)/shard_map/ppermute | solution.py:56
  106.2 7.5 %collective-permute-done.7 = bf16[1024,2304]{1,0:T(8,128)(2,1)S(1)} collective-permute-done((bf16[1024,2304]{1,0:T(8,128)(2,1)S(1)}, bf16[1024,2304]{1,0:T(8,128)(2,1)S(1)}, u32[]{:S(2)}, u32[]{:S(2)}) %collective-permute-start.7) | collective-permute-done | bytes 4718624 | tf_op jit(solution)/shard_map/ppermute | solution.py:56
  113.7 0.3 constant_dynamic-update-slice_fusion.6
  114.0 0.0 copy-start
  114.0 3.6 %copy-done = bf16[2048,2304]{1,0:T(8,128)(2,1)} copy-done((bf16[2048,2304]{1,0:T(8,128)(2,1)}, bf16[2048,2304]{1,0:T(8,128)(2,1)S(1)}, u32[]{:S(2)}) %copy-start) | copy-done | bytes 9437208
  117.6 0.2 slice.29
  117.8 55.6 %all-gather.2.cloned.1.call-done = bf16[2048,2304]{1,0:T(8,128)(2,1)} async-done(((bf16[128,2304]{1,0:T(8,128)(2,1)}), bf16[2048,2304]{1,0:T(8,128)(2,1)}) %all-gather.2.cloned.1.call-update) | async-done | bytes 9437200 | tf_op jit(solution)/shard_map/all_gather | solution.py:75
  173.4 19.8 %multiply_convert_fusion = bf16[1792,1792]{1,0:T(8,128)(2,1)} fusion(bf16[2048,2304]{1,0:T(8,128)(2,1)} %copy-done, bf16[2048,2304]{1,0:T(8,128)(2,1)} %all-gather.2.cloned.1.call-done), kind=kOutput, calls=%fused_computation | convolution fusion | flops 13159759872 | bytes 21102592 | tf_op jit(solution)/shard_map/dot_general | solution.py:17
  193.2 3.7 %fusion.7 = bf16[512,512]{1,0:T(8,128)(2,1)} fusion(bf16[2048,512]{1,0:T(8,128)(2,1)S(1)} %slice.29, bf16[2048,2304]{1,0:T(8,128)(2,1)} %all-gather.2.cloned.1.call-done), kind=kOutput, calls=%fused_computation.6 | convolution fusion | flops 1074266112 | bytes 4718592 | tf_op jit(solution)/shard_map/dot_general | solution.py:17
  (4 shorter events, 0.1 us)
Async XLA Ops:
  7.2 166.3 %all-gather.2.cloned.1.call-start = ((), (), s32[]{:S(2)}) async-start(), calls=%async_computation | async-start | bytes 10027008 | tf_op jit(solution)/shard_map/all_gather | solution.py:75
  7.2 35.1 %collective-permute-start = (bf16[128,1792]{1,0:T(8,128)(2,1)}, bf16[128,1792]{1,0:T(8,128)(2,1)S(1)}, u32[]{:S(2)}, u32[]{:S(2)}) collective-permute-start(bf16[128,1792]{1,0:T(8,128)(2,1)} %param.4), channel_id=1, source_target_pairs={{0,0},{16,1},{32,2},{48,3},{64,4},{80,5},{96,6},{112,7},{128,8},{1... | collective-permute-start | bytes 1376264 | tf_op jit(solution)/shard_map/ppermute | solution.py:73
  17.6 24.7 %collective-permute-start.1 = (bf16[128,512]{1,0:T(8,128)(2,1)}, bf16[128,512]{1,0:T(8,128)(2,1)S(1)}, u32[]{:S(2)}, u32[]{:S(2)}) collective-permute-start(bf16[128,512]{1,0:T(8,128)(2,1)} %param.5), channel_id=1, source_target_pairs={{0,0},{16,1},{32,2},{48,3},{64,4},{80,5},{96,6},{112,7},{128,8},{1... | collective-permute-start | bytes 393224 | tf_op jit(solution)/shard_map/ppermute | solution.py:74
  45.2 15.3 %collective-permute-start.2 = (bf16[128,2304]{1,0:T(8,128)(2,1)S(1)}, bf16[128,2304]{1,0:T(8,128)(2,1)S(1)}, u32[]{:S(2)}, u32[]{:S(2)}) collective-permute-start(bf16[128,2304]{1,0:T(8,128)(2,1)S(1)} %get-tuple-element.3), channel_id=1, source_target_pairs={{16,0},{0,16},{48,32},{32,48},{80,64},{64,80},{112,96},{96,112},{1... | collective-permute-start | bytes 1769480 | tf_op jit(solution)/shard_map/ppermute | solution.py:49
  60.6 27.2 %collective-permute-start.3 = (bf16[256,2304]{1,0:T(8,128)(2,1)S(1)}, bf16[256,2304]{1,0:T(8,128)(2,1)S(1)}, u32[]{:S(2)}, u32[]{:S(2)}) collective-permute-start(bf16[256,2304]{1,0:T(8,128)(2,1)S(1)} %pad_maximum_fusion), channel_id=1, source_target_pairs={{32,0},{48,16},{64,32},{80,48},{96,64},{112,80},{0,96},{16,112},{3... | collective-permute-start | bytes 3538952 | tf_op jit(solution)/shard_map/ppermute | solution.py:51
  60.7 27.7 %collective-permute-start.5 = (bf16[256,2304]{1,0:T(8,128)(2,1)S(1)}, bf16[256,2304]{1,0:T(8,128)(2,1)S(1)}, u32[]{:S(2)}, u32[]{:S(2)}) collective-permute-start(bf16[256,2304]{1,0:T(8,128)(2,1)S(1)} %pad_maximum_fusion), channel_id=1, source_target_pairs={{96,0},{112,16},{0,32},{16,48},{32,64},{48,80},{64,96},{80,112},{9... | collective-permute-start | bytes 3538952 | tf_op jit(solution)/shard_map/ppermute | solution.py:52
  87.9 13.8 %collective-permute-start.4 = (bf16[128,2304]{1,0:T(8,128)(2,1)S(1)}, bf16[128,2304]{1,0:T(8,128)(2,1)S(1)}, u32[]{:S(2)}, u32[]{:S(2)}) collective-permute-start(bf16[128,2304]{1,0:T(8,128)(2,1)S(1)} %slice.25), channel_id=1, source_target_pairs={{32,0},{48,16},{64,32},{80,48},{96,64},{112,80},{0,96},{16,112},{3... | collective-permute-start | bytes 1769480 | tf_op jit(solution)/shard_map/ppermute | solution.py:53
  88.4 14.2 %collective-permute-start.6 = (bf16[128,2304]{1,0:T(8,128)(2,1)S(1)}, bf16[128,2304]{1,0:T(8,128)(2,1)S(1)}, u32[]{:S(2)}, u32[]{:S(2)}) collective-permute-start(bf16[128,2304]{1,0:T(8,128)(2,1)S(1)} %slice.26), channel_id=1, source_target_pairs={{96,0},{112,16},{0,32},{16,48},{32,64},{48,80},{64,96},{80,112},{9... | collective-permute-start | bytes 1769480 | tf_op jit(solution)/shard_map/ppermute | solution.py:54
  102.9 10.8 %collective-permute-start.7 = (bf16[1024,2304]{1,0:T(8,128)(2,1)S(1)}, bf16[1024,2304]{1,0:T(8,128)(2,1)S(1)}, u32[]{:S(2)}, u32[]{:S(2)}) collective-permute-start(bf16[1024,2304]{1,0:T(8,128)(2,1)S(1)} %get-tuple-element.4), channel_id=1, source_target_pairs={{128,0},{0,128},{129,1},{1,129},{130,2},{2,130},{131,3},{3,131},{1... | collective-permute-start | bytes 14155784 | tf_op jit(solution)/shard_map/ppermute | solution.py:56
  114.0 3.7 %copy-start = (bf16[2048,2304]{1,0:T(8,128)(2,1)}, bf16[2048,2304]{1,0:T(8,128)(2,1)S(1)}, u32[]{:S(2)}) copy-start(bf16[2048,2304]{1,0:T(8,128)(2,1)S(1)} %constant_dynamic-update-slice_fusion.6) | copy-start | bytes 28311556
Sparse Core Ops, SparseCore 0:
  43.3 130.0 all-gather.1
